TPU v7x, 512 devices: a whole 4x8x8 slice. The times are simulated.
512 devices in a mesh: blk: 16 (over y_hi, z), bank: 32 (over y_lo, x, core).
Axes of the slice: x: 4, y: 8 (y_hi: 2, y_lo: 4; y = y_hi * 4 + y_lo), z: 8, core: 2. Of those that a mesh axis runs over, the one named last changes fastest.
Arguments:
- log_density: bfloat16 [2048, 32768], P(('blk', 'bank')), may hold values from -8 to 8
- assignment: int32 [2048], P(('blk', 'bank')), may hold values from 0 to 7, as said below
Outputs:
- centers: bfloat16 [8, 32768], P(None, 'bank')
- potentials: float32 [2048, 32768], P(('blk', 'bank'))
Inputs may be any that keep to these rules, and one draw needn't show every extreme that they name: Every barycenter index is the assignment of at least one member.
All inputs are finite; a program needn't handle non-finite values.
Results may differ from a plain program's by a relative error of at most 0.0051.
Values may be sent and summed in bfloat16 or wider, within the bound.
No kernel may reach another device: no remote copies, remote signals or barrier semaphores. Data moves between devices by JAX's collectives and lax.ppermute only.
A program may use at most 64 MiB of HBM per device.

v0:
```python
import jax
import jax.numpy as jnp
from jax import lax
from jax.sharding import PartitionSpec as P

G = 32
BARS = 8
ITERS = 2


def kernel_tables():
    grid_pos = jnp.arange(G, dtype=jnp.float32)
    offset = grid_pos[:, None] - grid_pos[None, :]
    kernel_line = jnp.exp(-0.5 * offset * offset)
    kernel_pair = (
        (kernel_line[:, None, :, None] * kernel_line[None, :, None, :])
        .reshape(G * G, G * G)
        .astype(jnp.bfloat16)
    )
    return (kernel_line, kernel_pair)


def log_convolve(field_log, kernel_line, kernel_pair):
    member_count = field_log.shape[0]
    raised = jnp.exp(field_log).astype(jnp.bfloat16).reshape(member_count * G, G * G)
    inner_sum = jnp.dot(raised, kernel_pair, preferred_element_type=jnp.float32).reshape(
        member_count, G, G * G
    )
    outer_sum = jnp.einsum("ij,mjc->mic", kernel_line, inner_sum, precision=lax.Precision.HIGHEST)
    return jnp.log(outer_sum).reshape(member_count, G * G * G)


def per_device(log_density, assignment):
    kernel_line, kernel_pair = kernel_tables()
    member_count = log_density.shape[0]
    cell_count = log_density.shape[1]
    row_count = cell_count // 128
    labels = jnp.arange(BARS, dtype=jnp.int32)
    onehot = (assignment[:, None] == labels[None, :]).astype(jnp.float32)
    counts = lax.psum(jnp.sum(onehot, axis=0), ("blk", "bank"))
    selector = onehot.astype(jnp.bfloat16)
    member_weights = jnp.transpose(onehot)
    potential = jnp.zeros((member_count, cell_count), jnp.float32)
    center_owned = jnp.zeros((row_count // lax.axis_size("bank"), BARS, 128), jnp.bfloat16)
    for iteration in range(ITERS):
        source = log_density.astype(jnp.float32) - log_convolve(potential, kernel_line, kernel_pair)
        smoothed = log_convolve(source, kernel_line, kernel_pair)
        blocks = smoothed.reshape(member_count, row_count, 128)
        reduced = lax.psum_scatter(
            jnp.einsum("km,mrl->rkl", member_weights, blocks, precision=lax.Precision.HIGHEST),
            "bank",
            scatter_dimension=0,
            tiled=True,
        )
        summed = lax.psum(reduced, "blk")
        center_slice = (summed / counts[None, :, None]).astype(jnp.bfloat16)
        center_all = lax.all_gather(center_slice, "bank", axis=0, tiled=True)
        center_owned = center_slice
        chosen = jnp.einsum("mk,rkl->mrl", selector, center_all, preferred_element_type=jnp.float32)
        potential = chosen.reshape(member_count, cell_count) - smoothed
    centers = jnp.transpose(center_owned, (1, 0, 2)).reshape(BARS, center_owned.shape[0] * 128)
    return (centers, potential)


def solution(mesh):
    placed = (P(("blk", "bank"), None), P(("blk", "bank")))
    return jax.shard_map(
        per_device,
        mesh=mesh,
        in_specs=placed,
        out_specs=(P(None, "bank"), P(("blk", "bank"), None)),
        check_vma=False,
    )
```

profile of v0, /device:TPU:1, one launch (start us, length us, event | category | flops | bytes accessed | tf_op | source)
XLA Modules:
  0.0 615.1 jit_solution(17114058292738188008)
XLA Ops:
  7.2 5.3 multiply_convert_fusion
  12.5 11.3 %reshape.101 = bf16[1024,1024,1]{1,0,2:T(8,128)(2,1)S(1)} reshape(bf16[32,32,32,32]{3,2,1,0:T(8,128)(2,1)} %multiply_convert_fusion) | data formatting | bytes 4194304 | tf_op jit(solution)/shard_map/convert_element_type | solution.py:18
  23.8 0.4 fusion.17
  24.3 0.6 fusion.3
  25.5 0.5 fusion.14
  25.9 0.6 fusion.2
  26.6 2.0 convolution_bitcast_fusion.2
  28.8 108.1 %psum.22 = f32[8]{0:T(128)S(1)} all-reduce(f32[8]{0:T(128)S(1)} %convert_reduce_fusion), channel_id=1, replica_groups=mesh['blk'=16,'bank'=32] {'blk','bank'}, use_global_device_ids=true, to_apply=%region_3.0 | all-reduce | flops 8 | bytes 64 | tf_op jit(solution)/shard_map/psum | solution.py:40
  136.9 42.7 %reduce-scatter.3.cloned.1.call-done = f32[8,8,128]{2,1,0:T(8,128)} async-done(((f32[256,8,128]{2,1,0:T(8,128)}), f32[8,8,128]{2,1,0:T(8,128)}) %reduce-scatter.3.cloned.1.call-update) | async-done | bytes 32784 | tf_op jit(solution)/shard_map/reduce_scatter | solution.py:49
  179.6 85.1 %psum.21 = f32[8,8,128]{2,1,0:T(8,128)S(1)} all-reduce(f32[8,8,128]{2,1,0:T(8,128)} %reduce-scatter.3.cloned.1.call-done), channel_id=1, replica_groups=mesh['blk'=16,'bank'=32] {'blk'}, use_global_device_ids=true, to_apply=%region_1.0 | all-reduce | flops 8192 | bytes 65536 | tf_op jit(solution)/shard_map/psum | solution.py:55
  264.7 55.8 %all_gather.6 = bf16[256,8,128]{2,1,0:T(8,128)(2,1)S(1)} all-gather(bf16[8,8,128]{2,1,0:T(8,128)(2,1)S(1)} %divide_convert_fusion.1), channel_id=1, replica_groups=mesh['blk'=16,'bank'=32] {'bank'}, dimensions={0}, use_global_device_ids=true | all-gather | bytes 540672 | tf_op jit(solution)/shard_map/all_gather | solution.py:57
  320.6 0.3 fusion.37
  320.9 0.8 copy.6
  321.7 1.1 reshape.96
  322.9 0.5 fusion.10
  323.3 0.6 fusion.1
  324.5 0.5 fusion.11
  325.0 0.6 convolution_log_fusion
  325.7 2.0 convolution_bitcast_fusion.1
  328.0 137.6 %reduce-scatter.5.cloned.1.call-done = f32[8,8,128]{2,1,0:T(8,128)} async-done(((f32[256,8,128]{2,1,0:T(8,128)}), f32[8,8,128]{2,1,0:T(8,128)}) %reduce-scatter.5.cloned.1.call-update) | async-done | bytes 32784 | tf_op jit(solution)/shard_map/reduce_scatter | solution.py:49
  465.6 85.1 %psum.23 = f32[8,8,128]{2,1,0:T(8,128)S(1)} all-reduce(f32[8,8,128]{2,1,0:T(8,128)} %reduce-scatter.5.cloned.1.call-done), channel_id=1, replica_groups=mesh['blk'=16,'bank'=32] {'blk'}, use_global_device_ids=true, to_apply=%region_5.0 | all-reduce | flops 8192 | bytes 65536 | tf_op jit(solution)/shard_map/psum | solution.py:55
  550.8 0.7 fusion.58
  551.5 55.6 %all_gather.7 = bf16[256,8,128]{2,1,0:T(8,128)(2,1)S(1)} all-gather(bf16[8,8,128]{2,1,0:T(8,128)(2,1)S(1)} %divide_convert_fusion), channel_id=1, replica_groups=mesh['blk'=16,'bank'=32] {'bank'}, dimensions={0}, use_global_device_ids=true | all-gather | bytes 540672 | tf_op jit(solution)/shard_map/all_gather | solution.py:57
  607.1 1.1 fusion
  (19 shorter events, 2.0 us)
Async XLA Ops:
  7.2 172.4 %reduce-scatter.3.cloned.1.call-start = ((), (), s32[]{:S(2)}) async-start(), calls=%async_computation.2 | async-start | bytes 1081344 | tf_op jit(solution)/shard_map/reduce_scatter | solution.py:49
  23.8 1.4 copy-start
  25.4 1.2 copy-start.1
  28.6 436.9 %reduce-scatter.5.cloned.1.call-start = ((), (), s32[]{:S(2)}) async-start(), calls=%async_computation.3 | async-start | bytes 1081344 | tf_op jit(solution)/shard_map/reduce_scatter | solution.py:49
Sparse Core Ops, SparseCore 0:
  28.7 150.7 reduce-scatter.2
  327.8 137.7 reduce-scatter.4
where the time goes:
time: 616 us; the launch traced here: 615 us
  blocking collectives  390 us (63%)
  waiting for transfers between devices  180 us (29%)
  local copies, waits for them, and re-layouts  14.5 us (2%)
  between operations  14.2 us (2%)
  matrix products  9.63 us (2%)
  other arithmetic  6.6 us (1%)
    reduce_scatter x2, waiting for transfers between devices, per_device(): lax.psum_scatter(jnp.einsum('km,mrl->rkl', member_weights, blocks, precis...  180 us
    psum x2, blocking collectives, per_device(): summed = lax.psum(reduced, 'blk')  170 us
    all_gather x2, blocking collectives, per_device(): center_all = lax.all_gather(center_slice, 'bank', axis=0, tiled=True)  111 us
    psum x1, blocking collectives, per_device(): counts = lax.psum(jnp.sum(onehot, axis=0), ('blk', 'bank'))  108 us
  transfers between devices with their start and end apart: 2, of which 2 were waited for; matrix products, arithmetic and copies ran while one was open for 0% of the time, Pallas kernels for 0%

commit v1 on v0

--- a/solution.py
+++ b/solution.py
@@ -34,31 +34,34 @@
     kernel_line, kernel_pair = kernel_tables()
     member_count = log_density.shape[0]
     cell_count = log_density.shape[1]
-    row_count = cell_count // 128
+    bank_size = lax.axis_size("bank")
+    owned = cell_count // bank_size
     labels = jnp.arange(BARS, dtype=jnp.int32)
     onehot = (assignment[:, None] == labels[None, :]).astype(jnp.float32)
-    counts = lax.psum(jnp.sum(onehot, axis=0), ("blk", "bank"))
+    local_counts = jnp.sum(onehot, axis=0)
     selector = onehot.astype(jnp.bfloat16)
     member_weights = jnp.transpose(onehot)
     potential = jnp.zeros((member_count, cell_count), jnp.float32)
-    center_owned = jnp.zeros((row_count // lax.axis_size("bank"), BARS, 128), jnp.bfloat16)
+    counts = None
+    center_all = None
     for iteration in range(ITERS):
         source = log_density.astype(jnp.float32) - log_convolve(potential, kernel_line, kernel_pair)
         smoothed = log_convolve(source, kernel_line, kernel_pair)
-        blocks = smoothed.reshape(member_count, row_count, 128)
-        reduced = lax.psum_scatter(
-            jnp.einsum("km,mrl->rkl", member_weights, blocks, precision=lax.Precision.HIGHEST),
-            "bank",
-            scatter_dimension=0,
-            tiled=True,
-        )
-        summed = lax.psum(reduced, "blk")
-        center_slice = (summed / counts[None, :, None]).astype(jnp.bfloat16)
-        center_all = lax.all_gather(center_slice, "bank", axis=0, tiled=True)
-        center_owned = center_slice
-        chosen = jnp.einsum("mk,rkl->mrl", selector, center_all, preferred_element_type=jnp.float32)
-        potential = chosen.reshape(member_count, cell_count) - smoothed
-    centers = jnp.transpose(center_owned, (1, 0, 2)).reshape(BARS, center_owned.shape[0] * 128)
+        local_sums = jnp.dot(member_weights, smoothed, precision=lax.Precision.HIGHEST)
+        if counts is None:
+            packed = jnp.concatenate(
+                [local_sums, jnp.broadcast_to(local_counts[:, None], (BARS, 128))], axis=1
+            )
+            packed = lax.psum(packed, ("blk", "bank"))
+            summed = packed[:, :cell_count]
+            counts = packed[:, cell_count]
+        else:
+            summed = lax.psum(local_sums, ("blk", "bank"))
+        center_all = (summed / counts[:, None]).astype(jnp.bfloat16)
+        chosen = jnp.dot(selector, center_all, preferred_element_type=jnp.float32)
+        potential = chosen - smoothed
+    start = lax.axis_index("bank") * owned
+    centers = lax.dynamic_slice_in_dim(center_all, start, owned, axis=1)
     return (centers, potential)
 
 

time: 616 us -> 600 us (0.974)
  blocking collectives: 390 us -> 0 us
  waiting for transfers between devices: 180 us -> 553 us
    psum x0 -> x2, waiting for transfers between devices: none -> 553 us  [the longest x1 281 us: per_device(): packed = lax.psum(packed, ('blk', 'bank'))]
    psum x3 -> x0, blocking collectives: 278 us -> none  [the longest x2 170 us: per_device(): summed = lax.psum(reduced, 'blk')]
    reduce_scatter x2 -> x0, waiting for transfers between devices: 180 us -> none  [per_device(): lax.psum_scatter(jnp.einsum('km,mrl->rkl', member_weights, blocks, precis...]
    all_gather x2 -> x0, blocking collectives: 111 us -> none  [per_device(): center_all = lax.all_gather(center_slice, 'bank', axis=0, tiled=True)]
where the time goes in v1:
time: 600 us; the launch traced here: 599 us
  waiting for transfers between devices  553 us (92%)
  local copies, waits for them, and re-layouts  14.2 us (2%)
  between operations  14.2 us (2%)
  matrix products  9.59 us (2%)
  other arithmetic  8.21 us (1%)
    psum x1, waiting for transfers between devices, per_device(): packed = lax.psum(packed, ('blk', 'bank'))  281 us
    psum x1, waiting for transfers between devices, per_device(): summed = lax.psum(local_sums, ('blk', 'bank'))  272 us
  transfers between devices with their start and end apart: 2, of which 2 were waited for; matrix products, arithmetic and copies ran while one was open for 0% of the time, Pallas kernels for 0%

profile of v1, /device:TPU:1, one launch (start us, length us, event | category | flops | bytes accessed | tf_op | source)
XLA Modules:
  0.0 599.1 jit_solution(9107554192033985823)
XLA Ops:
  7.2 5.3 multiply_convert_fusion
  12.5 11.3 %reshape.94 = bf16[1024,1024,1]{1,0,2:T(8,128)(2,1)S(1)} reshape(bf16[32,32,32,32]{3,2,1,0:T(8,128)(2,1)} %multiply_convert_fusion) | data formatting | bytes 4194304 | tf_op jit(solution)/shard_map/convert_element_type | solution.py:18
  23.8 0.4 fusion.21
  24.3 0.6 fusion.5
  24.9 0.3 copy.4
  25.5 0.5 fusion.18
  25.9 0.6 fusion.4
  26.5 0.3 copy.6
  27.0 0.8 fusion.37
  27.8 1.1 pad_maximum_fusion
  29.0 281.0 %all-reduce.3.cloned.1.call-done = f32[8,32896]{1,0:T(8,128)} async-done(((f32[8,32896]{1,0:T(8,128)}), f32[8,32896]{1,0:T(8,128)}) %all-reduce.3.cloned.1.call-update) | async-done | bytes 1052688 | tf_op jit(solution)/shard_map/psum | solution.py:55
  310.1 0.8 slice_reduce_fusion
  310.8 1.6 fusion.1
  312.5 0.5 fusion.15
  313.0 0.6 fusion.3
  313.6 0.3 copy.8
  314.1 0.5 fusion.12
  314.6 0.6 fusion.2
  315.2 0.3 copy.10
  315.5 1.8 fusion.36
  317.4 271.8 %all-reduce.5.cloned.1.call-done = f32[8,32768]{1,0:T(8,128)} async-done(((f32[8,32768]{1,0:T(8,128)}), f32[8,32768]{1,0:T(8,128)}) %all-reduce.5.cloned.1.call-update) | async-done | bytes 1048592 | tf_op jit(solution)/shard_map/psum | solution.py:59
  589.2 1.3 divide_convert_fusion
  590.5 1.1 convolution_subtract_fusion
  591.7 0.6 constant_dynamic-slice_fusion
  (13 shorter events, 0.7 us)
Async XLA Ops:
  7.2 302.9 %all-reduce.3.cloned.1.call-start = ((), (), s32[]{:S(2)}) async-start(), calls=%async_computation | async-start | bytes 2105344 | tf_op jit(solution)/shard_map/psum | solution.py:55
  23.8 1.4 copy-start
  25.4 1.4 copy-start.1
  29.0 560.2 %all-reduce.5.cloned.1.call-start = ((), (), s32[]{:S(2)}) async-start(), calls=%async_computation.1 | async-start | bytes 2097152 | tf_op jit(solution)/shard_map/psum | solution.py:59
Sparse Core Ops, SparseCore 0:
  29.1 280.9 all-reduce.2
  317.5 271.6 all-reduce.4

commit v2 on v1

--- a/solution.py
+++ b/solution.py
@@ -44,24 +44,27 @@
     potential = jnp.zeros((member_count, cell_count), jnp.float32)
     counts = None
     center_all = None
+    center_owned = None
     for iteration in range(ITERS):
         source = log_density.astype(jnp.float32) - log_convolve(potential, kernel_line, kernel_pair)
         smoothed = log_convolve(source, kernel_line, kernel_pair)
-        local_sums = jnp.dot(member_weights, smoothed, precision=lax.Precision.HIGHEST)
+        blocks = smoothed.reshape(member_count, bank_size, owned)
+        local_sums = jnp.einsum("km,mrc->rkc", member_weights, blocks, precision=lax.Precision.HIGHEST)
         if counts is None:
-            packed = jnp.concatenate(
-                [local_sums, jnp.broadcast_to(local_counts[:, None], (BARS, 128))], axis=1
+            local_sums = jnp.concatenate(
+                [local_sums, jnp.broadcast_to(local_counts[None, :, None], (bank_size, BARS, 128))], axis=2
             )
-            packed = lax.psum(packed, ("blk", "bank"))
-            summed = packed[:, :cell_count]
-            counts = packed[:, cell_count]
-        else:
-            summed = lax.psum(local_sums, ("blk", "bank"))
-        center_all = (summed / counts[:, None]).astype(jnp.bfloat16)
+        arrived = lax.all_to_all(local_sums, "bank", 0, 0, tiled=True)
+        group_sums = jnp.sum(arrived, axis=0)
+        summed = jnp.sum(lax.all_gather(group_sums, "blk", axis=0), axis=0)
+        if counts is None:
+            counts = summed[:, owned]
+            summed = summed[:, :owned]
+        center_owned = (summed / counts[:, None]).astype(jnp.bfloat16)
+        center_all = lax.all_gather(center_owned, "bank", axis=1, tiled=True)
         chosen = jnp.dot(selector, center_all, preferred_element_type=jnp.float32)
         potential = chosen - smoothed
-    start = lax.axis_index("bank") * owned
-    centers = lax.dynamic_slice_in_dim(center_all, start, owned, axis=1)
+    centers = center_owned
     return (centers, potential)
 
 

time: 600 us -> 294 us (0.49)
  waiting for transfers between devices: 553 us -> 53.5 us
  blocking collectives: 0 us -> 193 us
  starting transfers between devices: 0.08 us -> 14.2 us
  between operations: 14.2 us -> 0.82 us
    psum x2 -> x0, waiting for transfers between devices: 553 us -> none  [the longest x1 281 us: per_device(): packed = lax.psum(packed, ('blk', 'bank'))]
    all_gather x0 -> x4, blocking collectives: none -> 193 us  [the longest x2 99.4 us: per_device(): center_all = lax.all_gather(center_owned, 'bank', axis=1, tiled=True)]
    all_to_all x0 -> x2, waiting for transfers between devices: none -> 53.5 us  [per_device(): arrived = lax.all_to_all(local_sums, 'bank', 0, 0, tiled=True)]
    all_to_all x0 -> x2, starting transfers between devices: none -> 14.2 us  [per_device(): arrived = lax.all_to_all(local_sums, 'bank', 0, 0, tiled=True)]
  transfers between devices with their start and end apart: 2 -> 2, of which waited for: 2 -> 2; matrix products, arithmetic and copies ran while one was open for 0% -> 1% of each run, Pallas kernels for 0% -> 0%
where the time goes in v2:
time: 294 us
  blocking collectives  193 us (66%)
  waiting for transfers between devices  53.5 us (18%)
  local copies, waits for them, and re-layouts  15.5 us (5%)
  starting transfers between devices  14.2 us (5%)
  matrix products  8.71 us (3%)
  other arithmetic  7.83 us (3%)
    all_gather x2, blocking collectives, per_device(): center_all = lax.all_gather(center_owned, 'bank', axis=1, tiled=True)  99.4 us
    all_gather x2, blocking collectives, per_device(): summed = jnp.sum(lax.all_gather(group_sums, 'blk', axis=0), axis=0)  93.8 us
    all_to_all x2, waiting for transfers between devices, per_device(): arrived = lax.all_to_all(local_sums, 'bank', 0, 0, tiled=True)  53.5 us
    all_to_all x2, starting transfers between devices, per_device(): arrived = lax.all_to_all(local_sums, 'bank', 0, 0, tiled=True)  14.2 us
    convert_element_type x1, local copies, waits for them, and re-layouts, kernel_tables(): kernel_pair = (kernel_line[:, None, :, None] * kernel_line[None, :, None,...  11.3 us
  transfers between devices with their start and end apart: 2, of which 2 were waited for; matrix products, arithmetic and copies ran while one was open for 1% of the time, Pallas kernels for 0%

profile of v2, /device:TPU:1, one launch (start us, length us, event | category | flops | bytes accessed | tf_op | source)
XLA Modules:
  0.0 293.7 jit_solution(1050740770468275299)
XLA Ops:
  0.7 5.3 %multiply_convert_fusion = bf16[32,32,32,32]{3,2,1,0:T(8,128)(2,1)} fusion(f32[32,32]{1,0:T(8,128)S(1)} %fusion.22), kind=kLoop, calls=%fused_computation.4 | loop fusion | flops 2097152 | bytes 2101248 | tf_op jit(solution)/shard_map/convert_element_type | solution.py:18
  5.9 11.3 %reshape.96 = bf16[1024,1024,1]{1,0,2:T(8,128)(2,1)S(1)} reshape(bf16[32,32,32,32]{3,2,1,0:T(8,128)(2,1)} %multiply_convert_fusion) | data formatting | bytes 4194304 | tf_op jit(solution)/shard_map/convert_element_type | solution.py:18
  17.7 0.6 fusion.3
  18.9 0.5 fusion.16
  19.4 0.6 convolution_log_fusion.2
  20.1 0.7 copy-done
  20.8 1.0 convolution_bitcast_fusion.1
  21.8 1.1 pad_maximum_fusion
  22.9 10.4 %all-to-all-start = ((f32[32,8,1152]{2,1,0:T(8,128)}), f32[32,8,1152]{2,1,0:T(8,128)S(1)}, u32[]{:S(2)}, u32[]{:S(2)}) async-start(f32[32,8,1152]{2,1,0:T(8,128)} %pad_maximum_fusion), calls=%async_computation | async-start | bytes 2359296 | tf_op jit(solution)/shard_map/all_to_all | solution.py:57
  33.4 2.2 copy.12
  35.6 27.1 %all-to-all-done = f32[32,8,1152]{2,1,0:T(8,128)S(1)} async-done(((f32[32,8,1152]{2,1,0:T(8,128)}), f32[32,8,1152]{2,1,0:T(8,128)S(1)}, u32[]{:S(2)}, u32[]{:S(2)}) %all-to-all-start) | async-done | bytes 1179680 | tf_op jit(solution)/shard_map/all_to_all | solution.py:57
  62.7 0.7 reduce_sum.46
  63.4 51.5 %all-gather = f32[128,1152]{1,0:T(8,128)S(1)} all-gather(f32[8,1152]{1,0:T(8,128)} %reduce_sum.46), channel_id=2, replica_groups=mesh['blk'=16,'bank'=32] {'blk'}, dimensions={0}, use_global_device_ids=true | all-gather | bytes 626688 | tf_op jit(solution)/shard_map/all_gather | solution.py:59
  115.0 51.6 %all_gather.20 = bf16[8,32768]{1,0:T(8,128)(2,1)S(1)} all-gather(bf16[8,1024]{1,0:T(8,128)(2,1)S(1)} %fusion.21), channel_id=1, replica_groups=mesh['blk'=16,'bank'=32] {'bank'}, dimensions={1}, use_global_device_ids=true | all-gather | bytes 540672 | tf_op jit(solution)/shard_map/all_gather | solution.py:64
  167.1 0.5 fusion.13
  167.5 0.6 fusion.2
  168.7 0.5 fusion.10
  169.2 0.6 convolution_log_fusion
  169.8 2.0 convolution_bitcast_fusion
  171.8 3.8 %all-to-all-start.1 = ((f32[32,8,1024]{2,1,0:T(8,128)}), f32[32,8,1024]{2,1,0:T(8,128)S(1)}, u32[]{:S(2)}, u32[]{:S(2)}) async-start(f32[32,8,1024]{2,1,0:T(8,128)} %convolution_bitcast_fusion), calls=%async_computation.1 | async-start | bytes 2097152 | tf_op jit(solution)/shard_map/all_to_all | solution.py:57
  175.9 26.4 %all-to-all-done.1 = f32[32,8,1024]{2,1,0:T(8,128)S(1)} async-done(((f32[32,8,1024]{2,1,0:T(8,128)}), f32[32,8,1024]{2,1,0:T(8,128)S(1)}, u32[]{:S(2)}, u32[]{:S(2)}) %all-to-all-start.1) | async-done | bytes 1048608 | tf_op jit(solution)/shard_map/all_to_all | solution.py:57
  202.3 42.3 %all-gather.1 = f32[128,1024]{1,0:T(8,128)S(1)} all-gather(f32[8,1024]{1,0:T(8,128)S(1)} %reduce_sum.48), channel_id=3, replica_groups=mesh['blk'=16,'bank'=32] {'blk'}, dimensions={0}, use_global_device_ids=true | all-gather | bytes 557056 | tf_op jit(solution)/shard_map/all_gather | solution.py:59
  244.8 47.8 %all_gather.23 = bf16[8,32768]{1,0:T(8,128)(2,1)S(1)} all-gather(bf16[8,1024]{1,0:T(8,128)(2,1)S(1)} %divide_convert_fusion), channel_id=1, replica_groups=mesh['blk'=16,'bank'=32] {'bank'}, dimensions={1}, use_global_device_ids=true | all-gather | bytes 540672 | tf_op jit(solution)/shard_map/all_gather | solution.py:64
  292.6 1.1 convolution_subtract_fusion
  (25 shorter events, 2.9 us)
Async XLA Ops:
  17.2 1.4 copy-start.2
  18.9 1.1 copy-start.4
  20.0 0.8 copy-start
  22.9 39.7 %all-to-all-start = ((f32[32,8,1152]{2,1,0:T(8,128)}), f32[32,8,1152]{2,1,0:T(8,128)S(1)}, u32[]{:S(2)}, u32[]{:S(2)}) async-start(f32[32,8,1152]{2,1,0:T(8,128)} %pad_maximum_fusion), calls=%async_computation | async-start | bytes 2359296 | tf_op jit(solution)/shard_map/all_to_all | solution.py:57
  63.4 103.3 %copy-start.1 = (f32[1,4,32,1024]{3,1,2,0:T(4,128)S(1)}, f32[1,4,32,1024]{3,1,2,0:T(4,128)}, u32[]{:S(2)}) copy-start(f32[1,4,32,1024]{3,1,2,0:T(4,128)} %copy.12) | copy-start | bytes 1572868
  171.8 30.5 %all-to-all-start.1 = ((f32[32,8,1024]{2,1,0:T(8,128)}), f32[32,8,1024]{2,1,0:T(8,128)S(1)}, u32[]{:S(2)}, u32[]{:S(2)}) async-start(f32[32,8,1024]{2,1,0:T(8,128)} %convolution_bitcast_fusion), calls=%async_computation.1 | async-start | bytes 2097152 | tf_op jit(solution)/shard_map/all_to_all | solution.py:57
  244.8 49.0 %copy-start.3 = (bf16[8,1024]{1,0:T(8,128)(2,1)}, bf16[8,1024]{1,0:T(8,128)(2,1)S(1)}, u32[]{:S(2)}) copy-start(bf16[8,1024]{1,0:T(8,128)(2,1)S(1)} %divide_convert_fusion) | copy-start | bytes 49156

commit v3 on v2

--- a/solution.py
+++ b/solution.py
@@ -36,6 +36,8 @@
     cell_count = log_density.shape[1]
     bank_size = lax.axis_size("bank")
     owned = cell_count // bank_size
+    blk_size = lax.axis_size("blk")
+    blk_levels = blk_size.bit_length() - 1
     labels = jnp.arange(BARS, dtype=jnp.int32)
     onehot = (assignment[:, None] == labels[None, :]).astype(jnp.float32)
     local_counts = jnp.sum(onehot, axis=0)
@@ -56,14 +58,18 @@
             )
         arrived = lax.all_to_all(local_sums, "bank", 0, 0, tiled=True)
         group_sums = jnp.sum(arrived, axis=0)
-        summed = jnp.sum(lax.all_gather(group_sums, "blk", axis=0), axis=0)
+        summed = group_sums
+        for level in range(blk_levels):
+            partner = [(i, i ^ (1 << level)) for i in range(blk_size)]
+            summed = summed + lax.ppermute(summed, "blk", partner)
         if counts is None:
             counts = summed[:, owned]
             summed = summed[:, :owned]
         center_owned = (summed / counts[:, None]).astype(jnp.bfloat16)
-        center_all = lax.all_gather(center_owned, "bank", axis=1, tiled=True)
-        chosen = jnp.dot(selector, center_all, preferred_element_type=jnp.float32)
-        potential = chosen - smoothed
+        spread = jnp.broadcast_to(center_owned[None], (bank_size, BARS, owned))
+        center_all = lax.all_to_all(spread, "bank", 0, 0, tiled=True)
+        chosen = jnp.einsum("mk,rkc->mrc", selector, center_all, preferred_element_type=jnp.float32)
+        potential = chosen.reshape(member_count, cell_count) - smoothed
     centers = center_owned
     return (centers, potential)
 

time: 294 us -> 209 us (0.71)
  blocking collectives: 193 us -> 122 us
  waiting for transfers between devices: 53.5 us -> 17 us
  starting transfers between devices: 14.2 us -> 40.7 us
    all_gather x4 -> x0, blocking collectives: 193 us -> none  [the longest x2 99.4 us: per_device(): center_all = lax.all_gather(center_owned, 'bank', axis=1, tiled=True)]
    all_to_all x0 -> x4, blocking collectives: none -> 122 us  [the longest x2 71.7 us: per_device(): arrived = lax.all_to_all(local_sums, 'bank', 0, 0, tiled=True)]
    all_to_all x2 -> x0, waiting for transfers between devices: 53.5 us -> none  [per_device(): arrived = lax.all_to_all(local_sums, 'bank', 0, 0, tiled=True)]
    ppermute x0 -> x8, starting transfers between devices: none -> 40.7 us  [per_device(): summed = summed + lax.ppermute(summed, 'blk', partner)]
    ppermute x0 -> x8, waiting for transfers between devices: none -> 17 us  [per_device(): summed = summed + lax.ppermute(summed, 'blk', partner)]
    all_to_all x2 -> x0, starting transfers between devices: 14.2 us -> none  [per_device(): arrived = lax.all_to_all(local_sums, 'bank', 0, 0, tiled=True)]
  transfers between devices with their start and end apart: 2 -> 8, of which waited for: 2 -> 8; matrix products, arithmetic and copies ran while one was open for 1% -> 0% of each run, Pallas kernels for 0% -> 0%
where the time goes in v3:
time: 209 us; the launch traced here: 208 us
  blocking collectives  122 us (58%)
  starting transfers between devices  40.7 us (19%)
  waiting for transfers between devices  17 us (8%)
  local copies, waits for them, and re-layouts  13.5 us (6%)
  other arithmetic  7.77 us (4%)
  matrix products  7.13 us (3%)
    all_to_all x2, blocking collectives, per_device(): arrived = lax.all_to_all(local_sums, 'bank', 0, 0, tiled=True)  71.7 us
    all_to_all x2, blocking collectives, per_device(): center_all = lax.all_to_all(spread, 'bank', 0, 0, tiled=True)  49.8 us
    ppermute x8, starting transfers between devices, per_device(): summed = summed + lax.ppermute(summed, 'blk', partner)  40.7 us
    ppermute x8, waiting for transfers between devices, per_device(): summed = summed + lax.ppermute(summed, 'blk', partner)  17 us
    convert_element_type x1, local copies, waits for them, and re-layouts, kernel_tables(): kernel_pair = (kernel_line[:, None, :, None] * kernel_line[None, :, None,...  11.3 us
    convert_element_type x1, other arithmetic, kernel_tables(): kernel_pair = (kernel_line[:, None, :, None] * kernel_line[None, :, None,...  5.26 us
  transfers between devices with their start and end apart: 8, of which 8 were waited for; matrix products, arithmetic and copies ran while one was open for 0% of the time, Pallas kernels for 0%

profile of v3, /device:TPU:1, one launch (start us, length us, event | category | flops | bytes accessed | tf_op | source)
XLA Modules:
  0.0 208.5 jit_solution(15238067035781722975)
XLA Ops:
  0.7 5.3 %multiply_convert_fusion = bf16[32,32,32,32]{3,2,1,0:T(8,128)(2,1)} fusion(f32[32,32]{1,0:T(8,128)S(1)} %fusion.24), kind=kLoop, calls=%fused_computation | loop fusion | flops 2097152 | bytes 2101248 | tf_op jit(solution)/shard_map/convert_element_type | solution.py:18
  5.9 11.3 %reshape.92 = bf16[1024,1024,1]{1,0,2:T(8,128)(2,1)S(1)} reshape(bf16[32,32,32,32]{3,2,1,0:T(8,128)(2,1)} %multiply_convert_fusion) | data formatting | bytes 4194304 | tf_op jit(solution)/shard_map/convert_element_type | solution.py:18
  21.2 41.2 %all_to_all.20 = f32[32,8,1152]{2,1,0:T(8,128)} all-to-all(f32[32,8,1152]{2,1,0:T(8,128)S(1)} %pad_maximum_fusion), channel_id=1, replica_groups=mesh['blk'=16,'bank'=32] {'bank'}, dimensions={0} | all-to-all | bytes 2359296 | tf_op jit(solution)/shard_map/all_to_all | solution.py:59
  62.4 1.3 reduce_sum.28
  63.7 2.6 %collective-permute-start = (f32[8,1152]{1,0:T(8,128)S(1)}, f32[8,1152]{1,0:T(8,128)S(1)}, u32[]{:S(2)}, u32[]{:S(2)}) collective-permute-start(f32[8,1152]{1,0:T(8,128)S(1)} %reduce_sum.28), channel_id=1, source_target_pairs={{0,32},{32,0},{64,96},{96,64},{128,160},{160,128},{192,224},{224,1... | collective-permute-start | bytes 110600 | tf_op jit(solution)/shard_map/ppermute | solution.py:64
  66.3 2.1 %collective-permute-done = f32[8,1152]{1,0:T(8,128)S(1)} collective-permute-done((f32[8,1152]{1,0:T(8,128)S(1)}, f32[8,1152]{1,0:T(8,128)S(1)}, u32[]{:S(2)}, u32[]{:S(2)}) %collective-permute-start) | collective-permute-done | bytes 36896 | tf_op jit(solution)/shard_map/ppermute | solution.py:64
  68.4 5.1 %collective-permute-start.1 = (f32[8,1152]{1,0:T(8,128)S(1)}, f32[8,1152]{1,0:T(8,128)S(1)}, u32[]{:S(2)}, u32[]{:S(2)}) collective-permute-start(f32[8,1152]{1,0:T(8,128)S(1)} %add.24), channel_id=1, source_target_pairs={{0,64},{32,96},{64,0},{96,32},{128,192},{160,224},{192,128},{224,1... | collective-permute-start | bytes 110600 | tf_op jit(solution)/shard_map/ppermute | solution.py:64
  73.5 1.3 collective-permute-done.1
  74.8 8.4 %collective-permute-start.2 = (f32[8,1152]{1,0:T(8,128)S(1)}, f32[8,1152]{1,0:T(8,128)S(1)}, u32[]{:S(2)}, u32[]{:S(2)}) collective-permute-start(f32[8,1152]{1,0:T(8,128)S(1)} %add.25), channel_id=1, source_target_pairs={{0,128},{32,160},{64,192},{96,224},{128,0},{160,32},{192,64},{224,... | collective-permute-start | bytes 110600 | tf_op jit(solution)/shard_map/ppermute | solution.py:64
  83.3 1.4 collective-permute-done.2
  84.7 4.8 %collective-permute-start.3 = (f32[8,1152]{1,0:T(8,128)S(1)}, f32[8,1152]{1,0:T(8,128)S(1)}, u32[]{:S(2)}, u32[]{:S(2)}) collective-permute-start(f32[8,1152]{1,0:T(8,128)S(1)} %add.26), channel_id=1, source_target_pairs={{0,256},{32,288},{64,320},{96,352},{128,384},{160,416},{192,448},{... | collective-permute-start | bytes 110600 | tf_op jit(solution)/shard_map/ppermute | solution.py:64
  89.4 3.8 %collective-permute-done.3 = f32[8,1152]{1,0:T(8,128)S(1)} collective-permute-done((f32[8,1152]{1,0:T(8,128)S(1)}, f32[8,1152]{1,0:T(8,128)S(1)}, u32[]{:S(2)}, u32[]{:S(2)}) %collective-permute-start.3) | collective-permute-done | bytes 36896 | tf_op jit(solution)/shard_map/ppermute | solution.py:64
  93.5 24.5 %all_to_all.21 = bf16[32,8,1024]{2,1,0:T(8,128)(2,1)S(1)} all-to-all(bf16[32,8,1024]{2,1,0:T(8,128)(2,1)S(1)} %broadcast_in_dim.7), channel_id=1, replica_groups=mesh['blk'=16,'bank'=32] {'bank'}, dimensions={0} | all-to-all | bytes 1048576 | tf_op jit(solution)/shard_map/all_to_all | solution.py:70
  122.3 30.5 %all_to_all.22 = f32[32,8,1024]{2,1,0:T(8,128)S(1)} all-to-all(f32[32,8,1024]{2,1,0:T(8,128)S(1)} %convolution_bitcast_fusion), channel_id=1, replica_groups=mesh['blk'=16,'bank'=32] {'bank'}, dimensions={0} | all-to-all | bytes 2097152 | tf_op jit(solution)/shard_map/all_to_all | solution.py:59
  152.9 3.1 %collective-permute-start.4 = (f32[8,1024]{1,0:T(8,128)S(1)}, f32[8,1024]{1,0:T(8,128)S(1)}, u32[]{:S(2)}, u32[]{:S(2)}) collective-permute-start(f32[8,1024]{1,0:T(8,128)S(1)} %reduce_sum.29), channel_id=1, source_target_pairs={{0,32},{32,0},{64,96},{96,64},{128,160},{160,128},{192,224},{224,1... | collective-permute-start | bytes 98312 | tf_op jit(solution)/shard_map/ppermute | solution.py:64
  156.0 2.0 collective-permute-done.4
  158.0 4.6 %collective-permute-start.5 = (f32[8,1024]{1,0:T(8,128)S(1)}, f32[8,1024]{1,0:T(8,128)S(1)}, u32[]{:S(2)}, u32[]{:S(2)}) collective-permute-start(f32[8,1024]{1,0:T(8,128)S(1)} %add.28), channel_id=1, source_target_pairs={{0,64},{32,96},{64,0},{96,32},{128,192},{160,224},{192,128},{224,1... | collective-permute-start | bytes 98312 | tf_op jit(solution)/shard_map/ppermute | solution.py:64
  162.6 1.3 collective-permute-done.5
  163.9 7.5 %collective-permute-start.6 = (f32[8,1024]{1,0:T(8,128)S(1)}, f32[8,1024]{1,0:T(8,128)S(1)}, u32[]{:S(2)}, u32[]{:S(2)}) collective-permute-start(f32[8,1024]{1,0:T(8,128)S(1)} %add.29), channel_id=1, source_target_pairs={{0,128},{32,160},{64,192},{96,224},{128,0},{160,32},{192,64},{224,... | collective-permute-start | bytes 98312 | tf_op jit(solution)/shard_map/ppermute | solution.py:64
  171.4 1.3 collective-permute-done.6
  172.7 4.8 %collective-permute-start.7 = (f32[8,1024]{1,0:T(8,128)S(1)}, f32[8,1024]{1,0:T(8,128)S(1)}, u32[]{:S(2)}, u32[]{:S(2)}) collective-permute-start(f32[8,1024]{1,0:T(8,128)S(1)} %add.30), channel_id=1, source_target_pairs={{0,256},{32,288},{64,320},{96,352},{128,384},{160,416},{192,448},{... | collective-permute-start | bytes 98312 | tf_op jit(solution)/shard_map/ppermute | solution.py:64
  177.5 3.8 %collective-permute-done.7 = f32[8,1024]{1,0:T(8,128)S(1)} collective-permute-done((f32[8,1024]{1,0:T(8,128)S(1)}, f32[8,1024]{1,0:T(8,128)S(1)}, u32[]{:S(2)}, u32[]{:S(2)}) %collective-permute-start.7) | collective-permute-done | bytes 32800 | tf_op jit(solution)/shard_map/ppermute | solution.py:64
  181.4 25.3 %all_to_all.23 = bf16[32,8,1024]{2,1,0:T(8,128)(2,1)S(1)} all-to-all(bf16[32,8,1024]{2,1,0:T(8,128)(2,1)S(1)} %broadcast_in_dim.8), channel_id=1, replica_groups=mesh['blk'=16,'bank'=32] {'bank'}, dimensions={0} | all-to-all | bytes 1048576 | tf_op jit(solution)/shard_map/all_to_all | solution.py:70
  207.3 1.1 copy.12
  (40 shorter events, 9.3 us)
Async XLA Ops:
  17.2 1.4 copy-start
  18.9 1.1 copy-start.2
  63.7 4.7 %collective-permute-start = (f32[8,1152]{1,0:T(8,128)S(1)}, f32[8,1152]{1,0:T(8,128)S(1)}, u32[]{:S(2)}, u32[]{:S(2)}) collective-permute-start(f32[8,1152]{1,0:T(8,128)S(1)} %reduce_sum.28), channel_id=1, source_target_pairs={{0,32},{32,0},{64,96},{96,64},{128,160},{160,128},{192,224},{224,1... | collective-permute-start | bytes 110600 | tf_op jit(solution)/shard_map/ppermute | solution.py:64
  68.4 6.4 %collective-permute-start.1 = (f32[8,1152]{1,0:T(8,128)S(1)}, f32[8,1152]{1,0:T(8,128)S(1)}, u32[]{:S(2)}, u32[]{:S(2)}) collective-permute-start(f32[8,1152]{1,0:T(8,128)S(1)} %add.24), channel_id=1, source_target_pairs={{0,64},{32,96},{64,0},{96,32},{128,192},{160,224},{192,128},{224,1... | collective-permute-start | bytes 110600 | tf_op jit(solution)/shard_map/ppermute | solution.py:64
  74.8 9.8 %collective-permute-start.2 = (f32[8,1152]{1,0:T(8,128)S(1)}, f32[8,1152]{1,0:T(8,128)S(1)}, u32[]{:S(2)}, u32[]{:S(2)}) collective-permute-start(f32[8,1152]{1,0:T(8,128)S(1)} %add.25), channel_id=1, source_target_pairs={{0,128},{32,160},{64,192},{96,224},{128,0},{160,32},{192,64},{224,... | collective-permute-start | bytes 110600 | tf_op jit(solution)/shard_map/ppermute | solution.py:64
  84.7 8.6 %collective-permute-start.3 = (f32[8,1152]{1,0:T(8,128)S(1)}, f32[8,1152]{1,0:T(8,128)S(1)}, u32[]{:S(2)}, u32[]{:S(2)}) collective-permute-start(f32[8,1152]{1,0:T(8,128)S(1)} %add.26), channel_id=1, source_target_pairs={{0,256},{32,288},{64,320},{96,352},{128,384},{160,416},{192,448},{... | collective-permute-start | bytes 110600 | tf_op jit(solution)/shard_map/ppermute | solution.py:64
  152.9 5.0 %collective-permute-start.4 = (f32[8,1024]{1,0:T(8,128)S(1)}, f32[8,1024]{1,0:T(8,128)S(1)}, u32[]{:S(2)}, u32[]{:S(2)}) collective-permute-start(f32[8,1024]{1,0:T(8,128)S(1)} %reduce_sum.29), channel_id=1, source_target_pairs={{0,32},{32,0},{64,96},{96,64},{128,160},{160,128},{192,224},{224,1... | collective-permute-start | bytes 98312 | tf_op jit(solution)/shard_map/ppermute | solution.py:64
  158.0 5.9 %collective-permute-start.5 = (f32[8,1024]{1,0:T(8,128)S(1)}, f32[8,1024]{1,0:T(8,128)S(1)}, u32[]{:S(2)}, u32[]{:S(2)}) collective-permute-start(f32[8,1024]{1,0:T(8,128)S(1)} %add.28), channel_id=1, source_target_pairs={{0,64},{32,96},{64,0},{96,32},{128,192},{160,224},{192,128},{224,1... | collective-permute-start | bytes 98312 | tf_op jit(solution)/shard_map/ppermute | solution.py:64
  163.9 8.8 %collective-permute-start.6 = (f32[8,1024]{1,0:T(8,128)S(1)}, f32[8,1024]{1,0:T(8,128)S(1)}, u32[]{:S(2)}, u32[]{:S(2)}) collective-permute-start(f32[8,1024]{1,0:T(8,128)S(1)} %add.29), channel_id=1, source_target_pairs={{0,128},{32,160},{64,192},{96,224},{128,0},{160,32},{192,64},{224,... | collective-permute-start | bytes 98312 | tf_op jit(solution)/shard_map/ppermute | solution.py:64
  172.7 8.6 %collective-permute-start.7 = (f32[8,1024]{1,0:T(8,128)S(1)}, f32[8,1024]{1,0:T(8,128)S(1)}, u32[]{:S(2)}, u32[]{:S(2)}) collective-permute-start(f32[8,1024]{1,0:T(8,128)S(1)} %add.30), channel_id=1, source_target_pairs={{0,256},{32,288},{64,320},{96,352},{128,384},{160,416},{192,448},{... | collective-permute-start | bytes 98312 | tf_op jit(solution)/shard_map/ppermute | solution.py:64
  181.3 26.0 %copy-start.1 = (bf16[8,1024]{1,0:T(8,128)(2,1)}, bf16[8,1024]{1,0:T(8,128)(2,1)S(1)}, u32[]{:S(2)}) copy-start(bf16[8,1024]{1,0:T(8,128)(2,1)S(1)} %divide_convert_fusion) | copy-start | bytes 49156

commit v4 on v3

--- a/solution.py
+++ b/solution.py
@@ -12,11 +12,14 @@
     grid_pos = jnp.arange(G, dtype=jnp.float32)
     offset = grid_pos[:, None] - grid_pos[None, :]
     kernel_line = jnp.exp(-0.5 * offset * offset)
-    kernel_pair = (
-        (kernel_line[:, None, :, None] * kernel_line[None, :, None, :])
-        .reshape(G * G, G * G)
-        .astype(jnp.bfloat16)
-    )
+    row = lax.broadcasted_iota(jnp.int32, (G * G, G * G), 0)
+    col = lax.broadcasted_iota(jnp.int32, (G * G, G * G), 1)
+
+    def line_at(a, b):
+        gap = a.astype(jnp.float32) - b.astype(jnp.float32)
+        return jnp.exp(-0.5 * gap * gap)
+
+    kernel_pair = (line_at(row // G, col // G) * line_at(row % G, col % G)).astype(jnp.bfloat16)
     return (kernel_line, kernel_pair)
 
 

time: 209 us -> 198 us (0.947)
  local copies, waits for them, and re-layouts: 13.5 us -> 2.14 us
  matrix products: 7.13 us -> 13.4 us
  other arithmetic: 7.77 us -> 1.91 us
    convert_element_type x1 -> x0, local copies, waits for them, and re-layouts: 11.3 us -> none  [kernel_tables(): kernel_pair = (kernel_line[:, None, :, None] * kernel_line[None, :, None,...]
    dot_general x4, matrix products: 2.14 us -> 8.36 us  [log_convolve(): jnp.dot(raised, kernel_pair, preferred_element_type=jnp.float32)]
    convert_element_type x1 -> x0, other arithmetic: 5.26 us -> none  [kernel_tables(): kernel_pair = (kernel_line[:, None, :, None] * kernel_line[None, :, None,...]
where the time goes in v4:
time: 198 us; the launch traced here: 197 us
  blocking collectives  121 us (61%)
  starting transfers between devices  41.9 us (21%)
  waiting for transfers between devices  16.4 us (8%)
  matrix products  13.4 us (7%)
  local copies, waits for them, and re-layouts  2.14 us (1%)
    all_to_all x2, blocking collectives, per_device(): arrived = lax.all_to_all(local_sums, 'bank', 0, 0, tiled=True)  71 us
    all_to_all x2, blocking collectives, per_device(): center_all = lax.all_to_all(spread, 'bank', 0, 0, tiled=True)  49.8 us
    ppermute x8, starting transfers between devices, per_device(): summed = summed + lax.ppermute(summed, 'blk', partner)  41.9 us
    ppermute x8, waiting for transfers between devices, per_device(): summed = summed + lax.ppermute(summed, 'blk', partner)  16.4 us
    dot_general x4, matrix products, log_convolve(): jnp.dot(raised, kernel_pair, preferred_element_type=jnp.float32)  8.36 us
  transfers between devices with their start and end apart: 8, of which 8 were waited for; matrix products, arithmetic and copies ran while one was open for 0% of the time, Pallas kernels for 0%

profile of v4, /device:TPU:1, one launch (start us, length us, event | category | flops | bytes accessed | tf_op | source)
XLA Modules:
  0.0 197.4 jit_solution(11035686401145765933)
XLA Ops:
  1.4 2.0 %fusion.26 = f32[4,32,1024]{2,1,0:T(8,128)S(1)} fusion(s32[1024]{0:T(1024)S(1)} %get-tuple-element.3, s32[1024]{0:T(1024)S(1)} %get-tuple-element.4, s32[1024]{0:T(1024)S(1)} %get-tuple-element.2, s32[1024]{0:T(1024)S(1)} %get-tuple-element.5, pred[1024]{0:T(1024)(128)(4,1)S(1)} %get-tuple-element.6, pred[1024]{0:T(1024)(128)(4,1)S(1)} %get-tuple-element.7), kind=kOutput, calls=%fused_computation.38 | convolution fusion | flops 285212672 | bytes 542720 | tf_op jit(solution)/shard_map/dot_general | solution.py:29
  4.6 2.1 %fusion.23 = f32[4,32,1024]{2,1,0:T(8,128)S(1)} fusion(bf16[1,4,32,1024]{3,1,2,0:T(4,128)(2,1)S(1)} %bitcast.57, s32[1024]{0:T(1024)S(1)} %get-tuple-element.3, s32[1024]{0:T(1024)S(1)} %get-tuple-element.4, s32[1024]{0:T(1024)S(1)} %get-tuple-element.2, s32[1024]{0:T(1024)S(1)} %get-tuple-element.5, pred[1024]{0:T(1024)(128)(4,1)S(1)} %get-tuple-element.6, ...), kind=kOutput, calls=%fused_computation.35 | convolution fusion | flops 285212672 | bytes 804864 | tf_op jit(solution)/shard_map/dot_general | solution.py:29
  8.4 40.5 %all_to_all.20 = f32[32,8,1152]{2,1,0:T(8,128)S(1)} all-to-all(f32[32,8,1152]{2,1,0:T(8,128)S(1)} %pad_maximum_fusion), channel_id=1, replica_groups=mesh['blk'=16,'bank'=32] {'bank'}, dimensions={0} | all-to-all | bytes 2359296 | tf_op jit(solution)/shard_map/all_to_all | solution.py:62
  49.0 3.2 %collective-permute-start = (f32[8,1152]{1,0:T(8,128)S(1)}, f32[8,1152]{1,0:T(8,128)S(1)}, u32[]{:S(2)}, u32[]{:S(2)}) collective-permute-start(f32[8,1152]{1,0:T(8,128)S(1)} %reduce_sum.28), channel_id=1, source_target_pairs={{0,32},{32,0},{64,96},{96,64},{128,160},{160,128},{192,224},{224,1... | collective-permute-start | bytes 110600 | tf_op jit(solution)/shard_map/ppermute | solution.py:67
  52.2 1.5 collective-permute-done
  53.7 5.6 %collective-permute-start.1 = (f32[8,1152]{1,0:T(8,128)S(1)}, f32[8,1152]{1,0:T(8,128)S(1)}, u32[]{:S(2)}, u32[]{:S(2)}) collective-permute-start(f32[8,1152]{1,0:T(8,128)S(1)} %add.45), channel_id=1, source_target_pairs={{0,64},{32,96},{64,0},{96,32},{128,192},{160,224},{192,128},{224,1... | collective-permute-start | bytes 110600 | tf_op jit(solution)/shard_map/ppermute | solution.py:67
  59.4 1.3 collective-permute-done.1
  60.7 8.4 %collective-permute-start.2 = (f32[8,1152]{1,0:T(8,128)S(1)}, f32[8,1152]{1,0:T(8,128)S(1)}, u32[]{:S(2)}, u32[]{:S(2)}) collective-permute-start(f32[8,1152]{1,0:T(8,128)S(1)} %add.46), channel_id=1, source_target_pairs={{0,128},{32,160},{64,192},{96,224},{128,0},{160,32},{192,64},{224,... | collective-permute-start | bytes 110600 | tf_op jit(solution)/shard_map/ppermute | solution.py:67
  69.1 1.4 collective-permute-done.2
  70.5 4.7 %collective-permute-start.3 = (f32[8,1152]{1,0:T(8,128)S(1)}, f32[8,1152]{1,0:T(8,128)S(1)}, u32[]{:S(2)}, u32[]{:S(2)}) collective-permute-start(f32[8,1152]{1,0:T(8,128)S(1)} %add.47), channel_id=1, source_target_pairs={{0,256},{32,288},{64,320},{96,352},{128,384},{160,416},{192,448},{... | collective-permute-start | bytes 110600 | tf_op jit(solution)/shard_map/ppermute | solution.py:67
  75.3 3.8 %collective-permute-done.3 = f32[8,1152]{1,0:T(8,128)S(1)} collective-permute-done((f32[8,1152]{1,0:T(8,128)S(1)}, f32[8,1152]{1,0:T(8,128)S(1)}, u32[]{:S(2)}, u32[]{:S(2)}) %collective-permute-start.3) | collective-permute-done | bytes 36896 | tf_op jit(solution)/shard_map/ppermute | solution.py:67
  79.4 24.5 %all_to_all.21 = bf16[32,8,1024]{2,1,0:T(8,128)(2,1)S(1)} all-to-all(bf16[32,8,1024]{2,1,0:T(8,128)(2,1)S(1)} %broadcast_in_dim.7), channel_id=1, replica_groups=mesh['blk'=16,'bank'=32] {'bank'}, dimensions={0} | all-to-all | bytes 1048576 | tf_op jit(solution)/shard_map/all_to_all | solution.py:73
  104.2 2.2 %fusion.18 = f32[4,32,1024]{2,1,0:T(8,128)S(1)} fusion(f32[4,32,1024]{2,1,0:T(8,128)S(1)} %fusion.7, f32[4,32,1024]{2,0,1:T(4,128)S(1)} %fusion.51, s32[1024]{0:T(1024)S(1)} %get-tuple-element.3, s32[1024]{0:T(1024)S(1)} %get-tuple-element.4, s32[1024]{0:T(1024)S(1)} %get-tuple-element.2, s32[1024]{0:T(1024)S(1)} %get-tuple-element.5, ...), kind=kOutput, calls=%fused_computation.31 | convolution fusion | flops 285474816 | bytes 1591296 | tf_op jit(solution)/shard_map/dot_general | solution.py:29
  107.6 2.1 %fusion.20 = f32[4,32,1024]{2,1,0:T(8,128)S(1)} fusion(bf16[1,4,32,1024]{3,1,2,0:T(4,128)(2,1)S(1)} %bitcast.56, s32[1024]{0:T(1024)S(1)} %get-tuple-element.3, s32[1024]{0:T(1024)S(1)} %get-tuple-element.4, s32[1024]{0:T(1024)S(1)} %get-tuple-element.2, s32[1024]{0:T(1024)S(1)} %get-tuple-element.5, pred[1024]{0:T(1024)(128)(4,1)S(1)} %get-tuple-element.6, ...), kind=kOutput, calls=%fused_computation.32 | convolution fusion | flops 285212672 | bytes 804864 | tf_op jit(solution)/shard_map/dot_general | solution.py:29
  111.3 30.5 %all_to_all.22 = f32[32,8,1024]{2,1,0:T(8,128)S(1)} all-to-all(f32[32,8,1024]{2,1,0:T(8,128)S(1)} %convolution_bitcast_fusion), channel_id=1, replica_groups=mesh['blk'=16,'bank'=32] {'bank'}, dimensions={0} | all-to-all | bytes 2097152 | tf_op jit(solution)/shard_map/all_to_all | solution.py:62
  141.9 3.1 %collective-permute-start.4 = (f32[8,1024]{1,0:T(8,128)S(1)}, f32[8,1024]{1,0:T(8,128)S(1)}, u32[]{:S(2)}, u32[]{:S(2)}) collective-permute-start(f32[8,1024]{1,0:T(8,128)S(1)} %reduce_sum.29), channel_id=1, source_target_pairs={{0,32},{32,0},{64,96},{96,64},{128,160},{160,128},{192,224},{224,1... | collective-permute-start | bytes 98312 | tf_op jit(solution)/shard_map/ppermute | solution.py:67
  144.9 2.0 collective-permute-done.4
  146.9 4.6 %collective-permute-start.5 = (f32[8,1024]{1,0:T(8,128)S(1)}, f32[8,1024]{1,0:T(8,128)S(1)}, u32[]{:S(2)}, u32[]{:S(2)}) collective-permute-start(f32[8,1024]{1,0:T(8,128)S(1)} %add.49), channel_id=1, source_target_pairs={{0,64},{32,96},{64,0},{96,32},{128,192},{160,224},{192,128},{224,1... | collective-permute-start | bytes 98312 | tf_op jit(solution)/shard_map/ppermute | solution.py:67
  151.5 1.3 collective-permute-done.5
  152.8 7.5 %collective-permute-start.6 = (f32[8,1024]{1,0:T(8,128)S(1)}, f32[8,1024]{1,0:T(8,128)S(1)}, u32[]{:S(2)}, u32[]{:S(2)}) collective-permute-start(f32[8,1024]{1,0:T(8,128)S(1)} %add.50), channel_id=1, source_target_pairs={{0,128},{32,160},{64,192},{96,224},{128,0},{160,32},{192,64},{224,... | collective-permute-start | bytes 98312 | tf_op jit(solution)/shard_map/ppermute | solution.py:67
  160.3 1.3 collective-permute-done.6
  161.6 4.7 %collective-permute-start.7 = (f32[8,1024]{1,0:T(8,128)S(1)}, f32[8,1024]{1,0:T(8,128)S(1)}, u32[]{:S(2)}, u32[]{:S(2)}) collective-permute-start(f32[8,1024]{1,0:T(8,128)S(1)} %add.51), channel_id=1, source_target_pairs={{0,256},{32,288},{64,320},{96,352},{128,384},{160,416},{192,448},{... | collective-permute-start | bytes 98312 | tf_op jit(solution)/shard_map/ppermute | solution.py:67
  166.4 3.8 %collective-permute-done.7 = f32[8,1024]{1,0:T(8,128)S(1)} collective-permute-done((f32[8,1024]{1,0:T(8,128)S(1)}, f32[8,1024]{1,0:T(8,128)S(1)}, u32[]{:S(2)}, u32[]{:S(2)}) %collective-permute-start.7) | collective-permute-done | bytes 32800 | tf_op jit(solution)/shard_map/ppermute | solution.py:67
  170.3 25.3 %all_to_all.23 = bf16[32,8,1024]{2,1,0:T(8,128)(2,1)S(1)} all-to-all(bf16[32,8,1024]{2,1,0:T(8,128)(2,1)S(1)} %broadcast_in_dim.8), channel_id=1, replica_groups=mesh['blk'=16,'bank'=32] {'bank'}, dimensions={0} | all-to-all | bytes 1048576 | tf_op jit(solution)/shard_map/all_to_all | solution.py:73
  (40 shorter events, 9.0 us)
Async XLA Ops:
  3.4 1.0 copy-start
  4.6 2.7 %copy-start.2 = (s32[4]{0:T(128)S(1)}, s32[4]{0:T(128)}, u32[]{:S(2)}) copy-start(s32[4]{0:T(128)} %param.3) | copy-start | bytes 52
  49.0 4.7 %collective-permute-start = (f32[8,1152]{1,0:T(8,128)S(1)}, f32[8,1152]{1,0:T(8,128)S(1)}, u32[]{:S(2)}, u32[]{:S(2)}) collective-permute-start(f32[8,1152]{1,0:T(8,128)S(1)} %reduce_sum.28), channel_id=1, source_target_pairs={{0,32},{32,0},{64,96},{96,64},{128,160},{160,128},{192,224},{224,1... | collective-permute-start | bytes 110600 | tf_op jit(solution)/shard_map/ppermute | solution.py:67
  53.7 7.0 %collective-permute-start.1 = (f32[8,1152]{1,0:T(8,128)S(1)}, f32[8,1152]{1,0:T(8,128)S(1)}, u32[]{:S(2)}, u32[]{:S(2)}) collective-permute-start(f32[8,1152]{1,0:T(8,128)S(1)} %add.45), channel_id=1, source_target_pairs={{0,64},{32,96},{64,0},{96,32},{128,192},{160,224},{192,128},{224,1... | collective-permute-start | bytes 110600 | tf_op jit(solution)/shard_map/ppermute | solution.py:67
  60.7 9.8 %collective-permute-start.2 = (f32[8,1152]{1,0:T(8,128)S(1)}, f32[8,1152]{1,0:T(8,128)S(1)}, u32[]{:S(2)}, u32[]{:S(2)}) collective-permute-start(f32[8,1152]{1,0:T(8,128)S(1)} %add.46), channel_id=1, source_target_pairs={{0,128},{32,160},{64,192},{96,224},{128,0},{160,32},{192,64},{224,... | collective-permute-start | bytes 110600 | tf_op jit(solution)/shard_map/ppermute | solution.py:67
  70.5 8.6 %collective-permute-start.3 = (f32[8,1152]{1,0:T(8,128)S(1)}, f32[8,1152]{1,0:T(8,128)S(1)}, u32[]{:S(2)}, u32[]{:S(2)}) collective-permute-start(f32[8,1152]{1,0:T(8,128)S(1)} %add.47), channel_id=1, source_target_pairs={{0,256},{32,288},{64,320},{96,352},{128,384},{160,416},{192,448},{... | collective-permute-start | bytes 110600 | tf_op jit(solution)/shard_map/ppermute | solution.py:67
  141.9 5.0 %collective-permute-start.4 = (f32[8,1024]{1,0:T(8,128)S(1)}, f32[8,1024]{1,0:T(8,128)S(1)}, u32[]{:S(2)}, u32[]{:S(2)}) collective-permute-start(f32[8,1024]{1,0:T(8,128)S(1)} %reduce_sum.29), channel_id=1, source_target_pairs={{0,32},{32,0},{64,96},{96,64},{128,160},{160,128},{192,224},{224,1... | collective-permute-start | bytes 98312 | tf_op jit(solution)/shard_map/ppermute | solution.py:67
  146.9 5.9 %collective-permute-start.5 = (f32[8,1024]{1,0:T(8,128)S(1)}, f32[8,1024]{1,0:T(8,128)S(1)}, u32[]{:S(2)}, u32[]{:S(2)}) collective-permute-start(f32[8,1024]{1,0:T(8,128)S(1)} %add.49), channel_id=1, source_target_pairs={{0,64},{32,96},{64,0},{96,32},{128,192},{160,224},{192,128},{224,1... | collective-permute-start | bytes 98312 | tf_op jit(solution)/shard_map/ppermute | solution.py:67
  152.8 8.8 %collective-permute-start.6 = (f32[8,1024]{1,0:T(8,128)S(1)}, f32[8,1024]{1,0:T(8,128)S(1)}, u32[]{:S(2)}, u32[]{:S(2)}) collective-permute-start(f32[8,1024]{1,0:T(8,128)S(1)} %add.50), channel_id=1, source_target_pairs={{0,128},{32,160},{64,192},{96,224},{128,0},{160,32},{192,64},{224,... | collective-permute-start | bytes 98312 | tf_op jit(solution)/shard_map/ppermute | solution.py:67
  161.6 8.6 %collective-permute-start.7 = (f32[8,1024]{1,0:T(8,128)S(1)}, f32[8,1024]{1,0:T(8,128)S(1)}, u32[]{:S(2)}, u32[]{:S(2)}) collective-permute-start(f32[8,1024]{1,0:T(8,128)S(1)} %add.51), channel_id=1, source_target_pairs={{0,256},{32,288},{64,320},{96,352},{128,384},{160,416},{192,448},{... | collective-permute-start | bytes 98312 | tf_op jit(solution)/shard_map/ppermute | solution.py:67
  170.2 25.7 %copy-start.1 = (bf16[8,1024]{1,0:T(8,128)(2,1)}, bf16[8,1024]{1,0:T(8,128)(2,1)S(1)}, u32[]{:S(2)}) copy-start(bf16[8,1024]{1,0:T(8,128)(2,1)S(1)} %divide_convert_fusion) | copy-start | bytes 49156

commit v5 on v4

--- a/solution.py
+++ b/solution.py
@@ -20,7 +20,7 @@
         return jnp.exp(-0.5 * gap * gap)
 
     kernel_pair = (line_at(row // G, col // G) * line_at(row % G, col % G)).astype(jnp.bfloat16)
-    return (kernel_line, kernel_pair)
+    return (kernel_line, lax.optimization_barrier(kernel_pair))
 
 
 def log_convolve(field_log, kernel_line, kernel_pair):
@@ -62,9 +62,20 @@
         arrived = lax.all_to_all(local_sums, "bank", 0, 0, tiled=True)
         group_sums = jnp.sum(arrived, axis=0)
         summed = group_sums
-        for level in range(blk_levels):
-            partner = [(i, i ^ (1 << level)) for i in range(blk_size)]
-            summed = summed + lax.ppermute(summed, "blk", partner)
+        level = 0
+        while level < blk_levels:
+            if level + 1 < blk_levels:
+                near, far = 1 << level, 2 << level
+                got = [
+                    lax.ppermute(summed, "blk", [(i, i ^ step) for i in range(blk_size)])
+                    for step in (near, far, near | far)
+                ]
+                summed = (summed + got[0]) + (got[1] + got[2])
+                level += 2
+            else:
+                partner = [(i, i ^ (1 << level)) for i in range(blk_size)]
+                summed = summed + lax.ppermute(summed, "blk", partner)
+                level += 1
         if counts is None:
             counts = summed[:, owned]
             summed = summed[:, :owned]

time: 198 us -> 201 us (1.015)
  starting transfers between devices: 41.9 us -> 52.7 us
  matrix products: 13.4 us -> 7.13 us
  waiting for transfers between devices: 16.4 us -> 12.7 us
  other arithmetic: 1.91 us -> 5.32 us
    ppermute x8 -> x12, starting transfers between devices: 41.9 us -> 52.7 us  [per_device(): lax.ppermute(summed, 'blk', [(i, i ^ step) for i in range(blk_size)])]
    dot_general x4, matrix products: 8.36 us -> 2.13 us  [log_convolve(): jnp.dot(raised, kernel_pair, preferred_element_type=jnp.float32)]
    ppermute x8 -> x12, waiting for transfers between devices: 16.4 us -> 12.7 us  [per_device(): lax.ppermute(summed, 'blk', [(i, i ^ step) for i in range(blk_size)])]
    all_to_all x2, blocking collectives: 49.8 us -> 47.5 us  [per_device(): center_all = lax.all_to_all(spread, 'bank', 0, 0, tiled=True)]
    convert_element_type x0 -> x1, other arithmetic: none -> 2.16 us  [kernel_tables(): (line_at(row // G, col // G) * line_at(row % G, col % G)).astype(jnp.bflo...]
  transfers between devices with their start and end apart: 8 -> 12, of which waited for: 8 -> 6; matrix products, arithmetic and copies ran while one was open for 0% -> 0% of each run, Pallas kernels for 0% -> 0%
where the time goes in v5:
time: 201 us; the launch traced here: 200 us
  blocking collectives  119 us (59%)
  starting transfers between devices  52.7 us (26%)
  waiting for transfers between devices  12.7 us (6%)
  matrix products  7.13 us (4%)
  other arithmetic  5.32 us (3%)
  local copies, waits for them, and re-layouts  2.14 us (1%)
    all_to_all x2, blocking collectives, per_device(): arrived = lax.all_to_all(local_sums, 'bank', 0, 0, tiled=True)  71.7 us
    ppermute x12, starting transfers between devices, per_device(): lax.ppermute(summed, 'blk', [(i, i ^ step) for i in range(blk_size)])  52.7 us
    all_to_all x2, blocking collectives, per_device(): center_all = lax.all_to_all(spread, 'bank', 0, 0, tiled=True)  47.5 us
    ppermute x12, waiting for transfers between devices, per_device(): lax.ppermute(summed, 'blk', [(i, i ^ step) for i in range(blk_size)])  12.7 us
  transfers between devices with their start and end apart: 12, of which 6 were waited for; matrix products, arithmetic and copies ran while one was open for 0% of the time, Pallas kernels for 0%

profile of v5, /device:TPU:1, one launch (start us, length us, event | category | flops | bytes accessed | tf_op | source)
XLA Modules:
  0.0 200.1 jit_solution(14844049229312753569)
XLA Ops:
  1.4 2.2 %fusion.2 = bf16[1024,1024]{1,0:T(8,128)(2,1)S(1)} fusion(s32[1024]{0:T(1024)S(1)} %get-tuple-element.3, s32[1024]{0:T(1024)S(1)} %get-tuple-element.4, s32[1024]{0:T(1024)S(1)} %get-tuple-element.2, s32[1024]{0:T(1024)S(1)} %get-tuple-element.5, pred[1024]{0:T(1024)(128)(4,1)S(1)} %get-tuple-element.6, pred[1024]{0:T(1024)(128)(4,1)S(1)} %get-tuple-element.7), kind=kLoop, calls=%fused_computation.4 | loop fusion | flops 16777216 | bytes 2115584 | tf_op jit(solution)/shard_map/convert_element_type | solution.py:22
  7.5 41.2 %all_to_all.20 = f32[32,8,1152]{2,1,0:T(8,128)} all-to-all(f32[32,8,1152]{2,1,0:T(8,128)S(1)} %pad_maximum_fusion), channel_id=1, replica_groups=mesh['blk'=16,'bank'=32] {'bank'}, dimensions={0} | all-to-all | bytes 2359296 | tf_op jit(solution)/shard_map/all_to_all | solution.py:62
  48.6 1.3 reduce_sum.28
  50.0 6.2 %collective-permute-start.2 = (f32[8,1152]{1,0:T(8,128)S(1)}, f32[8,1152]{1,0:T(8,128)S(1)}, u32[]{:S(2)}, u32[]{:S(2)}) collective-permute-start(f32[8,1152]{1,0:T(8,128)S(1)} %reduce_sum.28), channel_id=1, source_target_pairs={{0,96},{32,64},{64,32},{96,0},{128,224},{160,192},{192,160},{224,1... | collective-permute-start | bytes 110600 | tf_op jit(solution)/shard_map/ppermute | solution.py:70
  56.2 1.9 collective-permute-start.1
  58.1 2.2 %collective-permute-start = (f32[8,1152]{1,0:T(8,128)S(1)}, f32[8,1152]{1,0:T(8,128)S(1)}, u32[]{:S(2)}, u32[]{:S(2)}) collective-permute-start(f32[8,1152]{1,0:T(8,128)S(1)} %reduce_sum.28), channel_id=1, source_target_pairs={{0,32},{32,0},{64,96},{96,64},{128,160},{160,128},{192,224},{224,1... | collective-permute-start | bytes 110600 | tf_op jit(solution)/shard_map/ppermute | solution.py:70
  60.4 1.5 collective-permute-done.1
  61.8 1.4 collective-permute-done
  63.3 10.5 %collective-permute-start.5 = (f32[8,1152]{1,0:T(8,128)S(1)}, f32[8,1152]{1,0:T(8,128)S(1)}, u32[]{:S(2)}, u32[]{:S(2)}) collective-permute-start(f32[8,1152]{1,0:T(8,128)S(1)} %add_add_fusion.1), channel_id=1, source_target_pairs={{0,384},{32,416},{64,448},{96,480},{128,256},{160,288},{192,320},{... | collective-permute-start | bytes 110600 | tf_op jit(solution)/shard_map/ppermute | solution.py:70
  73.8 4.4 %collective-permute-start.4 = (f32[8,1152]{1,0:T(8,128)S(1)}, f32[8,1152]{1,0:T(8,128)S(1)}, u32[]{:S(2)}, u32[]{:S(2)}) collective-permute-start(f32[8,1152]{1,0:T(8,128)S(1)} %add_add_fusion.1), channel_id=1, source_target_pairs={{0,256},{32,288},{64,320},{96,352},{128,384},{160,416},{192,448},{... | collective-permute-start | bytes 110600 | tf_op jit(solution)/shard_map/ppermute | solution.py:70
  78.2 1.9 collective-permute-start.3
  80.2 2.2 %collective-permute-done.4 = f32[8,1152]{1,0:T(8,128)S(1)} collective-permute-done((f32[8,1152]{1,0:T(8,128)S(1)}, f32[8,1152]{1,0:T(8,128)S(1)}, u32[]{:S(2)}, u32[]{:S(2)}) %collective-permute-start.4) | collective-permute-done | bytes 36896 | tf_op jit(solution)/shard_map/ppermute | solution.py:70
  82.4 4.6 %collective-permute-done.3 = f32[8,1152]{1,0:T(8,128)S(1)} collective-permute-done((f32[8,1152]{1,0:T(8,128)S(1)}, f32[8,1152]{1,0:T(8,128)S(1)}, u32[]{:S(2)}, u32[]{:S(2)}) %collective-permute-start.3) | collective-permute-done | bytes 36896 | tf_op jit(solution)/shard_map/ppermute | solution.py:70
  87.3 23.2 %all_to_all.21 = bf16[32,8,1024]{2,1,0:T(8,128)(2,1)S(1)} all-to-all(bf16[32,8,1024]{2,1,0:T(8,128)(2,1)S(1)} %broadcast_in_dim.7), channel_id=1, replica_groups=mesh['blk'=16,'bank'=32] {'bank'}, dimensions={0} | all-to-all | bytes 1048576 | tf_op jit(solution)/shard_map/all_to_all | solution.py:84
  114.7 30.5 %all_to_all.22 = f32[32,8,1024]{2,1,0:T(8,128)S(1)} all-to-all(f32[32,8,1024]{2,1,0:T(8,128)S(1)} %convolution_bitcast_fusion), channel_id=1, replica_groups=mesh['blk'=16,'bank'=32] {'bank'}, dimensions={0} | all-to-all | bytes 2097152 | tf_op jit(solution)/shard_map/all_to_all | solution.py:62
  145.4 3.6 %collective-permute-start.8 = (f32[8,1024]{1,0:T(8,128)S(1)}, f32[8,1024]{1,0:T(8,128)S(1)}, u32[]{:S(2)}, u32[]{:S(2)}) collective-permute-start(f32[8,1024]{1,0:T(8,128)S(1)} %reduce_sum.29), channel_id=1, source_target_pairs={{0,96},{32,64},{64,32},{96,0},{128,224},{160,192},{192,160},{224,1... | collective-permute-start | bytes 98312 | tf_op jit(solution)/shard_map/ppermute | solution.py:70
  148.9 2.7 %collective-permute-start.7 = (f32[8,1024]{1,0:T(8,128)S(1)}, f32[8,1024]{1,0:T(8,128)S(1)}, u32[]{:S(2)}, u32[]{:S(2)}) collective-permute-start(f32[8,1024]{1,0:T(8,128)S(1)} %reduce_sum.29), channel_id=1, source_target_pairs={{0,64},{32,96},{64,0},{96,32},{128,192},{160,224},{192,128},{224,1... | collective-permute-start | bytes 98312 | tf_op jit(solution)/shard_map/ppermute | solution.py:70
  151.7 3.0 %collective-permute-start.6 = (f32[8,1024]{1,0:T(8,128)S(1)}, f32[8,1024]{1,0:T(8,128)S(1)}, u32[]{:S(2)}, u32[]{:S(2)}) collective-permute-start(f32[8,1024]{1,0:T(8,128)S(1)} %reduce_sum.29), channel_id=1, source_target_pairs={{0,32},{32,0},{64,96},{96,64},{128,160},{160,128},{192,224},{224,1... | collective-permute-start | bytes 98312 | tf_op jit(solution)/shard_map/ppermute | solution.py:70
  154.7 1.6 collective-permute-done.6
  156.3 4.0 %collective-permute-start.11 = (f32[8,1024]{1,0:T(8,128)S(1)}, f32[8,1024]{1,0:T(8,128)S(1)}, u32[]{:S(2)}, u32[]{:S(2)}) collective-permute-start(f32[8,1024]{1,0:T(8,128)S(1)} %add_add_fusion.2), channel_id=1, source_target_pairs={{0,384},{32,416},{64,448},{96,480},{128,256},{160,288},{192,320},{... | collective-permute-start | bytes 98312 | tf_op jit(solution)/shard_map/ppermute | solution.py:70
  160.3 4.4 %collective-permute-start.10 = (f32[8,1024]{1,0:T(8,128)S(1)}, f32[8,1024]{1,0:T(8,128)S(1)}, u32[]{:S(2)}, u32[]{:S(2)}) collective-permute-start(f32[8,1024]{1,0:T(8,128)S(1)} %add_add_fusion.2), channel_id=1, source_target_pairs={{0,256},{32,288},{64,320},{96,352},{128,384},{160,416},{192,448},{... | collective-permute-start | bytes 98312 | tf_op jit(solution)/shard_map/ppermute | solution.py:70
  164.8 7.8 %collective-permute-start.9 = (f32[8,1024]{1,0:T(8,128)S(1)}, f32[8,1024]{1,0:T(8,128)S(1)}, u32[]{:S(2)}, u32[]{:S(2)}) collective-permute-start(f32[8,1024]{1,0:T(8,128)S(1)} %add_add_fusion.2), channel_id=1, source_target_pairs={{0,128},{32,160},{64,192},{96,224},{128,0},{160,32},{192,64},{224,... | collective-permute-start | bytes 98312 | tf_op jit(solution)/shard_map/ppermute | solution.py:70
  172.6 1.3 collective-permute-done.9
  174.0 24.3 %all_to_all.23 = bf16[32,8,1024]{2,1,0:T(8,128)(2,1)S(1)} all-to-all(bf16[32,8,1024]{2,1,0:T(8,128)(2,1)S(1)} %broadcast_in_dim.8), channel_id=1, replica_groups=mesh['blk'=16,'bank'=32] {'bank'}, dimensions={0} | all-to-all | bytes 1048576 | tf_op jit(solution)/shard_map/all_to_all | solution.py:84
  (45 shorter events, 11.1 us)
Async XLA Ops:
  3.6 1.4 copy-start
  5.2 1.1 copy-start.2
  50.0 10.4 %collective-permute-start.2 = (f32[8,1152]{1,0:T(8,128)S(1)}, f32[8,1152]{1,0:T(8,128)S(1)}, u32[]{:S(2)}, u32[]{:S(2)}) collective-permute-start(f32[8,1152]{1,0:T(8,128)S(1)} %reduce_sum.28), channel_id=1, source_target_pairs={{0,96},{32,64},{64,32},{96,0},{128,224},{160,192},{192,160},{224,1... | collective-permute-start | bytes 110600 | tf_op jit(solution)/shard_map/ppermute | solution.py:70
  56.2 5.6 %collective-permute-start.1 = (f32[8,1152]{1,0:T(8,128)S(1)}, f32[8,1152]{1,0:T(8,128)S(1)}, u32[]{:S(2)}, u32[]{:S(2)}) collective-permute-start(f32[8,1152]{1,0:T(8,128)S(1)} %reduce_sum.28), channel_id=1, source_target_pairs={{0,64},{32,96},{64,0},{96,32},{128,192},{160,224},{192,128},{224,1... | collective-permute-start | bytes 110600 | tf_op jit(solution)/shard_map/ppermute | solution.py:70
  58.1 5.1 %collective-permute-start = (f32[8,1152]{1,0:T(8,128)S(1)}, f32[8,1152]{1,0:T(8,128)S(1)}, u32[]{:S(2)}, u32[]{:S(2)}) collective-permute-start(f32[8,1152]{1,0:T(8,128)S(1)} %reduce_sum.28), channel_id=1, source_target_pairs={{0,32},{32,0},{64,96},{96,64},{128,160},{160,128},{192,224},{224,1... | collective-permute-start | bytes 110600 | tf_op jit(solution)/shard_map/ppermute | solution.py:70
  63.3 16.9 %collective-permute-start.5 = (f32[8,1152]{1,0:T(8,128)S(1)}, f32[8,1152]{1,0:T(8,128)S(1)}, u32[]{:S(2)}, u32[]{:S(2)}) collective-permute-start(f32[8,1152]{1,0:T(8,128)S(1)} %add_add_fusion.1), channel_id=1, source_target_pairs={{0,384},{32,416},{64,448},{96,480},{128,256},{160,288},{192,320},{... | collective-permute-start | bytes 110600 | tf_op jit(solution)/shard_map/ppermute | solution.py:70
  73.8 8.6 %collective-permute-start.4 = (f32[8,1152]{1,0:T(8,128)S(1)}, f32[8,1152]{1,0:T(8,128)S(1)}, u32[]{:S(2)}, u32[]{:S(2)}) collective-permute-start(f32[8,1152]{1,0:T(8,128)S(1)} %add_add_fusion.1), channel_id=1, source_target_pairs={{0,256},{32,288},{64,320},{96,352},{128,384},{160,416},{192,448},{... | collective-permute-start | bytes 110600 | tf_op jit(solution)/shard_map/ppermute | solution.py:70
  78.2 8.8 %collective-permute-start.3 = (f32[8,1152]{1,0:T(8,128)S(1)}, f32[8,1152]{1,0:T(8,128)S(1)}, u32[]{:S(2)}, u32[]{:S(2)}) collective-permute-start(f32[8,1152]{1,0:T(8,128)S(1)} %add_add_fusion.1), channel_id=1, source_target_pairs={{0,128},{32,160},{64,192},{96,224},{128,0},{160,32},{192,64},{224,... | collective-permute-start | bytes 110600 | tf_op jit(solution)/shard_map/ppermute | solution.py:70
  145.4 9.3 %collective-permute-start.8 = (f32[8,1024]{1,0:T(8,128)S(1)}, f32[8,1024]{1,0:T(8,128)S(1)}, u32[]{:S(2)}, u32[]{:S(2)}) collective-permute-start(f32[8,1024]{1,0:T(8,128)S(1)} %reduce_sum.29), channel_id=1, source_target_pairs={{0,96},{32,64},{64,32},{96,0},{128,224},{160,192},{192,160},{224,1... | collective-permute-start | bytes 98312 | tf_op jit(solution)/shard_map/ppermute | solution.py:70
  148.9 5.7 %collective-permute-start.7 = (f32[8,1024]{1,0:T(8,128)S(1)}, f32[8,1024]{1,0:T(8,128)S(1)}, u32[]{:S(2)}, u32[]{:S(2)}) collective-permute-start(f32[8,1024]{1,0:T(8,128)S(1)} %reduce_sum.29), channel_id=1, source_target_pairs={{0,64},{32,96},{64,0},{96,32},{128,192},{160,224},{192,128},{224,1... | collective-permute-start | bytes 98312 | tf_op jit(solution)/shard_map/ppermute | solution.py:70
  151.7 4.7 %collective-permute-start.6 = (f32[8,1024]{1,0:T(8,128)S(1)}, f32[8,1024]{1,0:T(8,128)S(1)}, u32[]{:S(2)}, u32[]{:S(2)}) collective-permute-start(f32[8,1024]{1,0:T(8,128)S(1)} %reduce_sum.29), channel_id=1, source_target_pairs={{0,32},{32,0},{64,96},{96,64},{128,160},{160,128},{192,224},{224,1... | collective-permute-start | bytes 98312 | tf_op jit(solution)/shard_map/ppermute | solution.py:70
  156.3 16.2 %collective-permute-start.11 = (f32[8,1024]{1,0:T(8,128)S(1)}, f32[8,1024]{1,0:T(8,128)S(1)}, u32[]{:S(2)}, u32[]{:S(2)}) collective-permute-start(f32[8,1024]{1,0:T(8,128)S(1)} %add_add_fusion.2), channel_id=1, source_target_pairs={{0,384},{32,416},{64,448},{96,480},{128,256},{160,288},{192,320},{... | collective-permute-start | bytes 98312 | tf_op jit(solution)/shard_map/ppermute | solution.py:70
  160.3 12.2 %collective-permute-start.10 = (f32[8,1024]{1,0:T(8,128)S(1)}, f32[8,1024]{1,0:T(8,128)S(1)}, u32[]{:S(2)}, u32[]{:S(2)}) collective-permute-start(f32[8,1024]{1,0:T(8,128)S(1)} %add_add_fusion.2), channel_id=1, source_target_pairs={{0,256},{32,288},{64,320},{96,352},{128,384},{160,416},{192,448},{... | collective-permute-start | bytes 98312 | tf_op jit(solution)/shard_map/ppermute | solution.py:70
  164.8 9.0 %collective-permute-start.9 = (f32[8,1024]{1,0:T(8,128)S(1)}, f32[8,1024]{1,0:T(8,128)S(1)}, u32[]{:S(2)}, u32[]{:S(2)}) collective-permute-start(f32[8,1024]{1,0:T(8,128)S(1)} %add_add_fusion.2), channel_id=1, source_target_pairs={{0,128},{32,160},{64,192},{96,224},{128,0},{160,32},{192,64},{224,... | collective-permute-start | bytes 98312 | tf_op jit(solution)/shard_map/ppermute | solution.py:70
  173.9 25.0 %copy-start.1 = (bf16[8,1024]{1,0:T(8,128)(2,1)}, bf16[8,1024]{1,0:T(8,128)(2,1)S(1)}, u32[]{:S(2)}) copy-start(bf16[8,1024]{1,0:T(8,128)(2,1)S(1)} %divide_convert_fusion) | copy-start | bytes 49156

commit v6 on v4

--- a/solution.py
+++ b/solution.py
@@ -20,7 +20,7 @@
         return jnp.exp(-0.5 * gap * gap)
 
     kernel_pair = (line_at(row // G, col // G) * line_at(row % G, col % G)).astype(jnp.bfloat16)
-    return (kernel_line, kernel_pair)
+    return (kernel_line, lax.optimization_barrier(kernel_pair))
 
 
 def log_convolve(field_log, kernel_line, kernel_pair):
@@ -43,24 +43,30 @@
     blk_levels = blk_size.bit_length() - 1
     labels = jnp.arange(BARS, dtype=jnp.int32)
     onehot = (assignment[:, None] == labels[None, :]).astype(jnp.float32)
-    local_counts = jnp.sum(onehot, axis=0)
     selector = onehot.astype(jnp.bfloat16)
-    member_weights = jnp.transpose(onehot)
     potential = jnp.zeros((member_count, cell_count), jnp.float32)
     counts = None
-    center_all = None
+    weights_in = None
     center_owned = None
     for iteration in range(ITERS):
         source = log_density.astype(jnp.float32) - log_convolve(potential, kernel_line, kernel_pair)
         smoothed = log_convolve(source, kernel_line, kernel_pair)
-        blocks = smoothed.reshape(member_count, bank_size, owned)
-        local_sums = jnp.einsum("km,mrc->rkc", member_weights, blocks, precision=lax.Precision.HIGHEST)
+        rows = jnp.transpose(smoothed.reshape(member_count, bank_size, owned), (1, 0, 2))
+        if weights_in is None:
+            label_lanes = jnp.broadcast_to(
+                assignment.astype(jnp.float32)[None, :, None], (bank_size, member_count, 128)
+            )
+            rows = jnp.concatenate([rows, label_lanes], axis=2)
+        arrived = lax.all_to_all(rows, "bank", 0, 0, tiled=True)
+        if weights_in is None:
+            weights_in = (arrived[:, :, owned, None] == labels.astype(jnp.float32)).astype(jnp.float32)
+            arrived = arrived[:, :, :owned]
+        group_sums = jnp.einsum("smk,smc->kc", weights_in, arrived, precision=lax.Precision.HIGHEST)
         if counts is None:
-            local_sums = jnp.concatenate(
-                [local_sums, jnp.broadcast_to(local_counts[None, :, None], (bank_size, BARS, 128))], axis=2
+            group_counts = jnp.sum(weights_in, axis=(0, 1))
+            group_sums = jnp.concatenate(
+                [group_sums, jnp.broadcast_to(group_counts[:, None], (BARS, 128))], axis=1
             )
-        arrived = lax.all_to_all(local_sums, "bank", 0, 0, tiled=True)
-        group_sums = jnp.sum(arrived, axis=0)
         summed = group_sums
         for level in range(blk_levels):
             partner = [(i, i ^ (1 << level)) for i in range(blk_size)]

time: 198 us -> 170 us (0.86)
  blocking collectives: 121 us -> 68.6 us
  waiting for transfers between devices: 16.4 us -> 35.6 us
  starting transfers between devices: 41.9 us -> 50.9 us
  matrix products: 13.4 us -> 6.37 us
    all_to_all x2 -> x1, blocking collectives: 71 us -> 20.3 us  [per_device(): arrived = lax.all_to_all(rows, 'bank', 0, 0, tiled=True)]
    all_to_all x0 -> x1, waiting for transfers between devices: none -> 17.8 us  [per_device(): arrived = lax.all_to_all(rows, 'bank', 0, 0, tiled=True)]
    all_to_all x0 -> x1, starting transfers between devices: none -> 10.4 us  [per_device(): arrived = lax.all_to_all(rows, 'bank', 0, 0, tiled=True)]
    dot_general x4, matrix products: 8.36 us -> 2.13 us  [log_convolve(): jnp.dot(raised, kernel_pair, preferred_element_type=jnp.float32)]
    convert_element_type x0 -> x3, other arithmetic: none -> 2.2 us  [the longest x1 2.2 us: kernel_tables(): (line_at(row // G, col // G) * line_at(row % G, col % G)).astype(jnp.bflo...]
  transfers between devices with their start and end apart: 8 -> 9, of which waited for: 8 -> 9; matrix products, arithmetic and copies ran while one was open for 0% -> 0% of each run, Pallas kernels for 0% -> 0%
where the time goes in v6:
time: 170 us
  blocking collectives  68.6 us (40%)
  starting transfers between devices  50.9 us (30%)
  waiting for transfers between devices  35.6 us (21%)
  matrix products  6.37 us (4%)
  local copies, waits for them, and re-layouts  3.91 us (2%)
  other arithmetic  3.36 us (2%)
    all_to_all x2, blocking collectives, per_device(): center_all = lax.all_to_all(spread, 'bank', 0, 0, tiled=True)  48.3 us
    ppermute x8, starting transfers between devices, per_device(): summed = summed + lax.ppermute(summed, 'blk', partner)  40.5 us
    all_to_all x1, blocking collectives, per_device(): arrived = lax.all_to_all(rows, 'bank', 0, 0, tiled=True)  20.3 us
    all_to_all x1, waiting for transfers between devices, per_device(): arrived = lax.all_to_all(rows, 'bank', 0, 0, tiled=True)  17.8 us
    ppermute x8, waiting for transfers between devices, per_device(): summed = summed + lax.ppermute(summed, 'blk', partner)  17.8 us
    all_to_all x1, starting transfers between devices, per_device(): arrived = lax.all_to_all(rows, 'bank', 0, 0, tiled=True)  10.4 us
  transfers between devices with their start and end apart: 9, of which 9 were waited for; matrix products, arithmetic and copies ran while one was open for 0% of the time, Pallas kernels for 0%

profile of v6, /device:TPU:1, one launch (start us, length us, event | category | flops | bytes accessed | tf_op | source)
XLA Modules:
  0.0 169.7 jit_solution(6575065493206710308)
XLA Ops:
  0.7 2.2 %fusion.2 = bf16[1024,1024]{1,0:T(8,128)(2,1)S(1)} fusion(s32[1024]{0:T(1024)S(1)} %get-tuple-element.3, s32[1024]{0:T(1024)S(1)} %get-tuple-element.4, s32[1024]{0:T(1024)S(1)} %get-tuple-element.2, s32[1024]{0:T(1024)S(1)} %get-tuple-element.5, pred[1024]{0:T(1024)(128)(4,1)S(1)} %get-tuple-element.6, pred[1024]{0:T(1024)(128)(4,1)S(1)} %get-tuple-element.7), kind=kLoop, calls=%fused_computation.4 | loop fusion | flops 16777216 | bytes 2115584 | tf_op jit(solution)/shard_map/convert_element_type | solution.py:22
  5.7 1.2 copy.6
  6.9 10.4 %all-to-all-start = ((f32[32,4,1152]{2,1,0:T(4,128)}), f32[32,4,1152]{2,1,0:T(4,128)S(1)}, u32[]{:S(2)}, u32[]{:S(2)}) async-start(f32[32,4,1152]{2,1,0:T(4,128)} %copy.6), calls=%async_computation | async-start | bytes 1179648 | tf_op jit(solution)/shard_map/all_to_all | solution.py:60
  17.3 17.8 %all-to-all-done = f32[32,4,1152]{2,1,0:T(4,128)S(1)} async-done(((f32[32,4,1152]{2,1,0:T(4,128)}), f32[32,4,1152]{2,1,0:T(4,128)S(1)}, u32[]{:S(2)}, u32[]{:S(2)}) %all-to-all-start) | async-done | bytes 589856 | tf_op jit(solution)/shard_map/all_to_all | solution.py:60
  36.2 2.5 %collective-permute-start = (f32[8,1152]{1,0:T(8,128)S(1)}, f32[8,1152]{1,0:T(8,128)S(1)}, u32[]{:S(2)}, u32[]{:S(2)}) collective-permute-start(f32[8,1152]{1,0:T(8,128)S(1)} %pad_maximum_fusion.1), channel_id=1, source_target_pairs={{0,32},{32,0},{64,96},{96,64},{128,160},{160,128},{192,224},{224,1... | collective-permute-start | bytes 110600 | tf_op jit(solution)/shard_map/ppermute | solution.py:73
  38.7 2.8 %collective-permute-done = f32[8,1152]{1,0:T(8,128)S(1)} collective-permute-done((f32[8,1152]{1,0:T(8,128)S(1)}, f32[8,1152]{1,0:T(8,128)S(1)}, u32[]{:S(2)}, u32[]{:S(2)}) %collective-permute-start) | collective-permute-done | bytes 36896 | tf_op jit(solution)/shard_map/ppermute | solution.py:73
  41.5 4.6 %collective-permute-start.1 = (f32[8,1152]{1,0:T(8,128)S(1)}, f32[8,1152]{1,0:T(8,128)S(1)}, u32[]{:S(2)}, u32[]{:S(2)}) collective-permute-start(f32[8,1152]{1,0:T(8,128)S(1)} %fusion.65), channel_id=1, source_target_pairs={{0,64},{32,96},{64,0},{96,32},{128,192},{160,224},{192,128},{224,1... | collective-permute-start | bytes 110600 | tf_op jit(solution)/shard_map/ppermute | solution.py:73
  46.1 1.3 collective-permute-done.1
  47.5 8.8 %collective-permute-start.2 = (f32[8,1152]{1,0:T(8,128)S(1)}, f32[8,1152]{1,0:T(8,128)S(1)}, u32[]{:S(2)}, u32[]{:S(2)}) collective-permute-start(f32[8,1152]{1,0:T(8,128)S(1)} %add.40), channel_id=1, source_target_pairs={{0,128},{32,160},{64,192},{96,224},{128,0},{160,32},{192,64},{224,... | collective-permute-start | bytes 110600 | tf_op jit(solution)/shard_map/ppermute | solution.py:73
  56.3 1.4 collective-permute-done.2
  57.6 4.7 %collective-permute-start.3 = (f32[8,1152]{1,0:T(8,128)S(1)}, f32[8,1152]{1,0:T(8,128)S(1)}, u32[]{:S(2)}, u32[]{:S(2)}) collective-permute-start(f32[8,1152]{1,0:T(8,128)S(1)} %add.41), channel_id=1, source_target_pairs={{0,256},{32,288},{64,320},{96,352},{128,384},{160,416},{192,448},{... | collective-permute-start | bytes 110600 | tf_op jit(solution)/shard_map/ppermute | solution.py:73
  62.4 3.9 %collective-permute-done.3 = f32[8,1152]{1,0:T(8,128)S(1)} collective-permute-done((f32[8,1152]{1,0:T(8,128)S(1)}, f32[8,1152]{1,0:T(8,128)S(1)}, u32[]{:S(2)}, u32[]{:S(2)}) %collective-permute-start.3) | collective-permute-done | bytes 36896 | tf_op jit(solution)/shard_map/ppermute | solution.py:73
  66.5 24.1 %all_to_all.20 = bf16[32,8,1024]{2,1,0:T(8,128)(2,1)S(1)} all-to-all(bf16[32,8,1024]{2,1,0:T(8,128)(2,1)S(1)} %broadcast_in_dim.10), channel_id=1, replica_groups=mesh['blk'=16,'bank'=32] {'bank'}, dimensions={0} | all-to-all | bytes 1048576 | tf_op jit(solution)/shard_map/all_to_all | solution.py:79
  94.3 20.3 %all_to_all.21 = f32[32,4,1024]{2,1,0:T(4,128)S(1)} all-to-all(f32[32,4,1024]{2,1,0:T(4,128)S(1)} %copy.10), channel_id=1, replica_groups=mesh['blk'=16,'bank'=32] {'bank'}, dimensions={0} | all-to-all | bytes 1048576 | tf_op jit(solution)/shard_map/all_to_all | solution.py:60
  115.2 3.1 %collective-permute-start.4 = (f32[8,1024]{1,0:T(8,128)S(1)}, f32[8,1024]{1,0:T(8,128)S(1)}, u32[]{:S(2)}, u32[]{:S(2)}) collective-permute-start(f32[8,1024]{1,0:T(8,128)S(1)} %convolution_bitcast_fusion), channel_id=1, source_target_pairs={{0,32},{32,0},{64,96},{96,64},{128,160},{160,128},{192,224},{224,1... | collective-permute-start | bytes 98312 | tf_op jit(solution)/shard_map/ppermute | solution.py:73
  118.3 2.0 %collective-permute-done.4 = f32[8,1024]{1,0:T(8,128)S(1)} collective-permute-done((f32[8,1024]{1,0:T(8,128)S(1)}, f32[8,1024]{1,0:T(8,128)S(1)}, u32[]{:S(2)}, u32[]{:S(2)}) %collective-permute-start.4) | collective-permute-done | bytes 32800 | tf_op jit(solution)/shard_map/ppermute | solution.py:73
  120.3 4.4 %collective-permute-start.5 = (f32[8,1024]{1,0:T(8,128)S(1)}, f32[8,1024]{1,0:T(8,128)S(1)}, u32[]{:S(2)}, u32[]{:S(2)}) collective-permute-start(f32[8,1024]{1,0:T(8,128)S(1)} %add.43), channel_id=1, source_target_pairs={{0,64},{32,96},{64,0},{96,32},{128,192},{160,224},{192,128},{224,1... | collective-permute-start | bytes 98312 | tf_op jit(solution)/shard_map/ppermute | solution.py:73
  124.7 1.3 collective-permute-done.5
  126.0 7.7 %collective-permute-start.6 = (f32[8,1024]{1,0:T(8,128)S(1)}, f32[8,1024]{1,0:T(8,128)S(1)}, u32[]{:S(2)}, u32[]{:S(2)}) collective-permute-start(f32[8,1024]{1,0:T(8,128)S(1)} %add.44), channel_id=1, source_target_pairs={{0,128},{32,160},{64,192},{96,224},{128,0},{160,32},{192,64},{224,... | collective-permute-start | bytes 98312 | tf_op jit(solution)/shard_map/ppermute | solution.py:73
  133.7 1.3 collective-permute-done.6
  135.0 4.7 %collective-permute-start.7 = (f32[8,1024]{1,0:T(8,128)S(1)}, f32[8,1024]{1,0:T(8,128)S(1)}, u32[]{:S(2)}, u32[]{:S(2)}) collective-permute-start(f32[8,1024]{1,0:T(8,128)S(1)} %add.45), channel_id=1, source_target_pairs={{0,256},{32,288},{64,320},{96,352},{128,384},{160,416},{192,448},{... | collective-permute-start | bytes 98312 | tf_op jit(solution)/shard_map/ppermute | solution.py:73
  139.8 3.8 %collective-permute-done.7 = f32[8,1024]{1,0:T(8,128)S(1)} collective-permute-done((f32[8,1024]{1,0:T(8,128)S(1)}, f32[8,1024]{1,0:T(8,128)S(1)}, u32[]{:S(2)}, u32[]{:S(2)}) %collective-permute-start.7) | collective-permute-done | bytes 32800 | tf_op jit(solution)/shard_map/ppermute | solution.py:73
  143.7 24.2 %all_to_all.22 = bf16[32,8,1024]{2,1,0:T(8,128)(2,1)S(1)} all-to-all(bf16[32,8,1024]{2,1,0:T(8,128)(2,1)S(1)} %broadcast_in_dim.11), channel_id=1, replica_groups=mesh['blk'=16,'bank'=32] {'bank'}, dimensions={0} | all-to-all | bytes 1048576 | tf_op jit(solution)/shard_map/all_to_all | solution.py:79
  168.6 1.1 copy.18
  (49 shorter events, 9.1 us)
Async XLA Ops:
  2.9 1.4 copy-start
  4.5 1.1 copy-start.2
  6.9 28.2 %all-to-all-start = ((f32[32,4,1152]{2,1,0:T(4,128)}), f32[32,4,1152]{2,1,0:T(4,128)S(1)}, u32[]{:S(2)}, u32[]{:S(2)}) async-start(f32[32,4,1152]{2,1,0:T(4,128)} %copy.6), calls=%async_computation | async-start | bytes 1179648 | tf_op jit(solution)/shard_map/all_to_all | solution.py:60
  36.2 5.3 %collective-permute-start = (f32[8,1152]{1,0:T(8,128)S(1)}, f32[8,1152]{1,0:T(8,128)S(1)}, u32[]{:S(2)}, u32[]{:S(2)}) collective-permute-start(f32[8,1152]{1,0:T(8,128)S(1)} %pad_maximum_fusion.1), channel_id=1, source_target_pairs={{0,32},{32,0},{64,96},{96,64},{128,160},{160,128},{192,224},{224,1... | collective-permute-start | bytes 110600 | tf_op jit(solution)/shard_map/ppermute | solution.py:73
  41.5 5.9 %collective-permute-start.1 = (f32[8,1152]{1,0:T(8,128)S(1)}, f32[8,1152]{1,0:T(8,128)S(1)}, u32[]{:S(2)}, u32[]{:S(2)}) collective-permute-start(f32[8,1152]{1,0:T(8,128)S(1)} %fusion.65), channel_id=1, source_target_pairs={{0,64},{32,96},{64,0},{96,32},{128,192},{160,224},{192,128},{224,1... | collective-permute-start | bytes 110600 | tf_op jit(solution)/shard_map/ppermute | solution.py:73
  47.5 10.1 %collective-permute-start.2 = (f32[8,1152]{1,0:T(8,128)S(1)}, f32[8,1152]{1,0:T(8,128)S(1)}, u32[]{:S(2)}, u32[]{:S(2)}) collective-permute-start(f32[8,1152]{1,0:T(8,128)S(1)} %add.40), channel_id=1, source_target_pairs={{0,128},{32,160},{64,192},{96,224},{128,0},{160,32},{192,64},{224,... | collective-permute-start | bytes 110600 | tf_op jit(solution)/shard_map/ppermute | solution.py:73
  57.6 8.6 %collective-permute-start.3 = (f32[8,1152]{1,0:T(8,128)S(1)}, f32[8,1152]{1,0:T(8,128)S(1)}, u32[]{:S(2)}, u32[]{:S(2)}) collective-permute-start(f32[8,1152]{1,0:T(8,128)S(1)} %add.41), channel_id=1, source_target_pairs={{0,256},{32,288},{64,320},{96,352},{128,384},{160,416},{192,448},{... | collective-permute-start | bytes 110600 | tf_op jit(solution)/shard_map/ppermute | solution.py:73
  115.2 5.1 %collective-permute-start.4 = (f32[8,1024]{1,0:T(8,128)S(1)}, f32[8,1024]{1,0:T(8,128)S(1)}, u32[]{:S(2)}, u32[]{:S(2)}) collective-permute-start(f32[8,1024]{1,0:T(8,128)S(1)} %convolution_bitcast_fusion), channel_id=1, source_target_pairs={{0,32},{32,0},{64,96},{96,64},{128,160},{160,128},{192,224},{224,1... | collective-permute-start | bytes 98312 | tf_op jit(solution)/shard_map/ppermute | solution.py:73
  120.3 5.7 %collective-permute-start.5 = (f32[8,1024]{1,0:T(8,128)S(1)}, f32[8,1024]{1,0:T(8,128)S(1)}, u32[]{:S(2)}, u32[]{:S(2)}) collective-permute-start(f32[8,1024]{1,0:T(8,128)S(1)} %add.43), channel_id=1, source_target_pairs={{0,64},{32,96},{64,0},{96,32},{128,192},{160,224},{192,128},{224,1... | collective-permute-start | bytes 98312 | tf_op jit(solution)/shard_map/ppermute | solution.py:73
  126.0 9.0 %collective-permute-start.6 = (f32[8,1024]{1,0:T(8,128)S(1)}, f32[8,1024]{1,0:T(8,128)S(1)}, u32[]{:S(2)}, u32[]{:S(2)}) collective-permute-start(f32[8,1024]{1,0:T(8,128)S(1)} %add.44), channel_id=1, source_target_pairs={{0,128},{32,160},{64,192},{96,224},{128,0},{160,32},{192,64},{224,... | collective-permute-start | bytes 98312 | tf_op jit(solution)/shard_map/ppermute | solution.py:73
  135.0 8.6 %collective-permute-start.7 = (f32[8,1024]{1,0:T(8,128)S(1)}, f32[8,1024]{1,0:T(8,128)S(1)}, u32[]{:S(2)}, u32[]{:S(2)}) collective-permute-start(f32[8,1024]{1,0:T(8,128)S(1)} %add.45), channel_id=1, source_target_pairs={{0,256},{32,288},{64,320},{96,352},{128,384},{160,416},{192,448},{... | collective-permute-start | bytes 98312 | tf_op jit(solution)/shard_map/ppermute | solution.py:73
  143.6 24.9 %copy-start.1 = (bf16[8,1024]{1,0:T(8,128)(2,1)}, bf16[8,1024]{1,0:T(8,128)(2,1)S(1)}, u32[]{:S(2)}) copy-start(bf16[8,1024]{1,0:T(8,128)(2,1)S(1)} %divide_convert_fusion) | copy-start | bytes 49156

commit v7 on v6

v7 whole, which is shorter than its diff:
```python
import jax
import jax.numpy as jnp
from jax import lax
from jax.sharding import Mesh, PartitionSpec as P

G = 32
BARS = 8
ITERS = 2


def kernel_tables():
    grid_pos = jnp.arange(G, dtype=jnp.float32)
    offset = grid_pos[:, None] - grid_pos[None, :]
    kernel_line = jnp.exp(-0.5 * offset * offset)
    row = lax.broadcasted_iota(jnp.int32, (G * G, G * G), 0)
    col = lax.broadcasted_iota(jnp.int32, (G * G, G * G), 1)

    def line_at(a, b):
        gap = a.astype(jnp.float32) - b.astype(jnp.float32)
        return jnp.exp(-0.5 * gap * gap)

    kernel_pair = (line_at(row // G, col // G) * line_at(row % G, col % G)).astype(jnp.bfloat16)
    return (kernel_line, lax.optimization_barrier(kernel_pair))


def log_convolve(field_log, kernel_line, kernel_pair):
    member_count = field_log.shape[0]
    raised = jnp.exp(field_log).astype(jnp.bfloat16).reshape(member_count * G, G * G)
    inner_sum = jnp.dot(raised, kernel_pair, preferred_element_type=jnp.float32).reshape(
        member_count, G, G * G
    )
    outer_sum = jnp.einsum("ij,mjc->mic", kernel_line, inner_sum, precision=lax.Precision.HIGHEST)
    return jnp.log(outer_sum).reshape(member_count, G * G * G)


def per_device(log_density, assignment):
    kernel_line, kernel_pair = kernel_tables()
    member_count = log_density.shape[0]
    cell_count = log_density.shape[1]
    spread_axes = ("hi", "bank")
    spread_size = lax.axis_size("hi") * lax.axis_size("bank")
    z_size = lax.axis_size("z")
    chunk = cell_count // spread_size
    owned = cell_count // lax.axis_size("bank")
    labels = jnp.arange(BARS, dtype=jnp.int32)
    onehot = (assignment[:, None] == labels[None, :]).astype(jnp.float32)
    selector = onehot.astype(jnp.bfloat16)
    potential = jnp.zeros((member_count, cell_count), jnp.float32)
    counts = None
    weights_in = None
    center_all = None
    for iteration in range(ITERS):
        source = log_density.astype(jnp.float32) - log_convolve(potential, kernel_line, kernel_pair)
        smoothed = log_convolve(source, kernel_line, kernel_pair)
        rows = jnp.transpose(smoothed.reshape(member_count, spread_size, chunk), (1, 0, 2))
        if weights_in is None:
            label_lanes = jnp.broadcast_to(
                assignment.astype(jnp.float32)[None, :, None], (spread_size, member_count, 128)
            )
            rows = jnp.concatenate([rows, label_lanes], axis=2)
        arrived = lax.all_to_all(rows, spread_axes, 0, 0, tiled=True)
        if weights_in is None:
            weights_in = (arrived[:, :, chunk, None] == labels.astype(jnp.float32)).astype(jnp.float32)
            arrived = arrived[:, :, :chunk]
        group_sums = jnp.einsum("smk,smc->kc", weights_in, arrived, precision=lax.Precision.HIGHEST)
        if counts is None:
            group_counts = jnp.sum(weights_in, axis=(0, 1))
            group_sums = jnp.concatenate(
                [group_sums, jnp.broadcast_to(group_counts[:, None], (BARS, 128))], axis=1
            )
        peers = jnp.broadcast_to(group_sums[None], (z_size,) + group_sums.shape)
        summed = jnp.sum(lax.all_to_all(peers, "z", 0, 0, tiled=True), axis=0)
        if counts is None:
            counts = summed[:, chunk]
            summed = summed[:, :chunk]
        center_chunk = (summed / counts[:, None]).astype(jnp.bfloat16)
        spread = jnp.broadcast_to(center_chunk[None], (spread_size, BARS, chunk))
        center_all = lax.all_to_all(spread, spread_axes, 0, 0, tiled=True)
        chosen = jnp.einsum("mk,jkc->mjc", selector, center_all, preferred_element_type=jnp.float32)
        potential = chosen.reshape(member_count, cell_count) - smoothed
    per_owned = owned // chunk
    mine = lax.dynamic_slice_in_dim(center_all, lax.axis_index("bank") * per_owned, per_owned, axis=0)
    centers = jnp.transpose(mine, (1, 0, 2)).reshape(BARS, owned)
    return (centers, potential)


def solution(mesh):
    blk_size = mesh.shape["blk"]
    hi_size = 2 if blk_size % 2 == 0 else 1
    devices = mesh.devices.reshape(hi_size, blk_size // hi_size, mesh.shape["bank"])
    view = Mesh(devices, ("hi", "z", "bank"))
    placed = (P(("hi", "z", "bank"), None), P(("hi", "z", "bank")))
    return jax.shard_map(
        per_device,
        mesh=view,
        in_specs=placed,
        out_specs=(P(None, "bank"), P(("hi", "z", "bank"), None)),
        check_vma=False,
    )
```

time: 170 us -> 152 us (0.89)
  starting transfers between devices: 50.9 us -> 18.2 us
  blocking collectives: 68.6 us -> 76.9 us
  local copies, waits for them, and re-layouts: 3.91 us -> 7.53 us
  waiting for transfers between devices: 35.6 us -> 37.7 us
    ppermute x8 -> x0, starting transfers between devices: 40.5 us -> none  [per_device(): summed = summed + lax.ppermute(summed, 'blk', partner)]
    all_to_all x1 -> x2, waiting for transfers between devices: 17.8 us -> 37.7 us  [the longest x1 20.3 us: per_device(): arrived = lax.all_to_all(rows, spread_axes, 0, 0, tiled=True)]
    ppermute x8 -> x0, waiting for transfers between devices: 17.8 us -> none  [per_device(): summed = summed + lax.ppermute(summed, 'blk', partner)]
    all_to_all x3 -> x4, blocking collectives: 68.6 us -> 76.9 us  [the longest x2 29 us: per_device(): summed = jnp.sum(lax.all_to_all(peers, 'z', 0, 0, tiled=True), axis=0)]
    all_to_all x1 -> x2, starting transfers between devices: 10.4 us -> 18.2 us  [the longest x1 11.6 us: per_device(): arrived = lax.all_to_all(rows, spread_axes, 0, 0, tiled=True)]
  transfers between devices with their start and end apart: 9 -> 2, of which waited for: 9 -> 2; matrix products, arithmetic and copies ran while one was open for 0% -> 0% of each run, Pallas kernels for 0% -> 0%
where the time goes in v7:
time: 152 us
  blocking collectives  76.9 us (51%)
  waiting for transfers between devices  37.7 us (25%)
  starting transfers between devices  18.2 us (12%)
  local copies, waits for them, and re-layouts  7.53 us (5%)
  matrix products  5.76 us (4%)
  other arithmetic  4.9 us (3%)
    all_to_all x2, blocking collectives, per_device(): summed = jnp.sum(lax.all_to_all(peers, 'z', 0, 0, tiled=True), axis=0)  29 us
    all_to_all x1, blocking collectives, per_device(): center_all = lax.all_to_all(spread, spread_axes, 0, 0, tiled=True)  24.8 us
    all_to_all x1, blocking collectives, per_device(): arrived = lax.all_to_all(rows, spread_axes, 0, 0, tiled=True)  23.2 us
    all_to_all x1, waiting for transfers between devices, per_device(): arrived = lax.all_to_all(rows, spread_axes, 0, 0, tiled=True)  20.3 us
    all_to_all x1, waiting for transfers between devices, per_device(): center_all = lax.all_to_all(spread, spread_axes, 0, 0, tiled=True)  17.3 us
    all_to_all x1, starting transfers between devices, per_device(): arrived = lax.all_to_all(rows, spread_axes, 0, 0, tiled=True)  11.6 us
    all_to_all x1, starting transfers between devices, per_device(): center_all = lax.all_to_all(spread, spread_axes, 0, 0, tiled=True)  6.64 us
  transfers between devices with their start and end apart: 2, of which 2 were waited for; matrix products, arithmetic and copies ran while one was open for 0% of the time, Pallas kernels for 0%

profile of v7, /device:TPU:1, one launch (start us, length us, event | category | flops | bytes accessed | tf_op | source)
XLA Modules:
  0.0 151.9 jit_solution(5394849398871887622)
XLA Ops:
  0.7 2.2 %fusion.2 = bf16[1024,1024]{1,0:T(8,128)(2,1)S(1)} fusion(s32[1024]{0:T(1024)S(1)} %get-tuple-element.3, s32[1024]{0:T(1024)S(1)} %get-tuple-element.4, s32[1024]{0:T(1024)S(1)} %get-tuple-element.2, s32[1024]{0:T(1024)S(1)} %get-tuple-element.5, pred[1024]{0:T(1024)(128)(4,1)S(1)} %get-tuple-element.6, pred[1024]{0:T(1024)(128)(4,1)S(1)} %get-tuple-element.7), kind=kLoop, calls=%fused_computation.4 | loop fusion | flops 16777216 | bytes 2115584 | tf_op jit(solution)/shard_map/convert_element_type | solution.py:22
  3.3 0.6 fusion.14
  4.5 0.5 fusion.8
  5.0 0.6 fusion.13
  6.1 1.0 pad_maximum_fusion
  7.1 11.6 %all-to-all-start = ((f32[64,4,640]{2,1,0:T(4,128)}), f32[64,4,640]{2,1,0:T(4,128)S(1)}, u32[]{:S(2)}, u32[]{:S(2)}) async-start(f32[64,4,640]{2,1,0:T(4,128)} %pad_maximum_fusion), calls=%async_computation | async-start | bytes 1310720 | tf_op jit(solution)/shard_map/all_to_all | solution.py:61
  18.7 20.3 %all-to-all-done = f32[64,4,640]{2,1,0:T(4,128)S(1)} async-done(((f32[64,4,640]{2,1,0:T(4,128)}), f32[64,4,640]{2,1,0:T(4,128)S(1)}, u32[]{:S(2)}, u32[]{:S(2)}) %all-to-all-start) | async-done | bytes 655392 | tf_op jit(solution)/shard_map/all_to_all | solution.py:61
  39.1 0.7 slice.16
  39.7 1.0 copy.25
  41.5 18.3 %all_to_all.30 = f32[8,8,640]{2,1,0:T(8,128)S(1)} all-to-all(f32[8,8,640]{2,1,0:T(8,128)S(1)} %broadcast_in_dim.14), channel_id=1, replica_groups=mesh['hi'=2,'z'=8,'bank'=32] {'z'}, dimensions={0} | all-to-all | bytes 327680 | tf_op jit(solution)/shard_map/all_to_all | solution.py:72
  60.0 24.8 %all_to_all.31 = bf16[64,8,512]{2,1,0:T(8,128)(2,1)S(1)} all-to-all(bf16[64,8,512]{2,1,0:T(8,128)(2,1)S(1)} %broadcast_in_dim.15), channel_id=1, replica_groups=mesh['hi'=2,'z'=8,'bank'=32] {'hi','bank'}, dimensions={0} | all-to-all | bytes 1048576 | tf_op jit(solution)/shard_map/all_to_all | solution.py:78
  85.2 1.0 copy.27
  86.1 1.2 reshape.71
  87.3 0.5 fusion.6
  87.8 0.6 fusion.12
  88.9 0.5 fusion.4
  89.4 0.6 convolution_log_fusion
  90.5 23.2 %all_to_all.32 = f32[64,4,512]{2,1,0:T(4,128)S(1)} all-to-all(f32[64,4,512]{2,1,0:T(4,128)S(1)} %bitcast.68), channel_id=1, replica_groups=mesh['hi'=2,'z'=8,'bank'=32] {'hi','bank'}, dimensions={0} | all-to-all | bytes 1048576 | tf_op jit(solution)/shard_map/all_to_all | solution.py:61
  114.1 10.7 %all_to_all.33 = f32[8,8,512]{2,1,0:T(8,128)S(1)} all-to-all(f32[8,8,512]{2,1,0:T(8,128)S(1)} %broadcast_in_dim.16), channel_id=1, replica_groups=mesh['hi'=2,'z'=8,'bank'=32] {'z'}, dimensions={0} | all-to-all | bytes 262144 | tf_op jit(solution)/shard_map/all_to_all | solution.py:72
  124.9 0.8 broadcast_in_dim.17
  125.7 6.6 %all-to-all-start.5 = ((bf16[64,8,512]{2,1,0:T(8,128)(2,1)}), bf16[64,8,512]{2,1,0:T(8,128)(2,1)S(1)}, u32[]{:S(2)}, u32[]{:S(2)}) async-start(bf16[64,8,512]{2,1,0:T(8,128)(2,1)} %broadcast_in_dim.17), calls=%async_computation.5 | async-start | bytes 1048576 | tf_op jit(solution)/shard_map/all_to_all | solution.py:78
  132.7 17.3 %all-to-all-done.5 = bf16[64,8,512]{2,1,0:T(8,128)(2,1)S(1)} async-done(((bf16[64,8,512]{2,1,0:T(8,128)(2,1)}), bf16[64,8,512]{2,1,0:T(8,128)(2,1)S(1)}, u32[]{:S(2)}, u32[]{:S(2)}) %all-to-all-start.5) | async-done | bytes 524320 | tf_op jit(solution)/shard_map/all_to_all | solution.py:78
  150.4 0.9 sub.70
  151.3 0.6 constant_dynamic-slice_fusion
  (36 shorter events, 5.0 us)
Async XLA Ops:
  2.9 1.4 copy-start
  5.0 1.0 copy-start.1
  7.1 32.0 %all-to-all-start = ((f32[64,4,640]{2,1,0:T(4,128)}), f32[64,4,640]{2,1,0:T(4,128)S(1)}, u32[]{:S(2)}, u32[]{:S(2)}) async-start(f32[64,4,640]{2,1,0:T(4,128)} %pad_maximum_fusion), calls=%async_computation | async-start | bytes 1310720 | tf_op jit(solution)/shard_map/all_to_all | solution.py:61
  125.7 24.3 %all-to-all-start.5 = ((bf16[64,8,512]{2,1,0:T(8,128)(2,1)}), bf16[64,8,512]{2,1,0:T(8,128)(2,1)S(1)}, u32[]{:S(2)}, u32[]{:S(2)}) async-start(bf16[64,8,512]{2,1,0:T(8,128)(2,1)} %broadcast_in_dim.17), calls=%async_computation.5 | async-start | bytes 1048576 | tf_op jit(solution)/shard_map/all_to_all | solution.py:78

commit v8 on v7

--- a/solution.py
+++ b/solution.py
@@ -37,18 +37,16 @@
     kernel_line, kernel_pair = kernel_tables()
     member_count = log_density.shape[0]
     cell_count = log_density.shape[1]
-    spread_axes = ("hi", "bank")
+    spread_axes = ("bank", "hi")
     spread_size = lax.axis_size("hi") * lax.axis_size("bank")
     z_size = lax.axis_size("z")
     chunk = cell_count // spread_size
-    owned = cell_count // lax.axis_size("bank")
     labels = jnp.arange(BARS, dtype=jnp.int32)
     onehot = (assignment[:, None] == labels[None, :]).astype(jnp.float32)
-    selector = onehot.astype(jnp.bfloat16)
     potential = jnp.zeros((member_count, cell_count), jnp.float32)
     counts = None
     weights_in = None
-    center_all = None
+    center_chunk = None
     for iteration in range(ITERS):
         source = log_density.astype(jnp.float32) - log_convolve(potential, kernel_line, kernel_pair)
         smoothed = log_convolve(source, kernel_line, kernel_pair)
@@ -74,13 +72,17 @@
             counts = summed[:, chunk]
             summed = summed[:, :chunk]
         center_chunk = (summed / counts[:, None]).astype(jnp.bfloat16)
-        spread = jnp.broadcast_to(center_chunk[None], (spread_size, BARS, chunk))
-        center_all = lax.all_to_all(spread, spread_axes, 0, 0, tiled=True)
-        chosen = jnp.einsum("mk,jkc->mjc", selector, center_all, preferred_element_type=jnp.float32)
-        potential = chosen.reshape(member_count, cell_count) - smoothed
-    per_owned = owned // chunk
-    mine = lax.dynamic_slice_in_dim(center_all, lax.axis_index("bank") * per_owned, per_owned, axis=0)
-    centers = jnp.transpose(mine, (1, 0, 2)).reshape(BARS, owned)
+        wanted = jnp.einsum(
+            "smk,kc->smc", weights_in.astype(jnp.bfloat16), center_chunk, preferred_element_type=jnp.float32
+        ).astype(jnp.bfloat16)
+        returned = lax.all_to_all(wanted, spread_axes, 0, 0, tiled=True)
+        chosen = jnp.transpose(returned, (1, 0, 2)).reshape(member_count, cell_count)
+        potential = chosen.astype(jnp.float32) - smoothed
+    other = lax.ppermute(center_chunk, "hi", [(0, 1), (1, 0)])
+    first = lax.axis_index("hi") == 0
+    centers = jnp.concatenate(
+        [jnp.where(first, center_chunk, other), jnp.where(first, other, center_chunk)], axis=1
+    )
     return (centers, potential)
 
 

time: 152 us -> 143 us (0.941)
  waiting for transfers between devices: 37.7 us -> 27.9 us
  starting transfers between devices: 18.2 us -> 23.2 us
  blocking collectives: 76.9 us -> 72 us
    all_to_all x1, waiting for transfers between devices: 17.3 us -> 2.08 us  [per_device(): returned = lax.all_to_all(wanted, spread_axes, 0, 0, tiled=True)]
    ppermute x0 -> x1, starting transfers between devices: none -> 7.17 us  [per_device(): other = lax.ppermute(center_chunk, 'hi', [(0, 1), (1, 0)])]
    all_to_all x1, blocking collectives: 24.8 us -> 17.9 us  [per_device(): returned = lax.all_to_all(wanted, spread_axes, 0, 0, tiled=True)]
    ppermute x0 -> x1, waiting for transfers between devices: none -> 3.52 us  [per_device(): other = lax.ppermute(center_chunk, 'hi', [(0, 1), (1, 0)])]
    convert_element_type x0 -> x4, local copies, waits for them, and re-layouts: none -> 3.29 us  [the longest x2 2.17 us: per_device(): potential = chosen.astype(jnp.float32) - smoothed]
    all_to_all x1, starting transfers between devices: 6.64 us -> 4.45 us  [per_device(): returned = lax.all_to_all(wanted, spread_axes, 0, 0, tiled=True)]
    all_to_all x2, blocking collectives: 29 us -> 30.9 us  [per_device(): summed = jnp.sum(lax.all_to_all(peers, 'z', 0, 0, tiled=True), axis=0)]
    all_to_all x1, waiting for transfers between devices: 20.3 us -> 22.3 us  [per_device(): arrived = lax.all_to_all(rows, spread_axes, 0, 0, tiled=True)]
  transfers between devices with their start and end apart: 2 -> 3, of which waited for: 2 -> 3; matrix products, arithmetic and copies ran while one was open for 0% -> 1% of each run, Pallas kernels for 0% -> 0%
where the time goes in v8:
time: 143 us; the launch traced here: 142 us
  blocking collectives  72 us (50%)
  waiting for transfers between devices  27.9 us (20%)
  starting transfers between devices  23.2 us (16%)
  local copies, waits for them, and re-layouts  7.17 us (5%)
  matrix products  5.74 us (4%)
  other arithmetic  5.58 us (4%)
    all_to_all x2, blocking collectives, per_device(): summed = jnp.sum(lax.all_to_all(peers, 'z', 0, 0, tiled=True), axis=0)  30.9 us
    all_to_all x1, blocking collectives, per_device(): arrived = lax.all_to_all(rows, spread_axes, 0, 0, tiled=True)  23.1 us
    all_to_all x1, waiting for transfers between devices, per_device(): arrived = lax.all_to_all(rows, spread_axes, 0, 0, tiled=True)  22.3 us
    all_to_all x1, blocking collectives, per_device(): returned = lax.all_to_all(wanted, spread_axes, 0, 0, tiled=True)  17.9 us
    all_to_all x1, starting transfers between devices, per_device(): arrived = lax.all_to_all(rows, spread_axes, 0, 0, tiled=True)  11.6 us
    ppermute x1, starting transfers between devices, per_device(): other = lax.ppermute(center_chunk, 'hi', [(0, 1), (1, 0)])  7.17 us
    all_to_all x1, starting transfers between devices, per_device(): returned = lax.all_to_all(wanted, spread_axes, 0, 0, tiled=True)  4.45 us
    ppermute x1, waiting for transfers between devices, per_device(): other = lax.ppermute(center_chunk, 'hi', [(0, 1), (1, 0)])  3.52 us
  transfers between devices with their start and end apart: 3, of which 3 were waited for; matrix products, arithmetic and copies ran while one was open for 1% of the time, Pallas kernels for 0%

profile of v8, /device:TPU:1, one launch (start us, length us, event | category | flops | bytes accessed | tf_op | source)
XLA Modules:
  0.0 142.5 jit_solution(3965647935119595655)
XLA Ops:
  0.7 2.2 %fusion.2 = bf16[1024,1024]{1,0:T(8,128)(2,1)S(1)} fusion(s32[1024]{0:T(1024)S(1)} %get-tuple-element.5, s32[1024]{0:T(1024)S(1)} %get-tuple-element.6, s32[1024]{0:T(1024)S(1)} %get-tuple-element.4, s32[1024]{0:T(1024)S(1)} %get-tuple-element.7, pred[1024]{0:T(1024)(128)(4,1)S(1)} %get-tuple-element.8, pred[1024]{0:T(1024)(128)(4,1)S(1)} %get-tuple-element.9), kind=kLoop, calls=%fused_computation.4 | loop fusion | flops 16777216 | bytes 2115584 | tf_op jit(solution)/shard_map/convert_element_type | solution.py:22
  3.3 0.6 fusion.14
  4.5 0.5 fusion.8
  5.0 0.6 fusion.13
  6.1 1.0 pad_maximum_fusion
  7.1 11.6 %all-to-all-start = ((f32[64,4,640]{2,1,0:T(4,128)}), f32[64,4,640]{2,1,0:T(4,128)S(1)}, u32[]{:S(2)}, u32[]{:S(2)}) async-start(f32[64,4,640]{2,1,0:T(4,128)} %pad_maximum_fusion), calls=%async_computation | async-start | bytes 1310720 | tf_op jit(solution)/shard_map/all_to_all | solution.py:59
  18.7 22.3 %all-to-all-done = f32[64,4,640]{2,1,0:T(4,128)S(1)} async-done(((f32[64,4,640]{2,1,0:T(4,128)}), f32[64,4,640]{2,1,0:T(4,128)S(1)}, u32[]{:S(2)}, u32[]{:S(2)}) %all-to-all-start) | async-done | bytes 655392 | tf_op jit(solution)/shard_map/all_to_all | solution.py:59
  41.0 0.7 slice.16
  41.7 1.0 copy.21
  43.4 19.3 %all_to_all.30 = f32[8,8,640]{2,1,0:T(8,128)S(1)} all-to-all(f32[8,8,640]{2,1,0:T(8,128)S(1)} %broadcast_in_dim.10), channel_id=1, replica_groups=mesh['hi'=2,'z'=8,'bank'=32] {'z'}, dimensions={0} | all-to-all | bytes 327680 | tf_op jit(solution)/shard_map/all_to_all | solution.py:70
  63.4 17.9 %all_to_all.31 = bf16[64,4,512]{2,1,0:T(4,128)(2,1)S(1)} all-to-all(bf16[64,4,512]{2,1,0:T(4,128)(2,1)S(1)} %copy.23), channel_id=1, replica_groups=mesh['hi'=2,'z'=8,'bank'=32] {'bank','hi'}, dimensions={0} | all-to-all | bytes 524288 | tf_op jit(solution)/shard_map/all_to_all | solution.py:78
  81.4 1.0 copy.24
  82.3 1.2 reshape.51
  84.0 0.6 fusion.12
  85.6 0.6 convolution_log_fusion
  86.7 23.1 %all_to_all.32 = f32[64,4,512]{2,1,0:T(4,128)S(1)} all-to-all(f32[64,4,512]{2,1,0:T(4,128)S(1)} %bitcast.69), channel_id=1, replica_groups=mesh['hi'=2,'z'=8,'bank'=32] {'bank','hi'}, dimensions={0} | all-to-all | bytes 1048576 | tf_op jit(solution)/shard_map/all_to_all | solution.py:59
  110.2 11.7 %all_to_all.33 = f32[8,8,512]{2,1,0:T(8,128)S(1)} all-to-all(f32[8,8,512]{2,1,0:T(8,128)S(1)} %broadcast_in_dim.11), channel_id=1, replica_groups=mesh['hi'=2,'z'=8,'bank'=32] {'z'}, dimensions={0} | all-to-all | bytes 262144 | tf_op jit(solution)/shard_map/all_to_all | solution.py:70
  122.3 0.9 copy.27
  123.2 4.5 %all-to-all-start.5 = ((bf16[64,4,512]{2,1,0:T(4,128)(2,1)}), bf16[64,4,512]{2,1,0:T(4,128)(2,1)S(1)}, u32[]{:S(2)}, u32[]{:S(2)}) async-start(bf16[64,4,512]{2,1,0:T(4,128)(2,1)} %copy.27), calls=%async_computation.5 | async-start | bytes 524288 | tf_op jit(solution)/shard_map/all_to_all | solution.py:78
  127.7 7.2 %collective-permute-start = (bf16[8,512]{1,0:T(8,128)(2,1)S(1)}, bf16[8,512]{1,0:T(8,128)(2,1)S(1)}, u32[]{:S(2)}, u32[]{:S(2)}) collective-permute-start(bf16[8,512]{1,0:T(8,128)(2,1)S(1)} %divide_convert_fusion), channel_id=1, source_target_pairs={{0,256},{256,0},{1,257},{257,1},{2,258},{258,2},{3,259},{259,3},{4... | collective-permute-start | bytes 24584 | tf_op jit(solution)/shard_map/ppermute | solution.py:81
  135.2 3.5 %collective-permute-done = bf16[8,512]{1,0:T(8,128)(2,1)S(1)} collective-permute-done((bf16[8,512]{1,0:T(8,128)(2,1)S(1)}, bf16[8,512]{1,0:T(8,128)(2,1)S(1)}, u32[]{:S(2)}, u32[]{:S(2)}) %collective-permute-start) | collective-permute-done | bytes 8224 | tf_op jit(solution)/shard_map/ppermute | solution.py:81
  138.8 0.6 pad_maximum_fusion.2
  139.4 2.1 %all-to-all-done.5 = bf16[64,4,512]{2,1,0:T(4,128)(2,1)S(1)} async-done(((bf16[64,4,512]{2,1,0:T(4,128)(2,1)}), bf16[64,4,512]{2,1,0:T(4,128)(2,1)S(1)}, u32[]{:S(2)}, u32[]{:S(2)}) %all-to-all-start.5) | async-done | bytes 262176 | tf_op jit(solution)/shard_map/all_to_all | solution.py:78
  141.5 0.9 sub.70
  (40 shorter events, 6.2 us)
Async XLA Ops:
  2.9 1.4 copy-start
  5.0 1.0 copy-start.1
  7.1 33.9 %all-to-all-start = ((f32[64,4,640]{2,1,0:T(4,128)}), f32[64,4,640]{2,1,0:T(4,128)S(1)}, u32[]{:S(2)}, u32[]{:S(2)}) async-start(f32[64,4,640]{2,1,0:T(4,128)} %pad_maximum_fusion), calls=%async_computation | async-start | bytes 1310720 | tf_op jit(solution)/shard_map/all_to_all | solution.py:59
  123.2 18.3 %all-to-all-start.5 = ((bf16[64,4,512]{2,1,0:T(4,128)(2,1)}), bf16[64,4,512]{2,1,0:T(4,128)(2,1)S(1)}, u32[]{:S(2)}, u32[]{:S(2)}) async-start(bf16[64,4,512]{2,1,0:T(4,128)(2,1)} %copy.27), calls=%async_computation.5 | async-start | bytes 524288 | tf_op jit(solution)/shard_map/all_to_all | solution.py:78
  127.7 11.1 %collective-permute-start = (bf16[8,512]{1,0:T(8,128)(2,1)S(1)}, bf16[8,512]{1,0:T(8,128)(2,1)S(1)}, u32[]{:S(2)}, u32[]{:S(2)}) collective-permute-start(bf16[8,512]{1,0:T(8,128)(2,1)S(1)} %divide_convert_fusion), channel_id=1, source_target_pairs={{0,256},{256,0},{1,257},{257,1},{2,258},{258,2},{3,259},{259,3},{4... | collective-permute-start | bytes 24584 | tf_op jit(solution)/shard_map/ppermute | solution.py:81

commit v9 on v8

--- a/solution.py
+++ b/solution.py
@@ -48,19 +48,23 @@
     weights_in = None
     center_chunk = None
     for iteration in range(ITERS):
-        source = log_density.astype(jnp.float32) - log_convolve(potential, kernel_line, kernel_pair)
+        if iteration == 0:
+            flat = log_convolve(jnp.zeros((1, cell_count), jnp.float32), kernel_line, kernel_pair)
+            source = log_density.astype(jnp.float32) - flat
+        else:
+            source = log_density.astype(jnp.float32) - log_convolve(potential, kernel_line, kernel_pair)
         smoothed = log_convolve(source, kernel_line, kernel_pair)
-        rows = jnp.transpose(smoothed.reshape(member_count, spread_size, chunk), (1, 0, 2))
+        rows = smoothed.reshape(member_count, spread_size, chunk)
         if weights_in is None:
             label_lanes = jnp.broadcast_to(
-                assignment.astype(jnp.float32)[None, :, None], (spread_size, member_count, 128)
+                assignment.astype(jnp.float32)[:, None, None], (member_count, spread_size, 128)
             )
             rows = jnp.concatenate([rows, label_lanes], axis=2)
-        arrived = lax.all_to_all(rows, spread_axes, 0, 0, tiled=True)
+        arrived = lax.all_to_all(rows, spread_axes, 1, 1, tiled=True)
         if weights_in is None:
             weights_in = (arrived[:, :, chunk, None] == labels.astype(jnp.float32)).astype(jnp.float32)
             arrived = arrived[:, :, :chunk]
-        group_sums = jnp.einsum("smk,smc->kc", weights_in, arrived, precision=lax.Precision.HIGHEST)
+        group_sums = jnp.einsum("msk,msc->kc", weights_in, arrived, precision=lax.Precision.HIGHEST)
         if counts is None:
             group_counts = jnp.sum(weights_in, axis=(0, 1))
             group_sums = jnp.concatenate(
@@ -73,10 +77,10 @@
             summed = summed[:, :chunk]
         center_chunk = (summed / counts[:, None]).astype(jnp.bfloat16)
         wanted = jnp.einsum(
-            "smk,kc->smc", weights_in.astype(jnp.bfloat16), center_chunk, preferred_element_type=jnp.float32
+            "msk,kc->msc", weights_in.astype(jnp.bfloat16), center_chunk, preferred_element_type=jnp.float32
         ).astype(jnp.bfloat16)
-        returned = lax.all_to_all(wanted, spread_axes, 0, 0, tiled=True)
-        chosen = jnp.transpose(returned, (1, 0, 2)).reshape(member_count, cell_count)
+        returned = lax.all_to_all(wanted, spread_axes, 1, 1, tiled=True)
+        chosen = returned.reshape(member_count, cell_count)
         potential = chosen.astype(jnp.float32) - smoothed
     other = lax.ppermute(center_chunk, "hi", [(0, 1), (1, 0)])
     first = lax.axis_index("hi") == 0

time: 143 us -> 142 us (level)
  no operation moved by 1% of the time
where the time goes in v9:
time: 142 us
  blocking collectives  71.9 us (51%)
  waiting for transfers between devices  27.9 us (20%)
  starting transfers between devices  23.2 us (16%)
  other arithmetic  6.37 us (4%)
  local copies, waits for them, and re-layouts  6.05 us (4%)
  matrix products  5.45 us (4%)
    all_to_all x2, blocking collectives, per_device(): summed = jnp.sum(lax.all_to_all(peers, 'z', 0, 0, tiled=True), axis=0)  30.9 us
    all_to_all x1, blocking collectives, per_device(): arrived = lax.all_to_all(rows, spread_axes, 1, 1, tiled=True)  23.1 us
    all_to_all x1, waiting for transfers between devices, per_device(): arrived = lax.all_to_all(rows, spread_axes, 1, 1, tiled=True)  22.3 us
    all_to_all x1, blocking collectives, per_device(): returned = lax.all_to_all(wanted, spread_axes, 1, 1, tiled=True)  17.9 us
    all_to_all x1, starting transfers between devices, per_device(): arrived = lax.all_to_all(rows, spread_axes, 1, 1, tiled=True)  11.6 us
    ppermute x1, starting transfers between devices, per_device(): other = lax.ppermute(center_chunk, 'hi', [(0, 1), (1, 0)])  7.17 us
    all_to_all x1, starting transfers between devices, per_device(): returned = lax.all_to_all(wanted, spread_axes, 1, 1, tiled=True)  4.46 us
    ppermute x1, waiting for transfers between devices, per_device(): other = lax.ppermute(center_chunk, 'hi', [(0, 1), (1, 0)])  3.52 us
  transfers between devices with their start and end apart: 3, of which 3 were waited for; matrix products, arithmetic and copies ran while one was open for 1% of the time, Pallas kernels for 0%

profile of v9, /device:TPU:1, one launch (start us, length us, event | category | flops | bytes accessed | tf_op | source)
XLA Modules:
  0.0 141.8 jit_solution(1028339036539996505)
XLA Ops:
  0.7 2.2 %fusion.2 = bf16[1024,1024]{1,0:T(8,128)(2,1)S(1)} fusion(s32[1024]{0:T(1024)S(1)} %get-tuple-element.5, s32[1024]{0:T(1024)S(1)} %get-tuple-element.6, s32[1024]{0:T(1024)S(1)} %get-tuple-element.4, s32[1024]{0:T(1024)S(1)} %get-tuple-element.7, pred[1024]{0:T(1024)(128)(4,1)S(1)} %get-tuple-element.8, pred[1024]{0:T(1024)(128)(4,1)S(1)} %get-tuple-element.9), kind=kLoop, calls=%fused_computation.4 | loop fusion | flops 16777216 | bytes 2115584 | tf_op jit(solution)/shard_map/convert_element_type | solution.py:22
  4.0 0.5 fusion.8
  4.5 0.6 fusion.11
  5.7 1.0 pad_maximum_fusion
  6.6 11.6 %all-to-all-start = ((f32[4,64,640]{2,0,1:T(4,128)}), f32[4,64,640]{2,0,1:T(4,128)S(1)}, u32[]{:S(2)}, u32[]{:S(2)}) async-start(f32[4,64,640]{2,0,1:T(4,128)} %pad_maximum_fusion), calls=%async_computation | async-start | bytes 1310720 | tf_op jit(solution)/shard_map/all_to_all | solution.py:63
  18.3 22.3 %all-to-all-done = f32[4,64,640]{2,0,1:T(4,128)S(1)} async-done(((f32[4,64,640]{2,0,1:T(4,128)}), f32[4,64,640]{2,0,1:T(4,128)S(1)}, u32[]{:S(2)}, u32[]{:S(2)}) %all-to-all-start) | async-done | bytes 655392 | tf_op jit(solution)/shard_map/all_to_all | solution.py:63
  40.5 0.7 slice.16
  41.2 1.0 copy.29
  43.0 19.3 %all_to_all.30 = f32[8,8,640]{2,1,0:T(8,128)S(1)} all-to-all(f32[8,8,640]{2,1,0:T(8,128)S(1)} %broadcast_in_dim.10), channel_id=1, replica_groups=mesh['hi'=2,'z'=8,'bank'=32] {'z'}, dimensions={0} | all-to-all | bytes 327680 | tf_op jit(solution)/shard_map/all_to_all | solution.py:74
  62.9 17.9 %all_to_all.31 = bf16[4,64,512]{2,0,1:T(4,128)(2,1)S(1)} all-to-all(bf16[4,64,512]{2,0,1:T(4,128)(2,1)S(1)} %copy.31), channel_id=1, replica_groups=mesh['hi'=2,'z'=8,'bank'=32] {'bank','hi'}, dimensions={1} | all-to-all | bytes 524288 | tf_op jit(solution)/shard_map/all_to_all | solution.py:82
  80.9 0.9 copy_convert_fusion
  81.7 1.2 reshape.52
  83.4 0.6 fusion.10
  84.6 0.5 fusion.4
  85.1 0.6 convolution_log_fusion
  86.1 23.1 %all_to_all.32 = f32[4,64,512]{2,0,1:T(4,128)S(1)} all-to-all(f32[4,64,512]{2,0,1:T(4,128)S(1)} %copy.33), channel_id=1, replica_groups=mesh['hi'=2,'z'=8,'bank'=32] {'bank','hi'}, dimensions={1} | all-to-all | bytes 1048576 | tf_op jit(solution)/shard_map/all_to_all | solution.py:63
  109.6 11.7 %all_to_all.33 = f32[8,8,512]{2,1,0:T(8,128)S(1)} all-to-all(f32[8,8,512]{2,1,0:T(8,128)S(1)} %broadcast_in_dim.11), channel_id=1, replica_groups=mesh['hi'=2,'z'=8,'bank'=32] {'z'}, dimensions={0} | all-to-all | bytes 262144 | tf_op jit(solution)/shard_map/all_to_all | solution.py:74
  121.7 0.9 copy.35
  122.6 4.5 %all-to-all-start.5 = ((bf16[4,64,512]{2,0,1:T(4,128)(2,1)}), bf16[4,64,512]{2,0,1:T(4,128)(2,1)S(1)}, u32[]{:S(2)}, u32[]{:S(2)}) async-start(bf16[4,64,512]{2,0,1:T(4,128)(2,1)} %copy.35), calls=%async_computation.5 | async-start | bytes 524288 | tf_op jit(solution)/shard_map/all_to_all | solution.py:82
  127.1 7.2 %collective-permute-start = (bf16[8,512]{1,0:T(8,128)(2,1)S(1)}, bf16[8,512]{1,0:T(8,128)(2,1)S(1)}, u32[]{:S(2)}, u32[]{:S(2)}) collective-permute-start(bf16[8,512]{1,0:T(8,128)(2,1)S(1)} %divide_convert_fusion), channel_id=1, source_target_pairs={{0,256},{256,0},{1,257},{257,1},{2,258},{258,2},{3,259},{259,3},{4... | collective-permute-start | bytes 24584 | tf_op jit(solution)/shard_map/ppermute | solution.py:85
  134.6 3.5 %collective-permute-done = bf16[8,512]{1,0:T(8,128)(2,1)S(1)} collective-permute-done((bf16[8,512]{1,0:T(8,128)(2,1)S(1)}, bf16[8,512]{1,0:T(8,128)(2,1)S(1)}, u32[]{:S(2)}, u32[]{:S(2)}) %collective-permute-start) | collective-permute-done | bytes 8224 | tf_op jit(solution)/shard_map/ppermute | solution.py:85
  138.2 0.6 pad_maximum_fusion.2
  138.8 2.1 %all-to-all-done.5 = bf16[4,64,512]{2,0,1:T(4,128)(2,1)S(1)} async-done(((bf16[4,64,512]{2,0,1:T(4,128)(2,1)}), bf16[4,64,512]{2,0,1:T(4,128)(2,1)S(1)}, u32[]{:S(2)}, u32[]{:S(2)}) %all-to-all-start.5) | async-done | bytes 262176 | tf_op jit(solution)/shard_map/all_to_all | solution.py:82
  140.9 0.9 convert_subtract_fusion.2
  (38 shorter events, 5.8 us)
Async XLA Ops:
  2.9 1.0 copy-start
  4.5 1.0 copy-start.1
  6.6 33.9 %all-to-all-start = ((f32[4,64,640]{2,0,1:T(4,128)}), f32[4,64,640]{2,0,1:T(4,128)S(1)}, u32[]{:S(2)}, u32[]{:S(2)}) async-start(f32[4,64,640]{2,0,1:T(4,128)} %pad_maximum_fusion), calls=%async_computation | async-start | bytes 1310720 | tf_op jit(solution)/shard_map/all_to_all | solution.py:63
  122.6 18.3 %all-to-all-start.5 = ((bf16[4,64,512]{2,0,1:T(4,128)(2,1)}), bf16[4,64,512]{2,0,1:T(4,128)(2,1)S(1)}, u32[]{:S(2)}, u32[]{:S(2)}) async-start(bf16[4,64,512]{2,0,1:T(4,128)(2,1)} %copy.35), calls=%async_computation.5 | async-start | bytes 524288 | tf_op jit(solution)/shard_map/all_to_all | solution.py:82
  127.1 11.1 %collective-permute-start = (bf16[8,512]{1,0:T(8,128)(2,1)S(1)}, bf16[8,512]{1,0:T(8,128)(2,1)S(1)}, u32[]{:S(2)}, u32[]{:S(2)}) collective-permute-start(bf16[8,512]{1,0:T(8,128)(2,1)S(1)} %divide_convert_fusion), channel_id=1, source_target_pairs={{0,256},{256,0},{1,257},{257,1},{2,258},{258,2},{3,259},{259,3},{4... | collective-permute-start | bytes 24584 | tf_op jit(solution)/shard_map/ppermute | solution.py:85

commit v10 on v9

--- a/solution.py
+++ b/solution.py
@@ -62,7 +62,8 @@
             rows = jnp.concatenate([rows, label_lanes], axis=2)
         arrived = lax.all_to_all(rows, spread_axes, 1, 1, tiled=True)
         if weights_in is None:
-            weights_in = (arrived[:, :, chunk, None] == labels.astype(jnp.float32)).astype(jnp.float32)
+            label_in = jnp.max(arrived[:, :, chunk:], axis=2)
+            weights_in = (label_in[:, :, None] == labels.astype(jnp.float32)).astype(jnp.float32)
             arrived = arrived[:, :, :chunk]
         group_sums = jnp.einsum("msk,msc->kc", weights_in, arrived, precision=lax.Precision.HIGHEST)
         if counts is None:

time: 142 us -> 142 us (level)
    slice x2 -> x0, local copies, waits for them, and re-layouts: 1.67 us -> none  [per_device(): arrived[:, :, chunk, None] == labels.astype(jnp.float32)]
where the time goes in v10:
time: 142 us
  blocking collectives  72 us (51%)
  waiting for transfers between devices  27.9 us (20%)
  starting transfers between devices  23.2 us (16%)
  other arithmetic  7.12 us (5%)
  matrix products  5.45 us (4%)
  local copies, waits for them, and re-layouts  5.22 us (4%)
    all_to_all x2, blocking collectives, per_device(): summed = jnp.sum(lax.all_to_all(peers, 'z', 0, 0, tiled=True), axis=0)  30.9 us
    all_to_all x1, blocking collectives, per_device(): arrived = lax.all_to_all(rows, spread_axes, 1, 1, tiled=True)  23.1 us
    all_to_all x1, waiting for transfers between devices, per_device(): arrived = lax.all_to_all(rows, spread_axes, 1, 1, tiled=True)  22.3 us
    all_to_all x1, blocking collectives, per_device(): returned = lax.all_to_all(wanted, spread_axes, 1, 1, tiled=True)  17.9 us
    all_to_all x1, starting transfers between devices, per_device(): arrived = lax.all_to_all(rows, spread_axes, 1, 1, tiled=True)  11.6 us
    ppermute x1, starting transfers between devices, per_device(): other = lax.ppermute(center_chunk, 'hi', [(0, 1), (1, 0)])  7.17 us
    all_to_all x1, starting transfers between devices, per_device(): returned = lax.all_to_all(wanted, spread_axes, 1, 1, tiled=True)  4.45 us
    ppermute x1, waiting for transfers between devices, per_device(): other = lax.ppermute(center_chunk, 'hi', [(0, 1), (1, 0)])  3.52 us
  transfers between devices with their start and end apart: 3, of which 3 were waited for; matrix products, arithmetic and copies ran while one was open for 1% of the time, Pallas kernels for 0%

profile of v10, /device:TPU:1, one launch (start us, length us, event | category | flops | bytes accessed | tf_op | source)
XLA Modules:
  0.0 141.7 jit_solution(17182260905473293885)
XLA Ops:
  0.7 2.2 %fusion.2 = bf16[1024,1024]{1,0:T(8,128)(2,1)S(1)} fusion(s32[1024]{0:T(1024)S(1)} %get-tuple-element.5, s32[1024]{0:T(1024)S(1)} %get-tuple-element.6, s32[1024]{0:T(1024)S(1)} %get-tuple-element.4, s32[1024]{0:T(1024)S(1)} %get-tuple-element.7, pred[1024]{0:T(1024)(128)(4,1)S(1)} %get-tuple-element.8, pred[1024]{0:T(1024)(128)(4,1)S(1)} %get-tuple-element.9), kind=kLoop, calls=%fused_computation.4 | loop fusion | flops 16777216 | bytes 2115584 | tf_op jit(solution)/shard_map/convert_element_type | solution.py:22
  4.0 0.5 fusion.8
  4.5 0.6 fusion.11
  5.7 1.0 pad_maximum_fusion
  6.6 11.6 %all-to-all-start = ((f32[4,64,640]{2,0,1:T(4,128)}), f32[4,64,640]{2,0,1:T(4,128)S(1)}, u32[]{:S(2)}, u32[]{:S(2)}) async-start(f32[4,64,640]{2,0,1:T(4,128)} %pad_maximum_fusion), calls=%async_computation | async-start | bytes 1310720 | tf_op jit(solution)/shard_map/all_to_all | solution.py:63
  18.3 22.3 %all-to-all-done = f32[4,64,640]{2,0,1:T(4,128)S(1)} async-done(((f32[4,64,640]{2,0,1:T(4,128)}), f32[4,64,640]{2,0,1:T(4,128)S(1)}, u32[]{:S(2)}, u32[]{:S(2)}) %all-to-all-start) | async-done | bytes 655392 | tf_op jit(solution)/shard_map/all_to_all | solution.py:63
  40.5 0.8 slice_reduce_fusion
  41.3 0.8 copy.36
  42.9 19.3 %all_to_all.30 = f32[8,8,640]{2,1,0:T(8,128)S(1)} all-to-all(f32[8,8,640]{2,1,0:T(8,128)S(1)} %broadcast_in_dim.10), channel_id=1, replica_groups=mesh['hi'=2,'z'=8,'bank'=32] {'z'}, dimensions={0} | all-to-all | bytes 327680 | tf_op jit(solution)/shard_map/all_to_all | solution.py:75
  62.8 17.9 %all_to_all.31 = bf16[4,64,512]{2,0,1:T(4,128)(2,1)S(1)} all-to-all(bf16[4,64,512]{2,0,1:T(4,128)(2,1)S(1)} %copy.38), channel_id=1, replica_groups=mesh['hi'=2,'z'=8,'bank'=32] {'bank','hi'}, dimensions={1} | all-to-all | bytes 524288 | tf_op jit(solution)/shard_map/all_to_all | solution.py:83
  80.8 0.9 copy_convert_fusion
  81.6 1.2 reshape.53
  83.3 0.6 fusion.10
  84.5 0.5 fusion.4
  85.0 0.6 convolution_log_fusion
  86.0 23.1 %all_to_all.32 = f32[4,64,512]{2,0,1:T(4,128)S(1)} all-to-all(f32[4,64,512]{2,0,1:T(4,128)S(1)} %copy.40), channel_id=1, replica_groups=mesh['hi'=2,'z'=8,'bank'=32] {'bank','hi'}, dimensions={1} | all-to-all | bytes 1048576 | tf_op jit(solution)/shard_map/all_to_all | solution.py:63
  109.5 11.7 %all_to_all.33 = f32[8,8,512]{2,1,0:T(8,128)S(1)} all-to-all(f32[8,8,512]{2,1,0:T(8,128)S(1)} %broadcast_in_dim.11), channel_id=1, replica_groups=mesh['hi'=2,'z'=8,'bank'=32] {'z'}, dimensions={0} | all-to-all | bytes 262144 | tf_op jit(solution)/shard_map/all_to_all | solution.py:75
  121.6 0.9 copy.42
  122.5 4.5 %all-to-all-start.5 = ((bf16[4,64,512]{2,0,1:T(4,128)(2,1)}), bf16[4,64,512]{2,0,1:T(4,128)(2,1)S(1)}, u32[]{:S(2)}, u32[]{:S(2)}) async-start(bf16[4,64,512]{2,0,1:T(4,128)(2,1)} %copy.42), calls=%async_computation.5 | async-start | bytes 524288 | tf_op jit(solution)/shard_map/all_to_all | solution.py:83
  127.0 7.2 %collective-permute-start = (bf16[8,512]{1,0:T(8,128)(2,1)S(1)}, bf16[8,512]{1,0:T(8,128)(2,1)S(1)}, u32[]{:S(2)}, u32[]{:S(2)}) collective-permute-start(bf16[8,512]{1,0:T(8,128)(2,1)S(1)} %divide_convert_fusion), channel_id=1, source_target_pairs={{0,256},{256,0},{1,257},{257,1},{2,258},{258,2},{3,259},{259,3},{4... | collective-permute-start | bytes 24584 | tf_op jit(solution)/shard_map/ppermute | solution.py:86
  134.5 3.5 %collective-permute-done = bf16[8,512]{1,0:T(8,128)(2,1)S(1)} collective-permute-done((bf16[8,512]{1,0:T(8,128)(2,1)S(1)}, bf16[8,512]{1,0:T(8,128)(2,1)S(1)}, u32[]{:S(2)}, u32[]{:S(2)}) %collective-permute-start) | collective-permute-done | bytes 8224 | tf_op jit(solution)/shard_map/ppermute | solution.py:86
  138.1 0.6 pad_maximum_fusion.2
  138.7 2.1 %all-to-all-done.5 = bf16[4,64,512]{2,0,1:T(4,128)(2,1)S(1)} async-done(((bf16[4,64,512]{2,0,1:T(4,128)(2,1)}), bf16[4,64,512]{2,0,1:T(4,128)(2,1)S(1)}, u32[]{:S(2)}, u32[]{:S(2)}) %all-to-all-start.5) | async-done | bytes 262176 | tf_op jit(solution)/shard_map/all_to_all | solution.py:83
  140.8 0.9 convert_subtract_fusion.2
  (38 shorter events, 5.8 us)
Async XLA Ops:
  2.9 1.0 copy-start
  4.5 1.0 copy-start.1
  6.6 33.9 %all-to-all-start = ((f32[4,64,640]{2,0,1:T(4,128)}), f32[4,64,640]{2,0,1:T(4,128)S(1)}, u32[]{:S(2)}, u32[]{:S(2)}) async-start(f32[4,64,640]{2,0,1:T(4,128)} %pad_maximum_fusion), calls=%async_computation | async-start | bytes 1310720 | tf_op jit(solution)/shard_map/all_to_all | solution.py:63
  122.5 18.3 %all-to-all-start.5 = ((bf16[4,64,512]{2,0,1:T(4,128)(2,1)}), bf16[4,64,512]{2,0,1:T(4,128)(2,1)S(1)}, u32[]{:S(2)}, u32[]{:S(2)}) async-start(bf16[4,64,512]{2,0,1:T(4,128)(2,1)} %copy.42), calls=%async_computation.5 | async-start | bytes 524288 | tf_op jit(solution)/shard_map/all_to_all | solution.py:83
  127.0 11.1 %collective-permute-start = (bf16[8,512]{1,0:T(8,128)(2,1)S(1)}, bf16[8,512]{1,0:T(8,128)(2,1)S(1)}, u32[]{:S(2)}, u32[]{:S(2)}) collective-permute-start(bf16[8,512]{1,0:T(8,128)(2,1)S(1)} %divide_convert_fusion), channel_id=1, source_target_pairs={{0,256},{256,0},{1,257},{257,1},{2,258},{258,2},{3,259},{259,3},{4... | collective-permute-start | bytes 24584 | tf_op jit(solution)/shard_map/ppermute | solution.py:86

commit v11 on v9

--- a/solution.py
+++ b/solution.py
@@ -1,4 +1,6 @@
 import jax
+import ml_dtypes
+import numpy as np
 import jax.numpy as jnp
 from jax import lax
 from jax.sharding import Mesh, PartitionSpec as P
@@ -12,15 +14,12 @@
     grid_pos = jnp.arange(G, dtype=jnp.float32)
     offset = grid_pos[:, None] - grid_pos[None, :]
     kernel_line = jnp.exp(-0.5 * offset * offset)
-    row = lax.broadcasted_iota(jnp.int32, (G * G, G * G), 0)
-    col = lax.broadcasted_iota(jnp.int32, (G * G, G * G), 1)
-
-    def line_at(a, b):
-        gap = a.astype(jnp.float32) - b.astype(jnp.float32)
-        return jnp.exp(-0.5 * gap * gap)
-
-    kernel_pair = (line_at(row // G, col // G) * line_at(row % G, col % G)).astype(jnp.bfloat16)
-    return (kernel_line, lax.optimization_barrier(kernel_pair))
+    line_np = np.arange(G, dtype=np.float32)
+    gap = line_np[:, None] - line_np[None, :]
+    line_np = np.exp(np.float32(-0.5) * gap * gap).astype(np.float32)
+    pair_np = (line_np[:, None, :, None] * line_np[None, :, None, :]).reshape(G * G, G * G)
+    kernel_pair = jnp.asarray(pair_np.astype(ml_dtypes.bfloat16))
+    return (kernel_line, kernel_pair)
 
 
 def log_convolve(field_log, kernel_line, kernel_pair):

time: 142 us -> 142 us (level)
  matrix products: 5.45 us -> 7.48 us
  local copies, waits for them, and re-layouts: 6.05 us -> 4.36 us
    convert_element_type x1 -> x0, other arithmetic: 2.2 us -> none  [kernel_tables(): (line_at(row // G, col // G) * line_at(row % G, col % G)).astype(jnp.bflo...]
    slice x2, local copies, waits for them, and re-layouts: 1.67 us -> 0.12 us  [per_device(): arrived[:, :, chunk, None] == labels.astype(jnp.float32)]
    dot_general x4 -> x3, matrix products: 1.9 us -> 3.03 us  [log_convolve(): jnp.dot(raised, kernel_pair, preferred_element_type=jnp.float32)]
where the time goes in v11:
time: 142 us; the launch traced here: 141 us
  blocking collectives  72.1 us (51%)
  waiting for transfers between devices  27.9 us (20%)
  starting transfers between devices  23.2 us (16%)
  matrix products  7.48 us (5%)
  other arithmetic  5.11 us (4%)
  local copies, waits for them, and re-layouts  4.36 us (3%)
    all_to_all x2, blocking collectives, per_device(): summed = jnp.sum(lax.all_to_all(peers, 'z', 0, 0, tiled=True), axis=0)  31.1 us
    all_to_all x1, blocking collectives, per_device(): arrived = lax.all_to_all(rows, spread_axes, 1, 1, tiled=True)  23.1 us
    all_to_all x1, waiting for transfers between devices, per_device(): arrived = lax.all_to_all(rows, spread_axes, 1, 1, tiled=True)  22.3 us
    all_to_all x1, blocking collectives, per_device(): returned = lax.all_to_all(wanted, spread_axes, 1, 1, tiled=True)  17.9 us
    all_to_all x1, starting transfers between devices, per_device(): arrived = lax.all_to_all(rows, spread_axes, 1, 1, tiled=True)  11.6 us
    ppermute x1, starting transfers between devices, per_device(): other = lax.ppermute(center_chunk, 'hi', [(0, 1), (1, 0)])  7.17 us
    all_to_all x1, starting transfers between devices, per_device(): returned = lax.all_to_all(wanted, spread_axes, 1, 1, tiled=True)  4.45 us
    ppermute x1, waiting for transfers between devices, per_device(): other = lax.ppermute(center_chunk, 'hi', [(0, 1), (1, 0)])  3.52 us
  transfers between devices with their start and end apart: 3, of which 3 were waited for; matrix products, arithmetic and copies ran while one was open for 1% of the time, Pallas kernels for 0%

profile of v11, /device:TPU:1, one launch (start us, length us, event | category | flops | bytes accessed | tf_op | source)
XLA Modules:
  0.0 141.0 jit_solution(2539507054539411592)
XLA Ops:
  0.6 1.2 fusion.2
  1.8 1.1 fusion.4
  3.0 2.1 %fusion.9 = f32[4,32,1024]{2,1,0:T(8,128)S(1)} fusion(bf16[1024,1024,1]{1,0,2:T(8,128)(2,1)} %constant.20, bf16[1,4,32,1024]{3,1,2,0:T(4,128)(2,1)S(1)} %bitcast.56), kind=kOutput, calls=%fused_computation.25 | convolution fusion | flops 268435456 | bytes 2883584 | tf_op jit(solution)/shard_map/dot_general | solution.py:28
  5.1 0.6 fusion.1
  6.2 1.0 pad_maximum_fusion
  7.2 11.6 %all-to-all-start = ((f32[4,64,640]{2,0,1:T(4,128)}), f32[4,64,640]{2,0,1:T(4,128)S(1)}, u32[]{:S(2)}, u32[]{:S(2)}) async-start(f32[4,64,640]{2,0,1:T(4,128)} %pad_maximum_fusion), calls=%async_computation | async-start | bytes 1310720 | tf_op jit(solution)/shard_map/all_to_all | solution.py:62
  18.8 22.3 %all-to-all-done = f32[4,64,640]{2,0,1:T(4,128)S(1)} async-done(((f32[4,64,640]{2,0,1:T(4,128)}), f32[4,64,640]{2,0,1:T(4,128)S(1)}, u32[]{:S(2)}, u32[]{:S(2)}) %all-to-all-start) | async-done | bytes 655392 | tf_op jit(solution)/shard_map/all_to_all | solution.py:62
  42.0 19.4 %all_to_all.30 = f32[8,8,640]{2,1,0:T(8,128)S(1)} all-to-all(f32[8,8,640]{2,1,0:T(8,128)S(1)} %broadcast_in_dim.10), channel_id=1, replica_groups=mesh['hi'=2,'z'=8,'bank'=32] {'z'}, dimensions={0} | all-to-all | bytes 327680 | tf_op jit(solution)/shard_map/all_to_all | solution.py:73
  62.1 17.9 %all_to_all.31 = bf16[4,64,512]{2,0,1:T(4,128)(2,1)S(1)} all-to-all(bf16[4,64,512]{2,0,1:T(4,128)(2,1)S(1)} %copy.32), channel_id=1, replica_groups=mesh['hi'=2,'z'=8,'bank'=32] {'bank','hi'}, dimensions={1} | all-to-all | bytes 524288 | tf_op jit(solution)/shard_map/all_to_all | solution.py:81
  80.0 0.9 copy_convert_fusion
  80.9 1.2 reshape.52
  82.1 0.5 fusion.11
  82.6 0.6 fusion
  83.8 0.5 fusion.10
  84.3 0.6 convolution_log_fusion
  85.3 23.1 %all_to_all.32 = f32[4,64,512]{2,0,1:T(4,128)S(1)} all-to-all(f32[4,64,512]{2,0,1:T(4,128)S(1)} %copy.34), channel_id=1, replica_groups=mesh['hi'=2,'z'=8,'bank'=32] {'bank','hi'}, dimensions={1} | all-to-all | bytes 1048576 | tf_op jit(solution)/shard_map/all_to_all | solution.py:62
  108.8 11.7 %all_to_all.33 = f32[8,8,512]{2,1,0:T(8,128)S(1)} all-to-all(f32[8,8,512]{2,1,0:T(8,128)S(1)} %broadcast_in_dim.11), channel_id=1, replica_groups=mesh['hi'=2,'z'=8,'bank'=32] {'z'}, dimensions={0} | all-to-all | bytes 262144 | tf_op jit(solution)/shard_map/all_to_all | solution.py:73
  120.9 0.9 copy.36
  121.8 4.4 %all-to-all-start.5 = ((bf16[4,64,512]{2,0,1:T(4,128)(2,1)}), bf16[4,64,512]{2,0,1:T(4,128)(2,1)S(1)}, u32[]{:S(2)}, u32[]{:S(2)}) async-start(bf16[4,64,512]{2,0,1:T(4,128)(2,1)} %copy.36), calls=%async_computation.5 | async-start | bytes 524288 | tf_op jit(solution)/shard_map/all_to_all | solution.py:81
  126.3 7.2 %collective-permute-start = (bf16[8,512]{1,0:T(8,128)(2,1)S(1)}, bf16[8,512]{1,0:T(8,128)(2,1)S(1)}, u32[]{:S(2)}, u32[]{:S(2)}) collective-permute-start(bf16[8,512]{1,0:T(8,128)(2,1)S(1)} %divide_convert_fusion), channel_id=1, source_target_pairs={{0,256},{256,0},{1,257},{257,1},{2,258},{258,2},{3,259},{259,3},{4... | collective-permute-start | bytes 24584 | tf_op jit(solution)/shard_map/ppermute | solution.py:84
  133.8 3.5 %collective-permute-done = bf16[8,512]{1,0:T(8,128)(2,1)S(1)} collective-permute-done((bf16[8,512]{1,0:T(8,128)(2,1)S(1)}, bf16[8,512]{1,0:T(8,128)(2,1)S(1)}, u32[]{:S(2)}, u32[]{:S(2)}) %collective-permute-start) | collective-permute-done | bytes 8224 | tf_op jit(solution)/shard_map/ppermute | solution.py:84
  137.4 0.6 pad_maximum_fusion.2
  138.0 2.1 %all-to-all-done.5 = bf16[4,64,512]{2,0,1:T(4,128)(2,1)S(1)} async-done(((bf16[4,64,512]{2,0,1:T(4,128)(2,1)}), bf16[4,64,512]{2,0,1:T(4,128)(2,1)S(1)}, u32[]{:S(2)}, u32[]{:S(2)}) %all-to-all-start.5) | async-done | bytes 262176 | tf_op jit(solution)/shard_map/all_to_all | solution.py:81
  140.1 0.9 convert_subtract_fusion.2
  (35 shorter events, 4.3 us)
Async XLA Ops:
  5.1 1.0 copy-start.2
  7.2 33.9 %all-to-all-start = ((f32[4,64,640]{2,0,1:T(4,128)}), f32[4,64,640]{2,0,1:T(4,128)S(1)}, u32[]{:S(2)}, u32[]{:S(2)}) async-start(f32[4,64,640]{2,0,1:T(4,128)} %pad_maximum_fusion), calls=%async_computation | async-start | bytes 1310720 | tf_op jit(solution)/shard_map/all_to_all | solution.py:62
  41.5 40.6 %copy-start = (bf16[1024,1024,1]{1,0,2:T(8,128)(2,1)S(1)}, bf16[1024,1024,1]{1,0,2:T(8,128)(2,1)}, u32[]{:S(2)}) copy-start(bf16[1024,1024,1]{1,0,2:T(8,128)(2,1)} %constant.20) | copy-start | bytes 6291460
  82.1 1.4 %copy-start.1 = (bf16[4,32768]{1,0:T(4,128)(2,1)S(1)}, bf16[4,32768]{1,0:T(4,128)(2,1)}, u32[]{:S(2)}) copy-start(bf16[4,32768]{1,0:T(4,128)(2,1)} %param.3) | copy-start | bytes 786436
  121.8 18.3 %all-to-all-start.5 = ((bf16[4,64,512]{2,0,1:T(4,128)(2,1)}), bf16[4,64,512]{2,0,1:T(4,128)(2,1)S(1)}, u32[]{:S(2)}, u32[]{:S(2)}) async-start(bf16[4,64,512]{2,0,1:T(4,128)(2,1)} %copy.36), calls=%async_computation.5 | async-start | bytes 524288 | tf_op jit(solution)/shard_map/all_to_all | solution.py:81
  126.3 11.1 %collective-permute-start = (bf16[8,512]{1,0:T(8,128)(2,1)S(1)}, bf16[8,512]{1,0:T(8,128)(2,1)S(1)}, u32[]{:S(2)}, u32[]{:S(2)}) collective-permute-start(bf16[8,512]{1,0:T(8,128)(2,1)S(1)} %divide_convert_fusion), channel_id=1, source_target_pairs={{0,256},{256,0},{1,257},{257,1},{2,258},{258,2},{3,259},{259,3},{4... | collective-permute-start | bytes 24584 | tf_op jit(solution)/shard_map/ppermute | solution.py:84

commit v12 on v9

--- a/solution.py
+++ b/solution.py
@@ -25,9 +25,11 @@
 
 def log_convolve(field_log, kernel_line, kernel_pair):
     member_count = field_log.shape[0]
-    raised = jnp.exp(field_log).astype(jnp.bfloat16).reshape(member_count * G, G * G)
-    inner_sum = jnp.dot(raised, kernel_pair, preferred_element_type=jnp.float32).reshape(
-        member_count, G, G * G
+    halves = field_log.shape[1] // G if field_log.ndim == 3 else 1
+    raised = jnp.exp(field_log).astype(jnp.bfloat16).reshape(member_count, G, halves, G * G // halves)
+    inner_sum = jnp.einsum(
+        "mxhc,hcd->mxd", raised, kernel_pair.reshape(halves, G * G // halves, G * G),
+        preferred_element_type=jnp.float32,
     )
     outer_sum = jnp.einsum("ij,mjc->mic", kernel_line, inner_sum, precision=lax.Precision.HIGHEST)
     return jnp.log(outer_sum).reshape(member_count, G * G * G)
@@ -80,14 +82,13 @@
             "msk,kc->msc", weights_in.astype(jnp.bfloat16), center_chunk, preferred_element_type=jnp.float32
         ).astype(jnp.bfloat16)
         returned = lax.all_to_all(wanted, spread_axes, 1, 1, tiled=True)
-        chosen = returned.reshape(member_count, cell_count)
-        potential = chosen.astype(jnp.float32) - smoothed
+        potential = returned.astype(jnp.float32) - smoothed.reshape(member_count, spread_size, chunk)
     other = lax.ppermute(center_chunk, "hi", [(0, 1), (1, 0)])
     first = lax.axis_index("hi") == 0
     centers = jnp.concatenate(
         [jnp.where(first, center_chunk, other), jnp.where(first, other, center_chunk)], axis=1
     )
-    return (centers, potential)
+    return (centers, potential.reshape(member_count, cell_count))
 
 
 def solution(mesh):

time: 142 us -> 141 us (level)
  local copies, waits for them, and re-layouts: 6.05 us -> 4.5 us
  transfers between devices with their start and end apart: 3 -> 3, of which waited for: 3 -> 3; matrix products, arithmetic and copies ran while one was open for 1% -> 0% of each run, Pallas kernels for 0% -> 0%
where the time goes in v12:
time: 141 us
  blocking collectives  71.9 us (51%)
  waiting for transfers between devices  28.2 us (20%)
  starting transfers between devices  23.2 us (16%)
  other arithmetic  6.24 us (4%)
  matrix products  5.45 us (4%)
  local copies, waits for them, and re-layouts  4.5 us (3%)
    all_to_all x2, blocking collectives, per_device(): summed = jnp.sum(lax.all_to_all(peers, 'z', 0, 0, tiled=True), axis=0)  30.9 us
    all_to_all x1, blocking collectives, per_device(): arrived = lax.all_to_all(rows, spread_axes, 1, 1, tiled=True)  23.1 us
    all_to_all x1, waiting for transfers between devices, per_device(): arrived = lax.all_to_all(rows, spread_axes, 1, 1, tiled=True)  22.3 us
    all_to_all x1, blocking collectives, per_device(): returned = lax.all_to_all(wanted, spread_axes, 1, 1, tiled=True)  17.9 us
    all_to_all x1, starting transfers between devices, per_device(): arrived = lax.all_to_all(rows, spread_axes, 1, 1, tiled=True)  11.6 us
    ppermute x1, starting transfers between devices, per_device(): other = lax.ppermute(center_chunk, 'hi', [(0, 1), (1, 0)])  7.17 us
    all_to_all x1, starting transfers between devices, per_device(): returned = lax.all_to_all(wanted, spread_axes, 1, 1, tiled=True)  4.46 us
    ppermute x1, waiting for transfers between devices, per_device(): other = lax.ppermute(center_chunk, 'hi', [(0, 1), (1, 0)])  3.87 us
  transfers between devices with their start and end apart: 3, of which 3 were waited for; matrix products, arithmetic and copies ran while one was open for 0% of the time, Pallas kernels for 0%

profile of v12, /device:TPU:1, one launch (start us, length us, event | category | flops | bytes accessed | tf_op | source)
XLA Modules:
  0.0 140.5 jit_solution(17265971739838453347)
XLA Ops:
  0.7 2.2 %fusion.2 = bf16[1024,1024]{1,0:T(8,128)(2,1)S(1)} fusion(s32[1024]{0:T(1024)S(1)} %get-tuple-element.5, s32[1024]{0:T(1024)S(1)} %get-tuple-element.6, s32[1024]{0:T(1024)S(1)} %get-tuple-element.4, s32[1024]{0:T(1024)S(1)} %get-tuple-element.7, pred[1024]{0:T(1024)(128)(4,1)S(1)} %get-tuple-element.8, pred[1024]{0:T(1024)(128)(4,1)S(1)} %get-tuple-element.9), kind=kLoop, calls=%fused_computation.4 | loop fusion | flops 16777216 | bytes 2115584 | tf_op jit(solution)/shard_map/convert_element_type | solution.py:22
  4.0 0.5 fusion.6
  4.5 0.6 fusion.10
  5.7 1.0 pad_maximum_fusion
  6.6 11.6 %all-to-all-start = ((f32[4,64,640]{2,0,1:T(4,128)}), f32[4,64,640]{2,0,1:T(4,128)S(1)}, u32[]{:S(2)}, u32[]{:S(2)}) async-start(f32[4,64,640]{2,0,1:T(4,128)} %pad_maximum_fusion), calls=%async_computation | async-start | bytes 1310720 | tf_op jit(solution)/shard_map/all_to_all | solution.py:65
  18.3 22.3 %all-to-all-done = f32[4,64,640]{2,0,1:T(4,128)S(1)} async-done(((f32[4,64,640]{2,0,1:T(4,128)}), f32[4,64,640]{2,0,1:T(4,128)S(1)}, u32[]{:S(2)}, u32[]{:S(2)}) %all-to-all-start) | async-done | bytes 655392 | tf_op jit(solution)/shard_map/all_to_all | solution.py:65
  40.5 0.7 slice.16
  41.2 1.0 copy.25
  43.0 19.3 %all_to_all.30 = f32[8,8,640]{2,1,0:T(8,128)S(1)} all-to-all(f32[8,8,640]{2,1,0:T(8,128)S(1)} %broadcast_in_dim.10), channel_id=1, replica_groups=mesh['hi'=2,'z'=8,'bank'=32] {'z'}, dimensions={0} | all-to-all | bytes 327680 | tf_op jit(solution)/shard_map/all_to_all | solution.py:76
  62.9 17.9 %all_to_all.31 = bf16[4,64,512]{2,0,1:T(4,128)(2,1)S(1)} all-to-all(bf16[4,64,512]{2,0,1:T(4,128)(2,1)S(1)} %copy.27), channel_id=1, replica_groups=mesh['hi'=2,'z'=8,'bank'=32] {'bank','hi'}, dimensions={1} | all-to-all | bytes 524288 | tf_op jit(solution)/shard_map/all_to_all | solution.py:84
  80.9 0.5 exponential_convert_fusion
  81.3 0.5 convolution_bitcast_fusion
  81.8 0.6 fusion.9
  83.0 0.5 fusion.4
  83.4 0.6 fusion.8
  84.5 23.1 %all_to_all.32 = f32[4,64,512]{2,0,1:T(4,128)S(1)} all-to-all(f32[4,64,512]{2,0,1:T(4,128)S(1)} %copy.30), channel_id=1, replica_groups=mesh['hi'=2,'z'=8,'bank'=32] {'bank','hi'}, dimensions={1} | all-to-all | bytes 1048576 | tf_op jit(solution)/shard_map/all_to_all | solution.py:65
  108.0 11.7 %all_to_all.33 = f32[8,8,512]{2,1,0:T(8,128)S(1)} all-to-all(f32[8,8,512]{2,1,0:T(8,128)S(1)} %broadcast_in_dim.11), channel_id=1, replica_groups=mesh['hi'=2,'z'=8,'bank'=32] {'z'}, dimensions={0} | all-to-all | bytes 262144 | tf_op jit(solution)/shard_map/all_to_all | solution.py:76
  120.1 0.9 copy.32
  121.0 4.5 %all-to-all-start.5 = ((bf16[4,64,512]{2,0,1:T(4,128)(2,1)}), bf16[4,64,512]{2,0,1:T(4,128)(2,1)S(1)}, u32[]{:S(2)}, u32[]{:S(2)}) async-start(bf16[4,64,512]{2,0,1:T(4,128)(2,1)} %copy.32), calls=%async_computation.5 | async-start | bytes 524288 | tf_op jit(solution)/shard_map/all_to_all | solution.py:84
  125.5 7.2 %collective-permute-start = (bf16[8,512]{1,0:T(8,128)(2,1)S(1)}, bf16[8,512]{1,0:T(8,128)(2,1)S(1)}, u32[]{:S(2)}, u32[]{:S(2)}) collective-permute-start(bf16[8,512]{1,0:T(8,128)(2,1)S(1)} %divide_convert_fusion), channel_id=1, source_target_pairs={{0,256},{256,0},{1,257},{257,1},{2,258},{258,2},{3,259},{259,3},{4... | collective-permute-start | bytes 24584 | tf_op jit(solution)/shard_map/ppermute | solution.py:86
  132.7 3.9 %collective-permute-done = bf16[8,512]{1,0:T(8,128)(2,1)S(1)} collective-permute-done((bf16[8,512]{1,0:T(8,128)(2,1)S(1)}, bf16[8,512]{1,0:T(8,128)(2,1)S(1)}, u32[]{:S(2)}, u32[]{:S(2)}) %collective-permute-start) | collective-permute-done | bytes 8224 | tf_op jit(solution)/shard_map/ppermute | solution.py:86
  136.6 0.6 pad_maximum_fusion.2
  137.2 2.1 %all-to-all-done.5 = bf16[4,64,512]{2,0,1:T(4,128)(2,1)S(1)} async-done(((bf16[4,64,512]{2,0,1:T(4,128)(2,1)}), bf16[4,64,512]{2,0,1:T(4,128)(2,1)S(1)}, u32[]{:S(2)}, u32[]{:S(2)}) %all-to-all-start.5) | async-done | bytes 262176 | tf_op jit(solution)/shard_map/all_to_all | solution.py:84
  139.3 1.2 convert_subtract_fusion.2
  (36 shorter events, 5.0 us)
Async XLA Ops:
  2.9 1.0 copy-start
  4.5 1.0 copy-start.1
  6.6 33.9 %all-to-all-start = ((f32[4,64,640]{2,0,1:T(4,128)}), f32[4,64,640]{2,0,1:T(4,128)S(1)}, u32[]{:S(2)}, u32[]{:S(2)}) async-start(f32[4,64,640]{2,0,1:T(4,128)} %pad_maximum_fusion), calls=%async_computation | async-start | bytes 1310720 | tf_op jit(solution)/shard_map/all_to_all | solution.py:65
  121.0 18.3 %all-to-all-start.5 = ((bf16[4,64,512]{2,0,1:T(4,128)(2,1)}), bf16[4,64,512]{2,0,1:T(4,128)(2,1)S(1)}, u32[]{:S(2)}, u32[]{:S(2)}) async-start(bf16[4,64,512]{2,0,1:T(4,128)(2,1)} %copy.32), calls=%async_computation.5 | async-start | bytes 524288 | tf_op jit(solution)/shard_map/all_to_all | solution.py:84
  125.5 11.1 %collective-permute-start = (bf16[8,512]{1,0:T(8,128)(2,1)S(1)}, bf16[8,512]{1,0:T(8,128)(2,1)S(1)}, u32[]{:S(2)}, u32[]{:S(2)}) collective-permute-start(bf16[8,512]{1,0:T(8,128)(2,1)S(1)} %divide_convert_fusion), channel_id=1, source_target_pairs={{0,256},{256,0},{1,257},{257,1},{2,258},{258,2},{3,259},{259,3},{4... | collective-permute-start | bytes 24584 | tf_op jit(solution)/shard_map/ppermute | solution.py:86

commit v13 on v12

--- a/solution.py
+++ b/solution.py
@@ -64,7 +64,8 @@
             rows = jnp.concatenate([rows, label_lanes], axis=2)
         arrived = lax.all_to_all(rows, spread_axes, 1, 1, tiled=True)
         if weights_in is None:
-            weights_in = (arrived[:, :, chunk, None] == labels.astype(jnp.float32)).astype(jnp.float32)
+            label_in = arrived[:, :, chunk].astype(jnp.int32)
+            weights_in = (label_in[:, :, None] == labels).astype(jnp.float32)
             arrived = arrived[:, :, :chunk]
         group_sums = jnp.einsum("msk,msc->kc", weights_in, arrived, precision=lax.Precision.HIGHEST)
         if counts is None:
@@ -78,9 +79,9 @@
             counts = summed[:, chunk]
             summed = summed[:, :chunk]
         center_chunk = (summed / counts[:, None]).astype(jnp.bfloat16)
-        wanted = jnp.einsum(
-            "msk,kc->msc", weights_in.astype(jnp.bfloat16), center_chunk, preferred_element_type=jnp.float32
-        ).astype(jnp.bfloat16)
+        wanted = jnp.broadcast_to(center_chunk[0], (member_count, spread_size, chunk))
+        for bar in range(1, BARS):
+            wanted = jnp.where(label_in[:, :, None] == bar, center_chunk[bar], wanted)
         returned = lax.all_to_all(wanted, spread_axes, 1, 1, tiled=True)
         potential = returned.astype(jnp.float32) - smoothed.reshape(member_count, spread_size, chunk)
     other = lax.ppermute(center_chunk, "hi", [(0, 1), (1, 0)])

time: 141 us -> 141 us (level)
  blocking collectives: 71.9 us -> 86.4 us
  waiting for transfers between devices: 28.2 us -> 14.6 us
  starting transfers between devices: 23.2 us -> 21.7 us
    all_to_all x1 -> x2, blocking collectives: 23.1 us -> 56.8 us  [per_device(): arrived = lax.all_to_all(rows, spread_axes, 1, 1, tiled=True)]
    all_to_all x2 -> x1, blocking collectives: 30.9 us -> 11.7 us  [per_device(): summed = jnp.sum(lax.all_to_all(peers, 'z', 0, 0, tiled=True), axis=0)]
    all_to_all x1, waiting for transfers between devices: 22.3 us -> 8.61 us  [per_device(): summed = jnp.sum(lax.all_to_all(peers, 'z', 0, 0, tiled=True), axis=0)]
    select_n x0 -> x2, other arithmetic: none -> 1.98 us  [per_device(): wanted = jnp.where(label_in[:, :, None] == bar, center_chunk[bar], wanted)]
    all_to_all x1, starting transfers between devices: 11.6 us -> 10 us  [per_device(): summed = jnp.sum(lax.all_to_all(peers, 'z', 0, 0, tiled=True), axis=0)]
  transfers between devices with their start and end apart: 3 -> 3, of which waited for: 3 -> 3; matrix products, arithmetic and copies ran while one was open for 0% -> 1% of each run, Pallas kernels for 0% -> 0%
where the time goes in v13:
time: 141 us
  blocking collectives  86.4 us (61%)
  starting transfers between devices  21.7 us (15%)
  waiting for transfers between devices  14.6 us (10%)
  other arithmetic  7.41 us (5%)
  local copies, waits for them, and re-layouts  4.98 us (4%)
  matrix products  4.77 us (3%)
    all_to_all x2, blocking collectives, per_device(): arrived = lax.all_to_all(rows, spread_axes, 1, 1, tiled=True)  56.8 us
    all_to_all x1, blocking collectives, per_device(): returned = lax.all_to_all(wanted, spread_axes, 1, 1, tiled=True)  17.9 us
    all_to_all x1, blocking collectives, per_device(): summed = jnp.sum(lax.all_to_all(peers, 'z', 0, 0, tiled=True), axis=0)  11.7 us
    all_to_all x1, starting transfers between devices, per_device(): summed = jnp.sum(lax.all_to_all(peers, 'z', 0, 0, tiled=True), axis=0)  10 us
    all_to_all x1, waiting for transfers between devices, per_device(): summed = jnp.sum(lax.all_to_all(peers, 'z', 0, 0, tiled=True), axis=0)  8.61 us
    ppermute x1, starting transfers between devices, per_device(): other = lax.ppermute(center_chunk, 'hi', [(0, 1), (1, 0)])  7.17 us
    all_to_all x1, starting transfers between devices, per_device(): returned = lax.all_to_all(wanted, spread_axes, 1, 1, tiled=True)  4.46 us
    ppermute x1, waiting for transfers between devices, per_device(): other = lax.ppermute(center_chunk, 'hi', [(0, 1), (1, 0)])  3.87 us
  transfers between devices with their start and end apart: 3, of which 3 were waited for; matrix products, arithmetic and copies ran while one was open for 1% of the time, Pallas kernels for 0%

profile of v13, /device:TPU:1, one launch (start us, length us, event | category | flops | bytes accessed | tf_op | source)
XLA Modules:
  0.0 140.7 jit_solution(3333638742714110245)
XLA Ops:
  0.7 2.2 %fusion.2 = bf16[1024,1024]{1,0:T(8,128)(2,1)S(1)} fusion(s32[1024]{0:T(1024)S(1)} %get-tuple-element.28, s32[1024]{0:T(1024)S(1)} %get-tuple-element.29, s32[1024]{0:T(1024)S(1)} %get-tuple-element.27, s32[1024]{0:T(1024)S(1)} %get-tuple-element.30, pred[1024]{0:T(1024)(128)(4,1)S(1)} %get-tuple-element.31, pred[1024]{0:T(1024)(128)(4,1)S(1)} %get-tuple-element.32), kind=kLoop, calls=%fused_computation.4 | loop fusion | flops 16777216 | bytes 2115584 | tf_op jit(solution)/shard_map/convert_element_type | solution.py:22
  4.0 0.5 fusion.6
  4.5 0.6 fusion.10
  5.8 33.7 %all_to_all.30 = f32[4,64,640]{2,0,1:T(4,128)S(1)} all-to-all(f32[4,64,640]{2,0,1:T(4,128)S(1)} %pad_maximum_fusion), channel_id=1, replica_groups=mesh['hi'=2,'z'=8,'bank'=32] {'bank','hi'}, dimensions={1} | all-to-all | bytes 1310720 | tf_op jit(solution)/shard_map/all_to_all | solution.py:65
  39.5 0.7 slice.80
  40.2 1.0 copy.86
  41.8 0.7 broadcast_in_dim.168
  42.5 10.0 %all-to-all-start.1 = ((f32[8,8,640]{2,1,0:T(8,128)}), f32[8,8,640]{2,1,0:T(8,128)S(1)}, u32[]{:S(2)}, u32[]{:S(2)}) async-start(f32[8,8,640]{2,1,0:T(8,128)} %broadcast_in_dim.168), calls=%async_computation.1 | async-start | bytes 327680 | tf_op jit(solution)/shard_map/all_to_all | solution.py:77
  53.4 8.6 %all-to-all-done.1 = f32[8,8,640]{2,1,0:T(8,128)S(1)} async-done(((f32[8,8,640]{2,1,0:T(8,128)}), f32[8,8,640]{2,1,0:T(8,128)S(1)}, u32[]{:S(2)}, u32[]{:S(2)}) %all-to-all-start.1) | async-done | bytes 163872 | tf_op jit(solution)/shard_map/all_to_all | solution.py:77
  62.3 0.7 select_select_fusion.1
  63.0 17.9 %all_to_all.31 = bf16[4,64,512]{2,0,1:T(4,128)(2,1)S(1)} all-to-all(bf16[4,64,512]{2,0,1:T(4,128)(2,1)S(1)} %select_select_fusion.1), channel_id=1, replica_groups=mesh['hi'=2,'z'=8,'bank'=32] {'bank','hi'}, dimensions={1} | all-to-all | bytes 524288 | tf_op jit(solution)/shard_map/all_to_all | solution.py:85
  81.3 0.5 convolution_bitcast_fusion
  81.8 0.6 fusion.9
  83.0 0.5 fusion.4
  83.5 0.6 fusion.8
  84.5 23.1 %all_to_all.32 = f32[4,64,512]{2,0,1:T(4,128)S(1)} all-to-all(f32[4,64,512]{2,0,1:T(4,128)S(1)} %copy.82), channel_id=1, replica_groups=mesh['hi'=2,'z'=8,'bank'=32] {'bank','hi'}, dimensions={1} | all-to-all | bytes 1048576 | tf_op jit(solution)/shard_map/all_to_all | solution.py:65
  108.0 11.7 %all_to_all.33 = f32[8,8,512]{2,1,0:T(8,128)S(1)} all-to-all(f32[8,8,512]{2,1,0:T(8,128)S(1)} %broadcast_in_dim.189), channel_id=1, replica_groups=mesh['hi'=2,'z'=8,'bank'=32] {'z'}, dimensions={0} | all-to-all | bytes 262144 | tf_op jit(solution)/shard_map/all_to_all | solution.py:77
  119.8 1.3 select_select_fusion
  121.2 4.5 %all-to-all-start.5 = ((bf16[4,64,512]{2,0,1:T(4,128)(2,1)}), bf16[4,64,512]{2,0,1:T(4,128)(2,1)S(1)}, u32[]{:S(2)}, u32[]{:S(2)}) async-start(bf16[4,64,512]{2,0,1:T(4,128)(2,1)} %select_select_fusion), calls=%async_computation.5 | async-start | bytes 524288 | tf_op jit(solution)/shard_map/all_to_all | solution.py:85
  125.6 7.2 %collective-permute-start = (bf16[8,512]{1,0:T(8,128)(2,1)S(1)}, bf16[8,512]{1,0:T(8,128)(2,1)S(1)}, u32[]{:S(2)}, u32[]{:S(2)}) collective-permute-start(bf16[8,512]{1,0:T(8,128)(2,1)S(1)} %divide_convert_fusion), channel_id=1, source_target_pairs={{0,256},{256,0},{1,257},{257,1},{2,258},{258,2},{3,259},{259,3},{4... | collective-permute-start | bytes 24584 | tf_op jit(solution)/shard_map/ppermute | solution.py:87
  132.8 3.9 %collective-permute-done = bf16[8,512]{1,0:T(8,128)(2,1)S(1)} collective-permute-done((bf16[8,512]{1,0:T(8,128)(2,1)S(1)}, bf16[8,512]{1,0:T(8,128)(2,1)S(1)}, u32[]{:S(2)}, u32[]{:S(2)}) %collective-permute-start) | collective-permute-done | bytes 8224 | tf_op jit(solution)/shard_map/ppermute | solution.py:87
  136.8 0.6 pad_maximum_fusion.2
  137.4 2.1 %all-to-all-done.5 = bf16[4,64,512]{2,0,1:T(4,128)(2,1)S(1)} async-done(((bf16[4,64,512]{2,0,1:T(4,128)(2,1)}), bf16[4,64,512]{2,0,1:T(4,128)(2,1)S(1)}, u32[]{:S(2)}, u32[]{:S(2)}) %all-to-all-start.5) | async-done | bytes 262176 | tf_op jit(solution)/shard_map/all_to_all | solution.py:85
  139.5 1.2 convert_subtract_fusion.2
  (45 shorter events, 5.6 us)
Async XLA Ops:
  2.9 1.0 copy-start
  4.5 1.0 copy-start.1
  42.5 19.5 %all-to-all-start.1 = ((f32[8,8,640]{2,1,0:T(8,128)}), f32[8,8,640]{2,1,0:T(8,128)S(1)}, u32[]{:S(2)}, u32[]{:S(2)}) async-start(f32[8,8,640]{2,1,0:T(8,128)} %broadcast_in_dim.168), calls=%async_computation.1 | async-start | bytes 327680 | tf_op jit(solution)/shard_map/all_to_all | solution.py:77
  121.2 18.3 %all-to-all-start.5 = ((bf16[4,64,512]{2,0,1:T(4,128)(2,1)}), bf16[4,64,512]{2,0,1:T(4,128)(2,1)S(1)}, u32[]{:S(2)}, u32[]{:S(2)}) async-start(bf16[4,64,512]{2,0,1:T(4,128)(2,1)} %select_select_fusion), calls=%async_computation.5 | async-start | bytes 524288 | tf_op jit(solution)/shard_map/all_to_all | solution.py:85
  125.6 11.1 %collective-permute-start = (bf16[8,512]{1,0:T(8,128)(2,1)S(1)}, bf16[8,512]{1,0:T(8,128)(2,1)S(1)}, u32[]{:S(2)}, u32[]{:S(2)}) collective-permute-start(bf16[8,512]{1,0:T(8,128)(2,1)S(1)} %divide_convert_fusion), channel_id=1, source_target_pairs={{0,256},{256,0},{1,257},{257,1},{2,258},{258,2},{3,259},{259,3},{4... | collective-permute-start | bytes 24584 | tf_op jit(solution)/shard_map/ppermute | solution.py:87

commit v14 on v12

--- a/solution.py
+++ b/solution.py
@@ -30,8 +30,9 @@
     inner_sum = jnp.einsum(
         "mxhc,hcd->mxd", raised, kernel_pair.reshape(halves, G * G // halves, G * G),
         preferred_element_type=jnp.float32,
-    )
-    outer_sum = jnp.einsum("ij,mjc->mic", kernel_line, inner_sum, precision=lax.Precision.HIGHEST)
+    ).reshape(member_count * G, G * G)
+    blocks = jnp.kron(jnp.eye(member_count, dtype=jnp.float32), kernel_line)
+    outer_sum = jnp.dot(blocks, inner_sum, precision=lax.Precision.HIGHEST)
     return jnp.log(outer_sum).reshape(member_count, G * G * G)
 
 

time: 141 us -> 140 us (level)
    slice x2, local copies, waits for them, and re-layouts: 1.67 us -> 0.12 us  [per_device(): arrived[:, :, chunk, None] == labels.astype(jnp.float32)]
where the time goes in v14:
time: 140 us
  blocking collectives  71.9 us (51%)
  waiting for transfers between devices  28.2 us (20%)
  starting transfers between devices  23.2 us (17%)
  other arithmetic  6.37 us (5%)
  matrix products  5.35 us (4%)
  local copies, waits for them, and re-layouts  3.58 us (3%)
    all_to_all x2, blocking collectives, per_device(): summed = jnp.sum(lax.all_to_all(peers, 'z', 0, 0, tiled=True), axis=0)  30.9 us
    all_to_all x1, blocking collectives, per_device(): arrived = lax.all_to_all(rows, spread_axes, 1, 1, tiled=True)  23.1 us
    all_to_all x1, waiting for transfers between devices, per_device(): arrived = lax.all_to_all(rows, spread_axes, 1, 1, tiled=True)  22.3 us
    all_to_all x1, blocking collectives, per_device(): returned = lax.all_to_all(wanted, spread_axes, 1, 1, tiled=True)  17.9 us
    all_to_all x1, starting transfers between devices, per_device(): arrived = lax.all_to_all(rows, spread_axes, 1, 1, tiled=True)  11.6 us
    ppermute x1, starting transfers between devices, per_device(): other = lax.ppermute(center_chunk, 'hi', [(0, 1), (1, 0)])  7.17 us
    all_to_all x1, starting transfers between devices, per_device(): returned = lax.all_to_all(wanted, spread_axes, 1, 1, tiled=True)  4.45 us
    ppermute x1, waiting for transfers between devices, per_device(): other = lax.ppermute(center_chunk, 'hi', [(0, 1), (1, 0)])  3.87 us
  transfers between devices with their start and end apart: 3, of which 3 were waited for; matrix products, arithmetic and copies ran while one was open for 0% of the time, Pallas kernels for 0%

profile of v14, /device:TPU:1, one launch (start us, length us, event | category | flops | bytes accessed | tf_op | source)
XLA Modules:
  0.0 139.7 jit_solution(17451296374526921110)
XLA Ops:
  0.7 2.2 %fusion.2 = bf16[1024,1024]{1,0:T(8,128)(2,1)S(1)} fusion(s32[1024]{0:T(1024)S(1)} %get-tuple-element.5, s32[1024]{0:T(1024)S(1)} %get-tuple-element.6, s32[1024]{0:T(1024)S(1)} %get-tuple-element.4, s32[1024]{0:T(1024)S(1)} %get-tuple-element.7, pred[1024]{0:T(1024)(128)(4,1)S(1)} %get-tuple-element.8, pred[1024]{0:T(1024)(128)(4,1)S(1)} %get-tuple-element.9), kind=kLoop, calls=%fused_computation.4 | loop fusion | flops 16777216 | bytes 2115584 | tf_op jit(solution)/shard_map/convert_element_type | solution.py:22
  2.9 0.5 fusion.11
  4.2 0.4 fusion.42
  5.0 0.6 convolution_log_fusion.2
  6.1 1.0 pad_maximum_fusion
  7.1 11.6 %all-to-all-start = ((f32[4,64,640]{2,0,1:T(4,128)}), f32[4,64,640]{2,0,1:T(4,128)S(1)}, u32[]{:S(2)}, u32[]{:S(2)}) async-start(f32[4,64,640]{2,0,1:T(4,128)} %pad_maximum_fusion), calls=%async_computation | async-start | bytes 1310720 | tf_op jit(solution)/shard_map/all_to_all | solution.py:66
  18.7 22.3 %all-to-all-done = f32[4,64,640]{2,0,1:T(4,128)S(1)} async-done(((f32[4,64,640]{2,0,1:T(4,128)}), f32[4,64,640]{2,0,1:T(4,128)S(1)}, u32[]{:S(2)}, u32[]{:S(2)}) %all-to-all-start) | async-done | bytes 655392 | tf_op jit(solution)/shard_map/all_to_all | solution.py:66
  41.4 0.4 convolution_bitcast_fusion.2
  41.9 19.3 %all_to_all.30 = f32[8,8,640]{2,1,0:T(8,128)S(1)} all-to-all(f32[8,8,640]{2,1,0:T(8,128)S(1)} %broadcast_in_dim.22), channel_id=1, replica_groups=mesh['hi'=2,'z'=8,'bank'=32] {'z'}, dimensions={0} | all-to-all | bytes 327680 | tf_op jit(solution)/shard_map/all_to_all | solution.py:77
  61.9 17.9 %all_to_all.31 = bf16[4,64,512]{2,0,1:T(4,128)(2,1)S(1)} all-to-all(bf16[4,64,512]{2,0,1:T(4,128)(2,1)S(1)} %copy.27), channel_id=1, replica_groups=mesh['hi'=2,'z'=8,'bank'=32] {'bank','hi'}, dimensions={1} | all-to-all | bytes 524288 | tf_op jit(solution)/shard_map/all_to_all | solution.py:85
  79.8 0.5 exponential_convert_fusion
  80.3 0.4 convolution_bitcast_fusion
  80.8 0.6 convolution_log_fusion.1
  82.1 0.4 fusion.43
  82.6 0.6 convolution_log_fusion
  83.6 23.1 %all_to_all.32 = f32[4,64,512]{2,0,1:T(4,128)S(1)} all-to-all(f32[4,64,512]{2,0,1:T(4,128)S(1)} %copy.30), channel_id=1, replica_groups=mesh['hi'=2,'z'=8,'bank'=32] {'bank','hi'}, dimensions={1} | all-to-all | bytes 1048576 | tf_op jit(solution)/shard_map/all_to_all | solution.py:66
  107.2 11.7 %all_to_all.33 = f32[8,8,512]{2,1,0:T(8,128)S(1)} all-to-all(f32[8,8,512]{2,1,0:T(8,128)S(1)} %broadcast_in_dim.23), channel_id=1, replica_groups=mesh['hi'=2,'z'=8,'bank'=32] {'z'}, dimensions={0} | all-to-all | bytes 262144 | tf_op jit(solution)/shard_map/all_to_all | solution.py:77
  119.3 0.9 copy.32
  120.2 4.5 %all-to-all-start.5 = ((bf16[4,64,512]{2,0,1:T(4,128)(2,1)}), bf16[4,64,512]{2,0,1:T(4,128)(2,1)S(1)}, u32[]{:S(2)}, u32[]{:S(2)}) async-start(bf16[4,64,512]{2,0,1:T(4,128)(2,1)} %copy.32), calls=%async_computation.5 | async-start | bytes 524288 | tf_op jit(solution)/shard_map/all_to_all | solution.py:85
  124.6 7.2 %collective-permute-start = (bf16[8,512]{1,0:T(8,128)(2,1)S(1)}, bf16[8,512]{1,0:T(8,128)(2,1)S(1)}, u32[]{:S(2)}, u32[]{:S(2)}) collective-permute-start(bf16[8,512]{1,0:T(8,128)(2,1)S(1)} %divide_convert_fusion), channel_id=1, source_target_pairs={{0,256},{256,0},{1,257},{257,1},{2,258},{258,2},{3,259},{259,3},{4... | collective-permute-start | bytes 24584 | tf_op jit(solution)/shard_map/ppermute | solution.py:87
  131.8 3.9 %collective-permute-done = bf16[8,512]{1,0:T(8,128)(2,1)S(1)} collective-permute-done((bf16[8,512]{1,0:T(8,128)(2,1)S(1)}, bf16[8,512]{1,0:T(8,128)(2,1)S(1)}, u32[]{:S(2)}, u32[]{:S(2)}) %collective-permute-start) | collective-permute-done | bytes 8224 | tf_op jit(solution)/shard_map/ppermute | solution.py:87
  135.8 0.6 pad_maximum_fusion.2
  136.4 2.1 %all-to-all-done.5 = bf16[4,64,512]{2,0,1:T(4,128)(2,1)S(1)} async-done(((bf16[4,64,512]{2,0,1:T(4,128)(2,1)}), bf16[4,64,512]{2,0,1:T(4,128)(2,1)S(1)}, u32[]{:S(2)}, u32[]{:S(2)}) %all-to-all-start.5) | async-done | bytes 262176 | tf_op jit(solution)/shard_map/all_to_all | solution.py:85
  138.5 1.2 convert_subtract_fusion.2
  (45 shorter events, 5.0 us)
Async XLA Ops:
  2.9 1.0 copy-start
  4.7 1.3 copy-start.2
  7.1 33.9 %all-to-all-start = ((f32[4,64,640]{2,0,1:T(4,128)}), f32[4,64,640]{2,0,1:T(4,128)S(1)}, u32[]{:S(2)}, u32[]{:S(2)}) async-start(f32[4,64,640]{2,0,1:T(4,128)} %pad_maximum_fusion), calls=%async_computation | async-start | bytes 1310720 | tf_op jit(solution)/shard_map/all_to_all | solution.py:66
  80.3 1.4 %copy-start.1 = (bf16[4,32768]{1,0:T(4,128)(2,1)S(1)}, bf16[4,32768]{1,0:T(4,128)(2,1)}, u32[]{:S(2)}) copy-start(bf16[4,32768]{1,0:T(4,128)(2,1)} %param.2) | copy-start | bytes 786436
  120.2 18.3 %all-to-all-start.5 = ((bf16[4,64,512]{2,0,1:T(4,128)(2,1)}), bf16[4,64,512]{2,0,1:T(4,128)(2,1)S(1)}, u32[]{:S(2)}, u32[]{:S(2)}) async-start(bf16[4,64,512]{2,0,1:T(4,128)(2,1)} %copy.32), calls=%async_computation.5 | async-start | bytes 524288 | tf_op jit(solution)/shard_map/all_to_all | solution.py:85
  124.6 11.1 %collective-permute-start = (bf16[8,512]{1,0:T(8,128)(2,1)S(1)}, bf16[8,512]{1,0:T(8,128)(2,1)S(1)}, u32[]{:S(2)}, u32[]{:S(2)}) collective-permute-start(bf16[8,512]{1,0:T(8,128)(2,1)S(1)} %divide_convert_fusion), channel_id=1, source_target_pairs={{0,256},{256,0},{1,257},{257,1},{2,258},{258,2},{3,259},{259,3},{4... | collective-permute-start | bytes 24584 | tf_op jit(solution)/shard_map/ppermute | solution.py:87

commit v15 on v14

--- a/solution.py
+++ b/solution.py
@@ -15,11 +15,12 @@
     row = lax.broadcasted_iota(jnp.int32, (G * G, G * G), 0)
     col = lax.broadcasted_iota(jnp.int32, (G * G, G * G), 1)
 
-    def line_at(a, b):
+    def squared_gap(a, b):
         gap = a.astype(jnp.float32) - b.astype(jnp.float32)
-        return jnp.exp(-0.5 * gap * gap)
+        return gap * gap
 
-    kernel_pair = (line_at(row // G, col // G) * line_at(row % G, col % G)).astype(jnp.bfloat16)
+    spread = squared_gap(row // G, col // G) + squared_gap(row % G, col % G)
+    kernel_pair = jnp.exp(-0.5 * spread).astype(jnp.bfloat16)
     return (kernel_line, lax.optimization_barrier(kernel_pair))
 
 

time: 140 us -> 140 us (level)
  no operation moved by 1% of the time
where the time goes in v15:
time: 140 us; the launch traced here: 139 us
  blocking collectives  71.9 us (51%)
  waiting for transfers between devices  28.2 us (20%)
  starting transfers between devices  23.2 us (17%)
  other arithmetic  6.08 us (4%)
  matrix products  5.35 us (4%)
  local copies, waits for them, and re-layouts  3.43 us (2%)
    all_to_all x2, blocking collectives, per_device(): summed = jnp.sum(lax.all_to_all(peers, 'z', 0, 0, tiled=True), axis=0)  30.9 us
    all_to_all x1, blocking collectives, per_device(): arrived = lax.all_to_all(rows, spread_axes, 1, 1, tiled=True)  23.1 us
    all_to_all x1, waiting for transfers between devices, per_device(): arrived = lax.all_to_all(rows, spread_axes, 1, 1, tiled=True)  22.3 us
    all_to_all x1, blocking collectives, per_device(): returned = lax.all_to_all(wanted, spread_axes, 1, 1, tiled=True)  17.9 us
    all_to_all x1, starting transfers between devices, per_device(): arrived = lax.all_to_all(rows, spread_axes, 1, 1, tiled=True)  11.6 us
    ppermute x1, starting transfers between devices, per_device(): other = lax.ppermute(center_chunk, 'hi', [(0, 1), (1, 0)])  7.17 us
    all_to_all x1, starting transfers between devices, per_device(): returned = lax.all_to_all(wanted, spread_axes, 1, 1, tiled=True)  4.46 us
    ppermute x1, waiting for transfers between devices, per_device(): other = lax.ppermute(center_chunk, 'hi', [(0, 1), (1, 0)])  3.87 us
  transfers between devices with their start and end apart: 3, of which 3 were waited for; matrix products, arithmetic and copies ran while one was open for 0% of the time, Pallas kernels for 0%

profile of v15, /device:TPU:1, one launch (start us, length us, event | category | flops | bytes accessed | tf_op | source)
XLA Modules:
  0.0 139.2 jit_solution(1623780441197340154)
XLA Ops:
  0.7 1.9 %exponential_convert_fusion = bf16[1024,1024]{1,0:T(8,128)(2,1)S(1)} fusion(s32[1024]{0:T(1024)S(1)} %get-tuple-element.5, s32[1024]{0:T(1024)S(1)} %get-tuple-element.6, s32[1024]{0:T(1024)S(1)} %get-tuple-element.4, s32[1024]{0:T(1024)S(1)} %get-tuple-element.7, pred[1024]{0:T(1024)(128)(4,1)S(1)} %get-tuple-element.8, pred[1024]{0:T(1024)(128)(4,1)S(1)} %get-tuple-element.9), kind=kLoop, calls=%fused_computation | loop fusion | flops 15728640 | bytes 2115584 | tf_op jit(solution)/shard_map/convert_element_type | solution.py:23
  2.6 0.5 fusion.7
  3.8 0.4 fusion.38
  4.5 0.6 convolution_log_fusion.2
  5.7 1.0 pad_maximum_fusion
  6.7 11.6 %all-to-all-start = ((f32[4,64,640]{2,0,1:T(4,128)}), f32[4,64,640]{2,0,1:T(4,128)S(1)}, u32[]{:S(2)}, u32[]{:S(2)}) async-start(f32[4,64,640]{2,0,1:T(4,128)} %pad_maximum_fusion), calls=%async_computation | async-start | bytes 1310720 | tf_op jit(solution)/shard_map/all_to_all | solution.py:67
  18.3 22.3 %all-to-all-done = f32[4,64,640]{2,0,1:T(4,128)S(1)} async-done(((f32[4,64,640]{2,0,1:T(4,128)}), f32[4,64,640]{2,0,1:T(4,128)S(1)}, u32[]{:S(2)}, u32[]{:S(2)}) %all-to-all-start) | async-done | bytes 655392 | tf_op jit(solution)/shard_map/all_to_all | solution.py:67
  40.9 0.4 convolution_bitcast_fusion.2
  41.5 19.3 %all_to_all.30 = f32[8,8,640]{2,1,0:T(8,128)S(1)} all-to-all(f32[8,8,640]{2,1,0:T(8,128)S(1)} %broadcast_in_dim.22), channel_id=1, replica_groups=mesh['hi'=2,'z'=8,'bank'=32] {'z'}, dimensions={0} | all-to-all | bytes 327680 | tf_op jit(solution)/shard_map/all_to_all | solution.py:78
  61.4 17.9 %all_to_all.31 = bf16[4,64,512]{2,0,1:T(4,128)(2,1)S(1)} all-to-all(bf16[4,64,512]{2,0,1:T(4,128)(2,1)S(1)} %copy.27), channel_id=1, replica_groups=mesh['hi'=2,'z'=8,'bank'=32] {'bank','hi'}, dimensions={1} | all-to-all | bytes 524288 | tf_op jit(solution)/shard_map/all_to_all | solution.py:86
  79.4 0.5 exponential_convert_fusion.1
  79.9 0.4 convolution_bitcast_fusion
  80.4 0.6 convolution_log_fusion.1
  81.7 0.4 fusion.39
  82.2 0.6 convolution_log_fusion
  83.2 23.1 %all_to_all.32 = f32[4,64,512]{2,0,1:T(4,128)S(1)} all-to-all(f32[4,64,512]{2,0,1:T(4,128)S(1)} %copy.30), channel_id=1, replica_groups=mesh['hi'=2,'z'=8,'bank'=32] {'bank','hi'}, dimensions={1} | all-to-all | bytes 1048576 | tf_op jit(solution)/shard_map/all_to_all | solution.py:67
  106.7 11.7 %all_to_all.33 = f32[8,8,512]{2,1,0:T(8,128)S(1)} all-to-all(f32[8,8,512]{2,1,0:T(8,128)S(1)} %broadcast_in_dim.23), channel_id=1, replica_groups=mesh['hi'=2,'z'=8,'bank'=32] {'z'}, dimensions={0} | all-to-all | bytes 262144 | tf_op jit(solution)/shard_map/all_to_all | solution.py:78
  118.8 0.9 copy.32
  119.7 4.5 %all-to-all-start.5 = ((bf16[4,64,512]{2,0,1:T(4,128)(2,1)}), bf16[4,64,512]{2,0,1:T(4,128)(2,1)S(1)}, u32[]{:S(2)}, u32[]{:S(2)}) async-start(bf16[4,64,512]{2,0,1:T(4,128)(2,1)} %copy.32), calls=%async_computation.5 | async-start | bytes 524288 | tf_op jit(solution)/shard_map/all_to_all | solution.py:86
  124.2 7.2 %collective-permute-start = (bf16[8,512]{1,0:T(8,128)(2,1)S(1)}, bf16[8,512]{1,0:T(8,128)(2,1)S(1)}, u32[]{:S(2)}, u32[]{:S(2)}) collective-permute-start(bf16[8,512]{1,0:T(8,128)(2,1)S(1)} %divide_convert_fusion), channel_id=1, source_target_pairs={{0,256},{256,0},{1,257},{257,1},{2,258},{258,2},{3,259},{259,3},{4... | collective-permute-start | bytes 24584 | tf_op jit(solution)/shard_map/ppermute | solution.py:88
  131.4 3.9 %collective-permute-done = bf16[8,512]{1,0:T(8,128)(2,1)S(1)} collective-permute-done((bf16[8,512]{1,0:T(8,128)(2,1)S(1)}, bf16[8,512]{1,0:T(8,128)(2,1)S(1)}, u32[]{:S(2)}, u32[]{:S(2)}) %collective-permute-start) | collective-permute-done | bytes 8224 | tf_op jit(solution)/shard_map/ppermute | solution.py:88
  135.3 0.6 pad_maximum_fusion.2
  135.9 2.1 %all-to-all-done.5 = bf16[4,64,512]{2,0,1:T(4,128)(2,1)S(1)} async-done(((bf16[4,64,512]{2,0,1:T(4,128)(2,1)}), bf16[4,64,512]{2,0,1:T(4,128)(2,1)S(1)}, u32[]{:S(2)}, u32[]{:S(2)}) %all-to-all-start.5) | async-done | bytes 262176 | tf_op jit(solution)/shard_map/all_to_all | solution.py:86
  138.0 1.2 convert_subtract_fusion.2
  (45 shorter events, 4.8 us)
Async XLA Ops:
  0.7 2.7 %copy-start = (bf16[4,32768]{1,0:T(4,128)(2,1)S(1)}, bf16[4,32768]{1,0:T(4,128)(2,1)}, u32[]{:S(2)}) copy-start(bf16[4,32768]{1,0:T(4,128)(2,1)} %param.2) | copy-start | bytes 786436
  4.3 1.3 copy-start.2
  6.7 33.9 %all-to-all-start = ((f32[4,64,640]{2,0,1:T(4,128)}), f32[4,64,640]{2,0,1:T(4,128)S(1)}, u32[]{:S(2)}, u32[]{:S(2)}) async-start(f32[4,64,640]{2,0,1:T(4,128)} %pad_maximum_fusion), calls=%async_computation | async-start | bytes 1310720 | tf_op jit(solution)/shard_map/all_to_all | solution.py:67
  79.9 1.4 %copy-start.1 = (bf16[4,32768]{1,0:T(4,128)(2,1)S(1)}, bf16[4,32768]{1,0:T(4,128)(2,1)}, u32[]{:S(2)}) copy-start(bf16[4,32768]{1,0:T(4,128)(2,1)} %param.2) | copy-start | bytes 786436
  119.7 18.3 %all-to-all-start.5 = ((bf16[4,64,512]{2,0,1:T(4,128)(2,1)}), bf16[4,64,512]{2,0,1:T(4,128)(2,1)S(1)}, u32[]{:S(2)}, u32[]{:S(2)}) async-start(bf16[4,64,512]{2,0,1:T(4,128)(2,1)} %copy.32), calls=%async_computation.5 | async-start | bytes 524288 | tf_op jit(solution)/shard_map/all_to_all | solution.py:86
  124.2 11.1 %collective-permute-start = (bf16[8,512]{1,0:T(8,128)(2,1)S(1)}, bf16[8,512]{1,0:T(8,128)(2,1)S(1)}, u32[]{:S(2)}, u32[]{:S(2)}) collective-permute-start(bf16[8,512]{1,0:T(8,128)(2,1)S(1)} %divide_convert_fusion), channel_id=1, source_target_pairs={{0,256},{256,0},{1,257},{257,1},{2,258},{258,2},{3,259},{259,3},{4... | collective-permute-start | bytes 24584 | tf_op jit(solution)/shard_map/ppermute | solution.py:88

commit v16 on v15

--- a/solution.py
+++ b/solution.py
@@ -84,7 +84,10 @@
             "msk,kc->msc", weights_in.astype(jnp.bfloat16), center_chunk, preferred_element_type=jnp.float32
         ).astype(jnp.bfloat16)
         returned = lax.all_to_all(wanted, spread_axes, 1, 1, tiled=True)
-        potential = returned.astype(jnp.float32) - smoothed.reshape(member_count, spread_size, chunk)
+        if iteration + 1 < ITERS:
+            potential = returned.astype(jnp.float32) - smoothed.reshape(member_count, spread_size, chunk)
+        else:
+            potential = returned.reshape(member_count, cell_count).astype(jnp.float32) - smoothed
     other = lax.ppermute(center_chunk, "hi", [(0, 1), (1, 0)])
     first = lax.axis_index("hi") == 0
     centers = jnp.concatenate(

time: 140 us -> 139 us (level)
  transfers between devices with their start and end apart: 3 -> 3, of which waited for: 3 -> 3; matrix products, arithmetic and copies ran while one was open for 0% -> 1% of each run, Pallas kernels for 0% -> 0%
where the time goes in v16:
time: 139 us
  blocking collectives  71.9 us (52%)
  waiting for transfers between devices  27.9 us (20%)
  starting transfers between devices  23.2 us (17%)
  other arithmetic  5.81 us (4%)
  matrix products  5.35 us (4%)
  local copies, waits for them, and re-layouts  3.78 us (3%)
    all_to_all x2, blocking collectives, per_device(): summed = jnp.sum(lax.all_to_all(peers, 'z', 0, 0, tiled=True), axis=0)  30.9 us
    all_to_all x1, blocking collectives, per_device(): arrived = lax.all_to_all(rows, spread_axes, 1, 1, tiled=True)  23.1 us
    all_to_all x1, waiting for transfers between devices, per_device(): arrived = lax.all_to_all(rows, spread_axes, 1, 1, tiled=True)  22.3 us
    all_to_all x1, blocking collectives, per_device(): returned = lax.all_to_all(wanted, spread_axes, 1, 1, tiled=True)  17.9 us
    all_to_all x1, starting transfers between devices, per_device(): arrived = lax.all_to_all(rows, spread_axes, 1, 1, tiled=True)  11.6 us
    ppermute x1, starting transfers between devices, per_device(): other = lax.ppermute(center_chunk, 'hi', [(0, 1), (1, 0)])  7.17 us
    all_to_all x1, starting transfers between devices, per_device(): returned = lax.all_to_all(wanted, spread_axes, 1, 1, tiled=True)  4.46 us
    ppermute x1, waiting for transfers between devices, per_device(): other = lax.ppermute(center_chunk, 'hi', [(0, 1), (1, 0)])  3.5 us
  transfers between devices with their start and end apart: 3, of which 3 were waited for; matrix products, arithmetic and copies ran while one was open for 1% of the time, Pallas kernels for 0%

profile of v16, /device:TPU:1, one launch (start us, length us, event | category | flops | bytes accessed | tf_op | source)
XLA Modules:
  0.0 139.0 jit_solution(9928111420692511669)
XLA Ops:
  0.7 1.9 %exponential_convert_fusion = bf16[1024,1024]{1,0:T(8,128)(2,1)S(1)} fusion(s32[1024]{0:T(1024)S(1)} %get-tuple-element.5, s32[1024]{0:T(1024)S(1)} %get-tuple-element.6, s32[1024]{0:T(1024)S(1)} %get-tuple-element.4, s32[1024]{0:T(1024)S(1)} %get-tuple-element.7, pred[1024]{0:T(1024)(128)(4,1)S(1)} %get-tuple-element.8, pred[1024]{0:T(1024)(128)(4,1)S(1)} %get-tuple-element.9), kind=kLoop, calls=%fused_computation | loop fusion | flops 15728640 | bytes 2115584 | tf_op jit(solution)/shard_map/convert_element_type | solution.py:23
  2.6 0.5 fusion.7
  3.8 0.4 fusion.38
  4.5 0.6 convolution_log_fusion.2
  5.7 1.0 pad_maximum_fusion
  6.7 11.6 %all-to-all-start = ((f32[4,64,640]{2,0,1:T(4,128)}), f32[4,64,640]{2,0,1:T(4,128)S(1)}, u32[]{:S(2)}, u32[]{:S(2)}) async-start(f32[4,64,640]{2,0,1:T(4,128)} %pad_maximum_fusion), calls=%async_computation | async-start | bytes 1310720 | tf_op jit(solution)/shard_map/all_to_all | solution.py:67
  18.3 22.3 %all-to-all-done = f32[4,64,640]{2,0,1:T(4,128)S(1)} async-done(((f32[4,64,640]{2,0,1:T(4,128)}), f32[4,64,640]{2,0,1:T(4,128)S(1)}, u32[]{:S(2)}, u32[]{:S(2)}) %all-to-all-start) | async-done | bytes 655392 | tf_op jit(solution)/shard_map/all_to_all | solution.py:67
  40.9 0.4 convolution_bitcast_fusion.2
  41.5 19.3 %all_to_all.30 = f32[8,8,640]{2,1,0:T(8,128)S(1)} all-to-all(f32[8,8,640]{2,1,0:T(8,128)S(1)} %broadcast_in_dim.22), channel_id=1, replica_groups=mesh['hi'=2,'z'=8,'bank'=32] {'z'}, dimensions={0} | all-to-all | bytes 327680 | tf_op jit(solution)/shard_map/all_to_all | solution.py:78
  61.4 17.9 %all_to_all.31 = bf16[4,64,512]{2,0,1:T(4,128)(2,1)S(1)} all-to-all(bf16[4,64,512]{2,0,1:T(4,128)(2,1)S(1)} %copy.25), channel_id=1, replica_groups=mesh['hi'=2,'z'=8,'bank'=32] {'bank','hi'}, dimensions={1} | all-to-all | bytes 524288 | tf_op jit(solution)/shard_map/all_to_all | solution.py:86
  79.4 0.5 exponential_convert_fusion.1
  79.9 0.4 convolution_bitcast_fusion
  80.4 0.6 convolution_log_fusion.1
  81.7 0.4 fusion.39
  82.2 0.6 convolution_log_fusion
  83.2 23.1 %all_to_all.32 = f32[4,64,512]{2,0,1:T(4,128)S(1)} all-to-all(f32[4,64,512]{2,0,1:T(4,128)S(1)} %copy.28), channel_id=1, replica_groups=mesh['hi'=2,'z'=8,'bank'=32] {'bank','hi'}, dimensions={1} | all-to-all | bytes 1048576 | tf_op jit(solution)/shard_map/all_to_all | solution.py:67
  106.7 11.7 %all_to_all.33 = f32[8,8,512]{2,1,0:T(8,128)S(1)} all-to-all(f32[8,8,512]{2,1,0:T(8,128)S(1)} %broadcast_in_dim.23), channel_id=1, replica_groups=mesh['hi'=2,'z'=8,'bank'=32] {'z'}, dimensions={0} | all-to-all | bytes 262144 | tf_op jit(solution)/shard_map/all_to_all | solution.py:78
  118.8 0.9 copy.30
  119.7 4.5 %all-to-all-start.5 = ((bf16[4,64,512]{2,0,1:T(4,128)(2,1)}), bf16[4,64,512]{2,0,1:T(4,128)(2,1)S(1)}, u32[]{:S(2)}, u32[]{:S(2)}) async-start(bf16[4,64,512]{2,0,1:T(4,128)(2,1)} %copy.30), calls=%async_computation.5 | async-start | bytes 524288 | tf_op jit(solution)/shard_map/all_to_all | solution.py:86
  124.2 7.2 %collective-permute-start = (bf16[8,512]{1,0:T(8,128)(2,1)S(1)}, bf16[8,512]{1,0:T(8,128)(2,1)S(1)}, u32[]{:S(2)}, u32[]{:S(2)}) collective-permute-start(bf16[8,512]{1,0:T(8,128)(2,1)S(1)} %divide_convert_fusion), channel_id=1, source_target_pairs={{0,256},{256,0},{1,257},{257,1},{2,258},{258,2},{3,259},{259,3},{4... | collective-permute-start | bytes 24584 | tf_op jit(solution)/shard_map/ppermute | solution.py:91
  131.8 3.5 %collective-permute-done = bf16[8,512]{1,0:T(8,128)(2,1)S(1)} collective-permute-done((bf16[8,512]{1,0:T(8,128)(2,1)S(1)}, bf16[8,512]{1,0:T(8,128)(2,1)S(1)}, u32[]{:S(2)}, u32[]{:S(2)}) %collective-permute-start) | collective-permute-done | bytes 8224 | tf_op jit(solution)/shard_map/ppermute | solution.py:91
  135.3 0.6 pad_maximum_fusion.2
  135.9 2.1 %all-to-all-done.5 = bf16[4,64,512]{2,0,1:T(4,128)(2,1)S(1)} async-done(((bf16[4,64,512]{2,0,1:T(4,128)(2,1)}), bf16[4,64,512]{2,0,1:T(4,128)(2,1)S(1)}, u32[]{:S(2)}, u32[]{:S(2)}) %all-to-all-start.5) | async-done | bytes 262176 | tf_op jit(solution)/shard_map/all_to_all | solution.py:86
  138.0 0.9 convert_subtract_fusion.2
  (46 shorter events, 5.2 us)
Async XLA Ops:
  0.7 2.7 %copy-start = (bf16[4,32768]{1,0:T(4,128)(2,1)S(1)}, bf16[4,32768]{1,0:T(4,128)(2,1)}, u32[]{:S(2)}) copy-start(bf16[4,32768]{1,0:T(4,128)(2,1)} %param.2) | copy-start | bytes 786436
  4.3 1.3 copy-start.2
  6.7 33.9 %all-to-all-start = ((f32[4,64,640]{2,0,1:T(4,128)}), f32[4,64,640]{2,0,1:T(4,128)S(1)}, u32[]{:S(2)}, u32[]{:S(2)}) async-start(f32[4,64,640]{2,0,1:T(4,128)} %pad_maximum_fusion), calls=%async_computation | async-start | bytes 1310720 | tf_op jit(solution)/shard_map/all_to_all | solution.py:67
  79.9 1.4 %copy-start.1 = (bf16[4,32768]{1,0:T(4,128)(2,1)S(1)}, bf16[4,32768]{1,0:T(4,128)(2,1)}, u32[]{:S(2)}) copy-start(bf16[4,32768]{1,0:T(4,128)(2,1)} %param.2) | copy-start | bytes 786436
  119.7 18.3 %all-to-all-start.5 = ((bf16[4,64,512]{2,0,1:T(4,128)(2,1)}), bf16[4,64,512]{2,0,1:T(4,128)(2,1)S(1)}, u32[]{:S(2)}, u32[]{:S(2)}) async-start(bf16[4,64,512]{2,0,1:T(4,128)(2,1)} %copy.30), calls=%async_computation.5 | async-start | bytes 524288 | tf_op jit(solution)/shard_map/all_to_all | solution.py:86
  124.2 11.1 %collective-permute-start = (bf16[8,512]{1,0:T(8,128)(2,1)S(1)}, bf16[8,512]{1,0:T(8,128)(2,1)S(1)}, u32[]{:S(2)}, u32[]{:S(2)}) collective-permute-start(bf16[8,512]{1,0:T(8,128)(2,1)S(1)} %divide_convert_fusion), channel_id=1, source_target_pairs={{0,256},{256,0},{1,257},{257,1},{2,258},{258,2},{3,259},{259,3},{4... | collective-permute-start | bytes 24584 | tf_op jit(solution)/shard_map/ppermute | solution.py:91

commit v17 on v16

--- a/solution.py
+++ b/solution.py
@@ -41,9 +41,10 @@
     kernel_line, kernel_pair = kernel_tables()
     member_count = log_density.shape[0]
     cell_count = log_density.shape[1]
-    spread_axes = ("bank", "hi")
-    spread_size = lax.axis_size("hi") * lax.axis_size("bank")
-    z_size = lax.axis_size("z")
+    spread_axes = ("bank", "zr")
+    spread_size = lax.axis_size("zr") * lax.axis_size("bank")
+    reduce_axes = ("hi", "zq")
+    z_size = lax.axis_size("hi") * lax.axis_size("zq")
     chunk = cell_count // spread_size
     labels = jnp.arange(BARS, dtype=jnp.int32)
     onehot = (assignment[:, None] == labels[None, :]).astype(jnp.float32)
@@ -75,7 +76,7 @@
                 [group_sums, jnp.broadcast_to(group_counts[:, None], (BARS, 128))], axis=1
             )
         peers = jnp.broadcast_to(group_sums[None], (z_size,) + group_sums.shape)
-        summed = jnp.sum(lax.all_to_all(peers, "z", 0, 0, tiled=True), axis=0)
+        summed = jnp.sum(lax.all_to_all(peers, reduce_axes, 0, 0, tiled=True), axis=0)
         if counts is None:
             counts = summed[:, chunk]
             summed = summed[:, :chunk]
@@ -88,8 +89,8 @@
             potential = returned.astype(jnp.float32) - smoothed.reshape(member_count, spread_size, chunk)
         else:
             potential = returned.reshape(member_count, cell_count).astype(jnp.float32) - smoothed
-    other = lax.ppermute(center_chunk, "hi", [(0, 1), (1, 0)])
-    first = lax.axis_index("hi") == 0
+    other = lax.ppermute(center_chunk, "zr", [(0, 1), (1, 0)])
+    first = lax.axis_index("zr") == 0
     centers = jnp.concatenate(
         [jnp.where(first, center_chunk, other), jnp.where(first, other, center_chunk)], axis=1
     )
@@ -98,14 +99,18 @@
 
 def solution(mesh):
     blk_size = mesh.shape["blk"]
-    hi_size = 2 if blk_size % 2 == 0 else 1
-    devices = mesh.devices.reshape(hi_size, blk_size // hi_size, mesh.shape["bank"])
-    view = Mesh(devices, ("hi", "z", "bank"))
-    placed = (P(("hi", "z", "bank"), None), P(("hi", "z", "bank")))
+    hi_size = 2 if blk_size % 4 == 0 else 1
+    pair_size = 2 if blk_size % 2 == 0 else 1
+    devices = mesh.devices.reshape(
+        hi_size, blk_size // (hi_size * pair_size), pair_size, mesh.shape["bank"]
+    )
+    view = Mesh(devices, ("hi", "zq", "zr", "bank"))
+    every = ("hi", "zq", "zr", "bank")
+    placed = (P(every, None), P(every))
     return jax.shard_map(
         per_device,
         mesh=view,
         in_specs=placed,
-        out_specs=(P(None, "bank"), P(("hi", "z", "bank"), None)),
+        out_specs=(P(None, "bank"), P(every, None)),
         check_vma=False,
     )

time: 139 us -> 141 us (1.014)
  blocking collectives: 71.9 us -> 77.1 us
  starting transfers between devices: 23.2 us -> 20.9 us
  waiting for transfers between devices: 27.9 us -> 26.4 us
    all_to_all x2, blocking collectives: 30.9 us -> 37.8 us  [per_device(): lax.all_to_all(peers, reduce_axes, 0, 0, tiled=True)]
    ppermute x1, starting transfers between devices: 7.17 us -> 3.27 us  [per_device(): other = lax.ppermute(center_chunk, 'zr', [(0, 1), (1, 0)])]
    all_to_all x1, waiting for transfers between devices: 2.08 us -> 5.88 us  [per_device(): returned = lax.all_to_all(wanted, spread_axes, 1, 1, tiled=True)]
    all_to_all x1, waiting for transfers between devices: 22.3 us -> 19.5 us  [per_device(): arrived = lax.all_to_all(rows, spread_axes, 1, 1, tiled=True)]
    ppermute x1, waiting for transfers between devices: 3.5 us -> 1.06 us  [per_device(): other = lax.ppermute(center_chunk, 'zr', [(0, 1), (1, 0)])]
    all_to_all x1, starting transfers between devices: 4.46 us -> 6.45 us  [per_device(): returned = lax.all_to_all(wanted, spread_axes, 1, 1, tiled=True)]
    all_to_all x1, blocking collectives: 23.1 us -> 21.5 us  [per_device(): arrived = lax.all_to_all(rows, spread_axes, 1, 1, tiled=True)]
where the time goes in v17:
time: 141 us; the launch traced here: 140 us
  blocking collectives  77.1 us (55%)
  waiting for transfers between devices  26.4 us (19%)
  starting transfers between devices  20.9 us (15%)
  other arithmetic  5.81 us (4%)
  matrix products  5.34 us (4%)
  local copies, waits for them, and re-layouts  3.78 us (3%)
    all_to_all x2, blocking collectives, per_device(): lax.all_to_all(peers, reduce_axes, 0, 0, tiled=True)  37.8 us
    all_to_all x1, blocking collectives, per_device(): arrived = lax.all_to_all(rows, spread_axes, 1, 1, tiled=True)  21.5 us
    all_to_all x1, waiting for transfers between devices, per_device(): arrived = lax.all_to_all(rows, spread_axes, 1, 1, tiled=True)  19.5 us
    all_to_all x1, blocking collectives, per_device(): returned = lax.all_to_all(wanted, spread_axes, 1, 1, tiled=True)  17.9 us
    all_to_all x1, starting transfers between devices, per_device(): arrived = lax.all_to_all(rows, spread_axes, 1, 1, tiled=True)  11.2 us
    all_to_all x1, starting transfers between devices, per_device(): returned = lax.all_to_all(wanted, spread_axes, 1, 1, tiled=True)  6.45 us
    all_to_all x1, waiting for transfers between devices, per_device(): returned = lax.all_to_all(wanted, spread_axes, 1, 1, tiled=True)  5.88 us
    ppermute x1, starting transfers between devices, per_device(): other = lax.ppermute(center_chunk, 'zr', [(0, 1), (1, 0)])  3.27 us
  transfers between devices with their start and end apart: 3, of which 3 were waited for; matrix products, arithmetic and copies ran while one was open for 1% of the time, Pallas kernels for 0%

profile of v17, /device:TPU:1, one launch (start us, length us, event | category | flops | bytes accessed | tf_op | source)
XLA Modules:
  0.0 140.3 jit_solution(2646330441764246731)
XLA Ops:
  0.7 1.9 %exponential_convert_fusion = bf16[1024,1024]{1,0:T(8,128)(2,1)S(1)} fusion(s32[1024]{0:T(1024)S(1)} %get-tuple-element.5, s32[1024]{0:T(1024)S(1)} %get-tuple-element.6, s32[1024]{0:T(1024)S(1)} %get-tuple-element.4, s32[1024]{0:T(1024)S(1)} %get-tuple-element.7, pred[1024]{0:T(1024)(128)(4,1)S(1)} %get-tuple-element.8, pred[1024]{0:T(1024)(128)(4,1)S(1)} %get-tuple-element.9), kind=kLoop, calls=%fused_computation | loop fusion | flops 15728640 | bytes 2115584 | tf_op jit(solution)/shard_map/convert_element_type | solution.py:23
  2.6 0.5 fusion.7
  3.8 0.4 fusion.38
  4.5 0.6 convolution_log_fusion.2
  5.7 1.0 pad_maximum_fusion
  6.7 11.2 %all-to-all-start = ((f32[4,64,640]{2,0,1:T(4,128)}), f32[4,64,640]{2,0,1:T(4,128)S(1)}, u32[]{:S(2)}, u32[]{:S(2)}) async-start(f32[4,64,640]{2,0,1:T(4,128)} %pad_maximum_fusion), calls=%async_computation | async-start | bytes 1310720 | tf_op jit(solution)/shard_map/all_to_all | solution.py:68
  17.9 19.5 %all-to-all-done = f32[4,64,640]{2,0,1:T(4,128)S(1)} async-done(((f32[4,64,640]{2,0,1:T(4,128)}), f32[4,64,640]{2,0,1:T(4,128)S(1)}, u32[]{:S(2)}, u32[]{:S(2)}) %all-to-all-start) | async-done | bytes 655392 | tf_op jit(solution)/shard_map/all_to_all | solution.py:68
  37.8 0.4 convolution_bitcast_fusion.2
  38.3 23.5 %all_to_all.30 = f32[8,8,640]{2,1,0:T(8,128)S(1)} all-to-all(f32[8,8,640]{2,1,0:T(8,128)S(1)} %broadcast_in_dim.22), channel_id=1, replica_groups=mesh['hi'=2,'zq'=4,'zr'=2,'bank'=32] {'hi','zq'}, dimensions={0} | all-to-all | bytes 327680 | tf_op jit(solution)/shard_map/all_to_all | solution.py:79
  62.4 17.9 %all_to_all.31 = bf16[4,64,512]{2,0,1:T(4,128)(2,1)S(1)} all-to-all(bf16[4,64,512]{2,0,1:T(4,128)(2,1)S(1)} %copy.25), channel_id=1, replica_groups=mesh['hi'=2,'zq'=4,'zr'=2,'bank'=32] {'bank','zr'}, dimensions={1} | all-to-all | bytes 524288 | tf_op jit(solution)/shard_map/all_to_all | solution.py:87
  80.3 0.5 exponential_convert_fusion.1
  80.9 0.4 convolution_bitcast_fusion
  81.3 0.6 convolution_log_fusion.1
  82.7 0.4 fusion.39
  83.1 0.6 convolution_log_fusion
  84.1 21.5 %all_to_all.32 = f32[4,64,512]{2,0,1:T(4,128)S(1)} all-to-all(f32[4,64,512]{2,0,1:T(4,128)S(1)} %copy.28), channel_id=1, replica_groups=mesh['hi'=2,'zq'=4,'zr'=2,'bank'=32] {'bank','zr'}, dimensions={1} | all-to-all | bytes 1048576 | tf_op jit(solution)/shard_map/all_to_all | solution.py:68
  106.0 14.3 %all_to_all.33 = f32[8,8,512]{2,1,0:T(8,128)S(1)} all-to-all(f32[8,8,512]{2,1,0:T(8,128)S(1)} %broadcast_in_dim.23), channel_id=1, replica_groups=mesh['hi'=2,'zq'=4,'zr'=2,'bank'=32] {'hi','zq'}, dimensions={0} | all-to-all | bytes 262144 | tf_op jit(solution)/shard_map/all_to_all | solution.py:79
  120.8 0.9 copy.30
  121.7 6.5 %all-to-all-start.5 = ((bf16[4,64,512]{2,0,1:T(4,128)(2,1)}), bf16[4,64,512]{2,0,1:T(4,128)(2,1)S(1)}, u32[]{:S(2)}, u32[]{:S(2)}) async-start(bf16[4,64,512]{2,0,1:T(4,128)(2,1)} %copy.30), calls=%async_computation.5 | async-start | bytes 524288 | tf_op jit(solution)/shard_map/all_to_all | solution.py:87
  128.1 3.3 %collective-permute-start = (bf16[8,512]{1,0:T(8,128)(2,1)S(1)}, bf16[8,512]{1,0:T(8,128)(2,1)S(1)}, u32[]{:S(2)}, u32[]{:S(2)}) collective-permute-start(bf16[8,512]{1,0:T(8,128)(2,1)S(1)} %divide_convert_fusion), channel_id=1, source_target_pairs={{0,32},{32,0},{1,33},{33,1},{2,34},{34,2},{3,35},{35,3},{4,36},{36... | collective-permute-start | bytes 24584 | tf_op jit(solution)/shard_map/ppermute | solution.py:92
  131.8 1.1 collective-permute-done
  132.9 0.6 pad_maximum_fusion.2
  133.5 5.9 %all-to-all-done.5 = bf16[4,64,512]{2,0,1:T(4,128)(2,1)S(1)} async-done(((bf16[4,64,512]{2,0,1:T(4,128)(2,1)}), bf16[4,64,512]{2,0,1:T(4,128)(2,1)S(1)}, u32[]{:S(2)}, u32[]{:S(2)}) %all-to-all-start.5) | async-done | bytes 262176 | tf_op jit(solution)/shard_map/all_to_all | solution.py:87
  139.4 0.9 convert_subtract_fusion.2
  (46 shorter events, 5.1 us)
Async XLA Ops:
  0.7 2.7 %copy-start = (bf16[4,32768]{1,0:T(4,128)(2,1)S(1)}, bf16[4,32768]{1,0:T(4,128)(2,1)}, u32[]{:S(2)}) copy-start(bf16[4,32768]{1,0:T(4,128)(2,1)} %param.2) | copy-start | bytes 786436
  4.3 1.3 copy-start.2
  6.7 30.7 %all-to-all-start = ((f32[4,64,640]{2,0,1:T(4,128)}), f32[4,64,640]{2,0,1:T(4,128)S(1)}, u32[]{:S(2)}, u32[]{:S(2)}) async-start(f32[4,64,640]{2,0,1:T(4,128)} %pad_maximum_fusion), calls=%async_computation | async-start | bytes 1310720 | tf_op jit(solution)/shard_map/all_to_all | solution.py:68
  80.8 1.4 %copy-start.1 = (bf16[4,32768]{1,0:T(4,128)(2,1)S(1)}, bf16[4,32768]{1,0:T(4,128)(2,1)}, u32[]{:S(2)}) copy-start(bf16[4,32768]{1,0:T(4,128)(2,1)} %param.2) | copy-start | bytes 786436
  121.7 17.7 %all-to-all-start.5 = ((bf16[4,64,512]{2,0,1:T(4,128)(2,1)}), bf16[4,64,512]{2,0,1:T(4,128)(2,1)S(1)}, u32[]{:S(2)}, u32[]{:S(2)}) async-start(bf16[4,64,512]{2,0,1:T(4,128)(2,1)} %copy.30), calls=%async_computation.5 | async-start | bytes 524288 | tf_op jit(solution)/shard_map/all_to_all | solution.py:87
  128.1 4.7 %collective-permute-start = (bf16[8,512]{1,0:T(8,128)(2,1)S(1)}, bf16[8,512]{1,0:T(8,128)(2,1)S(1)}, u32[]{:S(2)}, u32[]{:S(2)}) collective-permute-start(bf16[8,512]{1,0:T(8,128)(2,1)S(1)} %divide_convert_fusion), channel_id=1, source_target_pairs={{0,32},{32,0},{1,33},{33,1},{2,34},{34,2},{3,35},{35,3},{4,36},{36... | collective-permute-start | bytes 24584 | tf_op jit(solution)/shard_map/ppermute | solution.py:92
